TPU v7x, 512 devices: a whole 4x4x16 slice. The times are simulated.
512 devices in a mesh: harm: 8 (over x, z_hi), space: 64 (over z_lo, y, core).
Axes of the slice: x: 4, y: 4, z: 16 (z_hi: 2, z_lo: 8; z = z_hi * 8 + z_lo), core: 2. Of those that a mesh axis runs over, the one named last changes fastest.
Arguments:
- rhs_field: float32 [64, 16384], P('harm', 'space'), may hold values from -14 to 14
- neighbors: int32 [8, 16384], P(None, 'space'), may hold values from 0 to 16383, as said below
- nu_mean: float32 [8, 16384], P(None, 'space'), may hold values from 0.5 to 4
- nu_ripple: float32 [64, 8, 16384], P(None, None, 'space'), may hold values from -0.24 to 0.24
- mass_coeff: float32 [16384], P('space'), may hold values from 0.5 to 2
- eddy_coeff: float32 [16384], P('space'), may hold values from 0.25 to 2
Outputs:
- correction: float32 [64, 16384], P('harm', 'space')
- residual: float32 [64, 16384], P('harm', 'space')
Inputs may be any that keep to these rules, and one draw needn't show every extreme that they name: neighbors[d, n] is a node at most 64 places from n in the node order closed into a loop (node 16383 lies next to node 0), or n itself for an unused slot; slot 0 is always used, and some entry lies 64 places away in each direction.
All inputs are finite; a program needn't handle non-finite values.
Results may differ from a plain program's by a relative error of at most 0.0003.
Values sent between devices are 32-bit elements; how exact they have to be, the bound alone decides.
No kernel may reach another device: no remote copies, remote signals or barrier semaphores. Data moves between devices by JAX's collectives and lax.ppermute only.
A program may use at most 64 MiB of HBM per device.

v0:
```python
import jax
import jax.numpy as jnp
from jax import lax
from jax.sharding import PartitionSpec as P

IF = 64
ITERS = 8


def with_halo(array, sides, width):
    for axis, dim in sides:
        count, length = (lax.axis_size(axis), array.shape[dim])
        up = [(i, (i + 1) % count) for i in range(count)]
        down = [(j, i) for i, j in up]
        last = lax.slice_in_dim(array, length - width, length, axis=dim)
        leading = lax.slice_in_dim(array, 0, width, axis=dim)
        before = lax.ppermute(last, axis, up)
        after = lax.ppermute(leading, axis, down)
        array = jnp.concatenate([before, array, after], axis=dim)
    return array


def swap_pairs(vector_in):
    shaped = vector_in.reshape(vector_in.shape[0] // 2, 2, vector_in.shape[1])
    return shaped[:, ::-1, :].reshape(vector_in.shape)


def fourier_tables(harmonics):
    index_vals = jnp.arange(harmonics, dtype=jnp.int32)
    product_mod = jnp.mod(index_vals[:, None] * index_vals[None, :], harmonics).astype(jnp.float32)
    phase = 2.0 * jnp.pi * product_mod / harmonics
    return (jnp.cos(phase), jnp.sin(phase))


def matmul_high(left, right):
    return jnp.dot(left, right, precision=lax.Precision.HIGHEST, preferred_element_type=jnp.float32)


def least_squares(columns, beta_norm):
    steps_total = len(columns)
    rot_cos, rot_sin = ([], [])
    target = [beta_norm] + [jnp.zeros((), jnp.float32)] * steps_total
    triangle = []
    for j in range(steps_total):
        column_vals = list(columns[j])
        for i in range(j):
            first, second = (column_vals[i], column_vals[i + 1])
            column_vals[i] = rot_cos[i] * first + rot_sin[i] * second
            column_vals[i + 1] = rot_cos[i] * second - rot_sin[i] * first
        radius = jnp.sqrt(column_vals[j] * column_vals[j] + column_vals[j + 1] * column_vals[j + 1])
        cosine = column_vals[j] / radius
        sine_val = column_vals[j + 1] / radius
        rot_cos.append(cosine)
        rot_sin.append(sine_val)
        column_vals[j] = radius
        target[j + 1] = -sine_val * target[j]
        target[j] = cosine * target[j]
        triangle.append(column_vals[: j + 1])
    coeffs = [None] * steps_total
    for j in reversed(range(steps_total)):
        running = target[j]
        for k in range(j + 1, steps_total):
            running = running - triangle[k][j] * coeffs[k]
        coeffs[j] = running / triangle[j][j]
    return coeffs


def per_device(rhs_field, neighbors, nu_mean, nu_ripple, mass_coeff, eddy_coeff):
    block, nodes_own = rhs_field.shape
    harmonics = nu_ripple.shape[0]
    halo_width = IF
    harm_start = lax.axis_index("harm") * block
    kernel = nu_ripple.at[0].add(nu_mean)
    cos_table, sin_table = fourier_tables(harmonics)
    total_nodes = nodes_own * lax.axis_size("space")
    relative = jnp.mod(neighbors - lax.axis_index("space") * nodes_own, total_nodes)
    relative = jnp.where(relative >= total_nodes - halo_width, relative - total_nodes, relative)
    ext_index = relative + halo_width
    global_harm = harm_start + jnp.arange(block)
    harm_order = (global_harm // 2 + 1).astype(jnp.float32)
    sign_vals = jnp.where(global_harm % 2 == 0, 1.0, -1.0).astype(jnp.float32)
    factor = 4.0 * harm_order / harmonics * sign_vals
    node_share = nodes_own // lax.axis_size("harm")
    kernel_use = lax.dynamic_slice_in_dim(
        kernel, lax.axis_index("harm") * node_share, node_share, 2
    )
    kernel_flat = kernel_use.reshape(harmonics, -1)
    kernel_real = matmul_high(cos_table, kernel_flat)
    kernel_imag = -matmul_high(sin_table, kernel_flat)

    def convolve_spectrum(spec_real, spec_imag, out_cos, out_sin):
        prod_real = spec_real * kernel_real - spec_imag * kernel_imag
        prod_imag = spec_real * kernel_imag + spec_imag * kernel_real
        return (matmul_high(out_cos, prod_real) - matmul_high(out_sin, prod_imag)) / harmonics

    def operate(vector_in):
        extended = with_halo(vector_in, (("space", 1),), halo_width)
        gradients = extended[:, None, halo_width : halo_width + nodes_own] - extended[:, ext_index]
        spread = lax.all_to_all(gradients, "harm", split_axis=2, concat_axis=0, tiled=True)
        spread_flat = spread.reshape(harmonics, -1)
        spec_real = matmul_high(cos_table, spread_flat)
        spec_imag = -matmul_high(sin_table, spread_flat)
        fluxes = convolve_spectrum(spec_real, spec_imag, cos_table, sin_table)
        fluxes = fluxes.reshape(spread.shape)
        fluxes = lax.all_to_all(fluxes, "harm", split_axis=0, concat_axis=2, tiled=True)
        return (
            jnp.sum(fluxes, axis=1)
            + mass_coeff[None, :] * vector_in
            + eddy_coeff[None, :] * factor[:, None] * swap_pairs(vector_in)
        )

    beta_norm = jnp.sqrt(lax.psum(jnp.sum(rhs_field * rhs_field), ("harm", "space")))
    krylov = [rhs_field / beta_norm]
    columns = []
    for j in range(ITERS):
        image = operate(krylov[j])
        stacked = jnp.stack(krylov[: j + 1])
        local_dots = jnp.einsum("khn,hn->k", stacked, image, precision=lax.Precision.HIGHEST)
        projected = lax.psum(local_dots, ("harm", "space"))
        image = image - jnp.einsum("k,khn->hn", projected, stacked, precision=lax.Precision.HIGHEST)
        length = jnp.sqrt(lax.psum(jnp.sum(image * image), ("harm", "space")))
        columns.append([projected[i] for i in range(j + 1)] + [length])
        if j + 1 < ITERS:
            krylov.append(image / length)
    coeffs = least_squares(columns, beta_norm)
    correction = coeffs[0] * krylov[0]
    for j in range(1, ITERS):
        correction = correction + coeffs[j] * krylov[j]
    residual = rhs_field - operate(correction)
    return (correction, residual)


def solution(mesh):
    return jax.shard_map(
        per_device,
        mesh=mesh,
        in_specs=(
            P("harm", "space"),
            P(None, "space"),
            P(None, "space"),
            P(None, None, "space"),
            P("space"),
            P("space"),
        ),
        out_specs=(P("harm", "space"), P("harm", "space")),
        check_vma=False,
    )
```

profile of v0, /device:TPU:6, one launch (start us, length us, event | category | flops | bytes accessed | tf_op | source)
XLA Modules:
  0.0 2404.0 jit_solution(8581229826994617778)
XLA Ops:
  1.9 108.2 %psum.119 = f32[]{:T(128)} all-reduce(f32[]{:T(128)} %multiply_reduce_fusion.8), channel_id=1, replica_groups=mesh['harm'=8,'space'=64] {'harm','space'}, use_global_device_ids=true, to_apply=%region_1.2 | all-reduce | flops 1 | bytes 8 | tf_op jit(solution)/shard_map/psum | solution.py:112
  111.0 6.9 collective-permute-start.1
  121.0 10.5 collective-permute-done
  131.7 5.5 gather_fusion
  139.2 8.1 all-to-all-start
  148.1 12.3 all-to-all-done
  165.2 5.4 all-to-all-start.1
  170.7 12.8 all-to-all-done.1
  185.9 98.7 %psum.120 = f32[]{:T(128)} all-reduce(f32[]{:T(128)} %multiply_reduce_fusion), channel_id=1, replica_groups=mesh['harm'=8,'space'=64] {'harm','space'}, use_global_device_ids=true, to_apply=%region_3.4 | all-reduce | flops 1 | bytes 8 | tf_op jit(solution)/shard_map/psum | solution.py:119
  286.0 100.3 %psum.121 = f32[]{:T(128)} all-reduce(f32[]{:T(128)} %get-tuple-element.36), channel_id=1, replica_groups=mesh['harm'=8,'space'=64] {'harm','space'}, use_global_device_ids=true, to_apply=%region_5.6 | all-reduce | flops 1 | bytes 8 | tf_op jit(solution)/shard_map/psum | solution.py:121
  391.4 11.5 collective-permute-done.2
  403.1 5.5 gather_fusion.1
  410.0 25.5 %all_to_all.216 = f32[8,1,2048]{2,1,0:T(1,128)S(1)} all-to-all(f32[8,1,2048]{2,1,0:T(1,128)S(1)} %reshape.392), channel_id=1, replica_groups=mesh['harm'=8,'space'=64] {'harm'}, dimensions={0} | all-to-all | bytes 131072 | tf_op jit(solution)/shard_map/all_to_all | solution.py:99
  445.3 12.8 all-to-all-done.3
  459.5 98.8 %psum.122 = f32[2]{0:T(128)S(1)} all-reduce(f32[2]{0:T(128)S(1)} %convolution_bitcast_fusion.6), channel_id=1, replica_groups=mesh['harm'=8,'space'=64] {'harm','space'}, use_global_device_ids=true, to_apply=%region_7.8 | all-reduce | flops 2 | bytes 16 | tf_op jit(solution)/shard_map/psum | solution.py:119
  559.2 100.2 %psum.123 = f32[]{:T(128)} all-reduce(f32[]{:T(128)} %multiply_reduce_fusion.6), channel_id=1, replica_groups=mesh['harm'=8,'space'=64] {'harm','space'}, use_global_device_ids=true, to_apply=%region_9.10 | all-reduce | flops 1 | bytes 8 | tf_op jit(solution)/shard_map/psum | solution.py:121
  664.7 11.5 collective-permute-done.4
  676.4 5.5 gather_fusion.2
  683.3 25.3 %all_to_all.217 = f32[8,1,2048]{2,1,0:T(1,128)S(1)} all-to-all(f32[8,1,2048]{2,1,0:T(1,128)S(1)} %reshape.396), channel_id=1, replica_groups=mesh['harm'=8,'space'=64] {'harm'}, dimensions={0} | all-to-all | bytes 131072 | tf_op jit(solution)/shard_map/all_to_all | solution.py:99
  712.9 5.4 all-to-all-start.5
  718.4 12.8 all-to-all-done.5
  732.6 98.8 %psum.124 = f32[3]{0:T(128)S(1)} all-reduce(f32[3]{0:T(128)S(1)} %convolution_bitcast_fusion.5), channel_id=1, replica_groups=mesh['harm'=8,'space'=64] {'harm','space'}, use_global_device_ids=true, to_apply=%region_11.12 | all-reduce | flops 3 | bytes 24 | tf_op jit(solution)/shard_map/psum | solution.py:119
  832.2 100.2 %psum.125 = f32[]{:T(128)} all-reduce(f32[]{:T(128)} %multiply_reduce_fusion.5), channel_id=1, replica_groups=mesh['harm'=8,'space'=64] {'harm','space'}, use_global_device_ids=true, to_apply=%region_13.14 | all-reduce | flops 1 | bytes 8 | tf_op jit(solution)/shard_map/psum | solution.py:121
  938.2 11.1 collective-permute-done.6
  949.5 5.5 gather_fusion.3
  956.4 25.3 %all_to_all.218 = f32[8,1,2048]{2,1,0:T(1,128)S(1)} all-to-all(f32[8,1,2048]{2,1,0:T(1,128)S(1)} %reshape.400), channel_id=1, replica_groups=mesh['harm'=8,'space'=64] {'harm'}, dimensions={0} | all-to-all | bytes 131072 | tf_op jit(solution)/shard_map/all_to_all | solution.py:99
  986.0 5.4 all-to-all-start.7
  991.5 12.8 all-to-all-done.7
  1005.7 98.8 %psum.126 = f32[4]{0:T(128)S(1)} all-reduce(f32[4]{0:T(128)S(1)} %convolution_bitcast_fusion.4), channel_id=1, replica_groups=mesh['harm'=8,'space'=64] {'harm','space'}, use_global_device_ids=true, to_apply=%region_15.16 | all-reduce | flops 4 | bytes 32 | tf_op jit(solution)/shard_map/psum | solution.py:119
  1105.3 100.2 %psum.127 = f32[]{:T(128)} all-reduce(f32[]{:T(128)} %multiply_reduce_fusion.4), channel_id=1, replica_groups=mesh['harm'=8,'space'=64] {'harm','space'}, use_global_device_ids=true, to_apply=%region_17.18 | all-reduce | flops 1 | bytes 8 | tf_op jit(solution)/shard_map/psum | solution.py:121
  1210.9 11.5 collective-permute-done.8
  1222.6 5.5 gather_fusion.4
  1230.1 12.4 all-to-all-start.8
  1242.5 13.1 all-to-all-done.8
  1259.9 5.4 all-to-all-start.9
  1265.4 12.8 all-to-all-done.9
  1279.6 99.0 %psum.128 = f32[5]{0:T(128)S(1)} all-reduce(f32[5]{0:T(128)S(1)} %convolution_bitcast_fusion.3), channel_id=1, replica_groups=mesh['harm'=8,'space'=64] {'harm','space'}, use_global_device_ids=true, to_apply=%region_19.20 | all-reduce | flops 5 | bytes 40 | tf_op jit(solution)/shard_map/psum | solution.py:119
  1379.4 100.2 %psum.129 = f32[]{:T(128)} all-reduce(f32[]{:T(128)} %multiply_reduce_fusion.3), channel_id=1, replica_groups=mesh['harm'=8,'space'=64] {'harm','space'}, use_global_device_ids=true, to_apply=%region_21.22 | all-reduce | flops 1 | bytes 8 | tf_op jit(solution)/shard_map/psum | solution.py:121
  1484.9 11.5 collective-permute-done.10
  1496.7 5.5 gather_fusion.5
  1503.5 25.3 %all_to_all.219 = f32[8,1,2048]{2,1,0:T(1,128)S(1)} all-to-all(f32[8,1,2048]{2,1,0:T(1,128)S(1)} %reshape.408), channel_id=1, replica_groups=mesh['harm'=8,'space'=64] {'harm'}, dimensions={0} | all-to-all | bytes 131072 | tf_op jit(solution)/shard_map/all_to_all | solution.py:99
  1533.1 5.4 all-to-all-start.11
  1538.7 12.8 all-to-all-done.11
  1552.9 98.8 %psum.130 = f32[6]{0:T(128)S(1)} all-reduce(f32[6]{0:T(128)S(1)} %convolution_bitcast_fusion.2), channel_id=1, replica_groups=mesh['harm'=8,'space'=64] {'harm','space'}, use_global_device_ids=true, to_apply=%region_23.24 | all-reduce | flops 6 | bytes 48 | tf_op jit(solution)/shard_map/psum | solution.py:119
  1652.5 100.2 %psum.131 = f32[]{:T(128)} all-reduce(f32[]{:T(128)} %multiply_reduce_fusion.2), channel_id=1, replica_groups=mesh['harm'=8,'space'=64] {'harm','space'}, use_global_device_ids=true, to_apply=%region_25.26 | all-reduce | flops 1 | bytes 8 | tf_op jit(solution)/shard_map/psum | solution.py:121
  1758.0 11.5 collective-permute-done.12
  1769.8 5.5 gather_fusion.6
  1777.3 12.7 all-to-all-start.12
  1792.0 11.0 all-to-all-done.12
  1807.3 5.4 all-to-all-start.13
  1816.0 9.6 all-to-all-done.13
  1827.0 98.8 %psum.132 = f32[7]{0:T(128)S(1)} all-reduce(f32[7]{0:T(128)S(1)} %convolution_bitcast_fusion.1), channel_id=1, replica_groups=mesh['harm'=8,'space'=64] {'harm','space'}, use_global_device_ids=true, to_apply=%region_27.28 | all-reduce | flops 7 | bytes 56 | tf_op jit(solution)/shard_map/psum | solution.py:119
  1926.6 100.2 %psum.133 = f32[]{:T(128)} all-reduce(f32[]{:T(128)} %multiply_reduce_fusion.1), channel_id=1, replica_groups=mesh['harm'=8,'space'=64] {'harm','space'}, use_global_device_ids=true, to_apply=%region_29.30 | all-reduce | flops 1 | bytes 8 | tf_op jit(solution)/shard_map/psum | solution.py:121
  2033.9 9.7 collective-permute-done.14
  2043.7 5.5 gather_fusion.7
  2051.2 12.4 all-to-all-start.14
  2083.4 14.4 all-to-all-start.15
  2117.1 98.8 %psum.134 = f32[8]{0:T(128)S(1)} all-reduce(f32[8]{0:T(128)S(1)} %convolution_bitcast_fusion), channel_id=1, replica_groups=mesh['harm'=8,'space'=64] {'harm','space'}, use_global_device_ids=true, to_apply=%region_31.32 | all-reduce | flops 8 | bytes 64 | tf_op jit(solution)/shard_map/psum | solution.py:119
  2227.3 103.0 %psum.135 = f32[]{:T(128)} all-reduce(f32[]{:T(128)} %fusion.190), channel_id=1, replica_groups=mesh['harm'=8,'space'=64] {'harm','space'}, use_global_device_ids=true, to_apply=%region_33.34 | all-reduce | flops 1 | bytes 8 | tf_op jit(solution)/shard_map/psum | solution.py:121
  2331.7 6.0 collective-permute-start.17
  2340.0 11.6 collective-permute-done.16
  2351.8 5.5 gather_fusion.8
  2358.7 20.5 all_to_all.220
  2389.0 12.8 all-to-all-done.17
  (345 shorter events, 132.3 us)
Async XLA Ops:
  0.6 0.7 copy-start.4
  0.6 119.3 %copy-start = (f32[64,8,256]{2,1,0:T(8,128)S(1)}, f32[64,8,256]{2,1,0:T(8,128)}, u32[]{:S(2)}) copy-start(f32[64,8,256]{2,1,0:T(8,128)} %param.11) | copy-start | bytes 1572868
  110.9 8.9 copy-start.6
  111.0 10.0 collective-permute-start.1
  117.9 13.6 collective-permute-start
  119.9 0.7 copy-start.5
  139.2 21.1 all-to-all-start
  165.2 18.3 all-to-all-start.1
  184.5 0.7 copy-start.2
  184.5 0.7 copy-start.3
  386.9 4.5 collective-permute-start.3
  389.3 13.6 collective-permute-start.2
  439.8 18.3 all-to-all-start.3
  660.2 4.5 collective-permute-start.5
  662.6 13.6 collective-permute-start.4
  712.9 18.3 all-to-all-start.5
  933.3 4.9 collective-permute-start.7
  935.6 13.6 collective-permute-start.6
  986.0 18.3 all-to-all-start.7
  1206.4 4.5 collective-permute-start.9
  1208.7 13.6 collective-permute-start.8
  1230.1 25.5 %all-to-all-start.8 = ((f32[8,1,2048]{2,1,0:T(1,128)}), f32[8,1,2048]{2,1,0:T(1,128)S(1)}, u32[]{:S(2)}, u32[]{:S(2)}) async-start(f32[8,1,2048]{2,1,0:T(1,128)} %reshape.404), calls=%async_computation.8 | async-start | bytes 131072 | tf_op jit(solution)/shard_map/all_to_all | solution.py:99
  1259.9 18.3 all-to-all-start.9
  1480.5 4.5 collective-permute-start.11
  1482.8 13.6 collective-permute-start.10
  1533.1 18.3 all-to-all-start.11
  1753.6 4.5 collective-permute-start.13
  1755.9 13.6 collective-permute-start.12
  1777.3 25.7 %all-to-all-start.12 = ((f32[8,1,2048]{2,1,0:T(1,128)}), f32[8,1,2048]{2,1,0:T(1,128)S(1)}, u32[]{:S(2)}, u32[]{:S(2)}) async-start(f32[8,1,2048]{2,1,0:T(1,128)} %reshape.412), calls=%async_computation.12 | async-start | bytes 131072 | tf_op jit(solution)/shard_map/all_to_all | solution.py:99
  1807.3 18.3 all-to-all-start.13
  2027.6 6.3 collective-permute-start.15
  2029.9 13.6 collective-permute-start.14
  2051.2 27.8 %all-to-all-start.14 = ((f32[8,1,2048]{2,1,0:T(1,128)}), f32[8,1,2048]{2,1,0:T(1,128)S(1)}, u32[]{:S(2)}, u32[]{:S(2)}) async-start(f32[8,1,2048]{2,1,0:T(1,128)} %reshape.416), calls=%async_computation.14 | async-start | bytes 131072 | tf_op jit(solution)/shard_map/all_to_all | solution.py:99
  2083.4 32.4 %all-to-all-start.15 = ((f32[8,1,2048]{2,1,0:T(1,128)}), f32[8,1,2048]{2,1,0:T(1,128)S(1)}, u32[]{:S(2)}, u32[]{:S(2)}) async-start(f32[8,1,2048]{2,1,0:T(1,128)} %reshape.418), calls=%async_computation.15 | async-start | bytes 131072 | tf_op jit(solution)/shard_map/all_to_all | solution.py:105
  2331.6 71.3 %copy-start.1 = (f32[8,256]{1,0:T(8,128)}, f32[8,256]{1,0:T(8,128)S(1)}, u32[]{:S(2)}) copy-start(f32[8,256]{1,0:T(8,128)S(1)} %multiply_add_fusion) | copy-start | bytes 24580
  2331.7 8.3 collective-permute-start.17
  2337.7 13.9 collective-permute-start.16
  2383.5 18.3 all-to-all-start.17
where the time goes:
time: 2420 us; the launch traced here: 2400 us
  blocking collectives  1830 us (76%)
  waiting for transfers between devices  236 us (10%)
  starting transfers between devices  151 us (6%)
  local copies, waits for them, and re-layouts  92.9 us (4%)
  between operations  56.2 us (2%)
  other arithmetic  27.6 us (1%)
    psum x8, blocking collectives, per_device(): length = jnp.sqrt(lax.psum(jnp.sum(image * image), ('harm', 'space')))  805 us
    psum x8, blocking collectives, per_device(): projected = lax.psum(local_dots, ('harm', 'space'))  790 us
    all_to_all x5, blocking collectives, operate(): lax.all_to_all(gradients, 'harm', split_axis=2, concat_axis=0, tiled=True)  122 us
    psum x1, blocking collectives, per_device(): lax.psum(jnp.sum(rhs_field * rhs_field), ('harm', 'space'))  108 us
    ppermute x9, waiting for transfers between devices, with_halo(): before = lax.ppermute(last, axis, up)  100 us
    all_to_all x9, waiting for transfers between devices, operate(): lax.all_to_all(fluxes, 'harm', split_axis=0, concat_axis=2, tiled=True)  99.4 us
    all_to_all x9, starting transfers between devices, operate(): lax.all_to_all(fluxes, 'harm', split_axis=0, concat_axis=2, tiled=True)  57.2 us
    gather x18, local copies, waits for them, and re-layouts, operate(): extended[:, ext_index]  53.9 us
  transfers between devices with their start and end apart: 31, of which 20 were waited for; matrix products, arithmetic and copies ran while one was open for 0% of the time, Pallas kernels for 0%

commit v1 on v0

--- a/solution.py
+++ b/solution.py
@@ -65,6 +65,19 @@
     return coeffs
 
 
+def all_sum(values):
+    for axis in ("harm", "space"):
+        count = lax.axis_size(axis)
+        if count & (count - 1):
+            values = lax.psum(values, axis)
+            continue
+        stride = 1
+        while stride < count:
+            values = values + lax.ppermute(values, axis, [(i, i ^ stride) for i in range(count)])
+            stride *= 2
+    return values
+
+
 def per_device(rhs_field, neighbors, nu_mean, nu_ripple, mass_coeff, eddy_coeff):
     block, nodes_own = rhs_field.shape
     harmonics = nu_ripple.shape[0]
@@ -109,24 +122,35 @@
             + eddy_coeff[None, :] * factor[:, None] * swap_pairs(vector_in)
         )
 
-    beta_norm = jnp.sqrt(lax.psum(jnp.sum(rhs_field * rhs_field), ("harm", "space")))
+    local_rows = lambda rows, other: jnp.sum(jnp.stack(rows) * other[None], axis=(1, 2))
+    sums = all_sum(jnp.concatenate([local_rows([rhs_field], rhs_field), local_rows([rhs_field], image := operate(rhs_field))]))
+    beta_norm = jnp.sqrt(sums[0])
     krylov = [rhs_field / beta_norm]
-    columns = []
-    for j in range(ITERS):
-        image = operate(krylov[j])
-        stacked = jnp.stack(krylov[: j + 1])
-        local_dots = jnp.einsum("khn,hn->k", stacked, image, precision=lax.Precision.HIGHEST)
-        projected = lax.psum(local_dots, ("harm", "space"))
-        image = image - jnp.einsum("k,khn->hn", projected, stacked, precision=lax.Precision.HIGHEST)
-        length = jnp.sqrt(lax.psum(jnp.sum(image * image), ("harm", "space")))
-        columns.append([projected[i] for i in range(j + 1)] + [length])
-        if j + 1 < ITERS:
-            krylov.append(image / length)
+    images = [image / beta_norm]
+    columns = [[sums[1] / beta_norm / beta_norm]]
+    ortho = images[0] - columns[0][0] * krylov[0]
+    for j in range(1, ITERS):
+        image = operate(ortho)
+        sums = all_sum(
+            jnp.concatenate([local_rows([ortho], ortho), local_rows(krylov + [ortho], image)])
+        )
+        length = jnp.sqrt(sums[0])
+        columns[j - 1].append(length)
+        krylov.append(ortho / length)
+        images.append(image / length)
+        projected = [sums[1 + i] / length for i in range(j)] + [sums[1 + j] / length / length]
+        columns.append(projected)
+        ortho = images[j]
+        for i in range(j + 1):
+            ortho = ortho - projected[i] * krylov[i]
+    columns[ITERS - 1].append(jnp.sqrt(all_sum(jnp.sum(ortho * ortho)[None])[0]))
     coeffs = least_squares(columns, beta_norm)
     correction = coeffs[0] * krylov[0]
+    applied = coeffs[0] * images[0]
     for j in range(1, ITERS):
         correction = correction + coeffs[j] * krylov[j]
-    residual = rhs_field - operate(correction)
+        applied = applied + coeffs[j] * images[j]
+    residual = rhs_field - applied
     return (correction, residual)
 
 

time: 2420 us -> 1180 us (0.49)
  blocking collectives: 1830 us -> 69.9 us
  waiting for transfers between devices: 236 us -> 533 us
  starting transfers between devices: 151 us -> 388 us
    psum x17 -> x0, blocking collectives: 1700 us -> none  [the longest x8 805 us: per_device(): length = jnp.sqrt(lax.psum(jnp.sum(image * image), ('harm', 'space')))]
    ppermute x0 -> x81, waiting for transfers between devices: none -> 373 us  [all_sum(): lax.ppermute(values, axis, [(i, i ^ stride) for i in range(count)])]
    ppermute x0 -> x81, starting transfers between devices: none -> 196 us  [all_sum(): lax.ppermute(values, axis, [(i, i ^ stride) for i in range(count)])]
    ppermute x9 -> x8, waiting for transfers between devices: 100 us -> 0.02 us  [with_halo(): before = lax.ppermute(last, axis, up)]
    ppermute x9 -> x8, starting transfers between devices: 29.2 us -> 102 us  [with_halo(): after = lax.ppermute(leading, axis, down)]
    all_to_all x5 -> x4, blocking collectives: 122 us -> 69.9 us  [operate(): lax.all_to_all(gradients, 'harm', split_axis=2, concat_axis=0, tiled=True)]
    all_to_all x9 -> x8, starting transfers between devices: 57.2 us -> 42.9 us  [operate(): lax.all_to_all(fluxes, 'harm', split_axis=0, concat_axis=2, tiled=True)]
    gather x18 -> x16, local copies, waits for them, and re-layouts: 53.9 us -> 47.9 us  [operate(): extended[:, ext_index]]
  transfers between devices with their start and end apart: 31 -> 109, of which waited for: 20 -> 100; matrix products, arithmetic and copies ran while one was open for 0% -> 0% of each run, Pallas kernels for 0% -> 0%
where the time goes in v1:
time: 1180 us; the launch traced here: 1170 us
  waiting for transfers between devices  533 us (45%)
  starting transfers between devices  388 us (33%)
  local copies, waits for them, and re-layouts  85 us (7%)
  blocking collectives  69.9 us (6%)
  other arithmetic  39.1 us (3%)
  between operations  39.1 us (3%)
    ppermute x81, waiting for transfers between devices, all_sum(): lax.ppermute(values, axis, [(i, i ^ stride) for i in range(count)])  373 us
    ppermute x81, starting transfers between devices, all_sum(): lax.ppermute(values, axis, [(i, i ^ stride) for i in range(count)])  196 us
    ppermute x8, starting transfers between devices, with_halo(): after = lax.ppermute(leading, axis, down)  102 us
    all_to_all x8, waiting for transfers between devices, operate(): lax.all_to_all(fluxes, 'harm', split_axis=0, concat_axis=2, tiled=True)  102 us
    all_to_all x4, blocking collectives, operate(): lax.all_to_all(gradients, 'harm', split_axis=2, concat_axis=0, tiled=True)  69.9 us
    all_to_all x4, waiting for transfers between devices, operate(): lax.all_to_all(gradients, 'harm', split_axis=2, concat_axis=0, tiled=True)  49.8 us
    gather x16, local copies, waits for them, and re-layouts, operate(): extended[:, ext_index]  47.9 us
    all_to_all x8, starting transfers between devices, operate(): lax.all_to_all(fluxes, 'harm', split_axis=0, concat_axis=2, tiled=True)  42.9 us
  transfers between devices with their start and end apart: 109, of which 100 were waited for; matrix products, arithmetic and copies ran while one was open for 0% of the time, Pallas kernels for 0%

profile of v1, /device:TPU:6, one launch (start us, length us, event | category | flops | bytes accessed | tf_op | source)
XLA Modules:
  0.0 1165.1 jit_solution(5116992246322767686)
XLA Ops:
  3.3 15.0 %collective-permute-start.1 = (f32[8,64]{1,0:T(8,128)S(1)}, f32[8,64]{1,0:T(8,128)S(1)}, u32[]{:S(2)}, u32[]{:S(2)}) collective-permute-start(f32[8,64]{1,0:T(8,128)S(1)} %get-tuple-element.76), channel_id=1, source_target_pairs={{1,0},{2,1},{3,2},{4,3},{5,4},{6,5},{7,6},{8,7},{9,8},{10,9},{11,1... | collective-permute-start | bytes 6152 | tf_op jit(solution)/shard_map/ppermute | solution.py:18
  20.4 5.5 gather_fusion
  27.9 15.3 %all-to-all-start = ((f32[8,1,2048]{2,1,0:T(1,128)}), f32[8,1,2048]{2,1,0:T(1,128)S(1)}, u32[]{:S(2)}, u32[]{:S(2)}) async-start(f32[8,1,2048]{2,1,0:T(1,128)} %reshape.355), calls=%async_computation | async-start | bytes 131072 | tf_op jit(solution)/shard_map/all_to_all | solution.py:112
  44.0 12.3 %all-to-all-done = f32[8,1,2048]{2,1,0:T(1,128)S(1)} async-done(((f32[8,1,2048]{2,1,0:T(1,128)}), f32[8,1,2048]{2,1,0:T(1,128)S(1)}, u32[]{:S(2)}, u32[]{:S(2)}) %all-to-all-start) | async-done | bytes 65568 | tf_op jit(solution)/shard_map/all_to_all | solution.py:112
  61.0 5.4 all-to-all-start.1
  66.6 12.8 %all-to-all-done.1 = f32[8,1,2048]{2,1,0:T(1,128)S(1)} async-done(((f32[8,1,2048]{2,1,0:T(1,128)}), f32[8,1,2048]{2,1,0:T(1,128)S(1)}, u32[]{:S(2)}, u32[]{:S(2)}) %all-to-all-start.1) | async-done | bytes 65568 | tf_op jit(solution)/shard_map/all_to_all | solution.py:118
  85.7 11.5 collective-permute-done.2
  122.6 5.0 collective-permute-done.7
  141.4 7.4 collective-permute-done.10
  153.3 12.4 %collective-permute-start.12 = (f32[8,64]{1,0:T(8,128)S(1)}, f32[8,64]{1,0:T(8,128)S(1)}, u32[]{:S(2)}, u32[]{:S(2)}) collective-permute-start(f32[8,64]{1,0:T(8,128)S(1)} %get-tuple-element.73), channel_id=1, source_target_pairs={{1,0},{2,1},{3,2},{4,3},{5,4},{6,5},{7,6},{8,7},{9,8},{10,9},{11,1... | collective-permute-start | bytes 6152 | tf_op jit(solution)/shard_map/ppermute | solution.py:18
  167.2 5.5 gather_fusion.1
  174.1 17.5 %all_to_all.192 = f32[8,1,2048]{2,1,0:T(1,128)S(1)} all-to-all(f32[8,1,2048]{2,1,0:T(1,128)S(1)} %reshape.359), channel_id=1, replica_groups=mesh['harm'=8,'space'=64] {'harm'}, dimensions={0} | all-to-all | bytes 131072 | tf_op jit(solution)/shard_map/all_to_all | solution.py:112
  195.8 5.4 all-to-all-start.3
  201.3 12.8 %all-to-all-done.3 = f32[8,1,2048]{2,1,0:T(1,128)S(1)} async-done(((f32[8,1,2048]{2,1,0:T(1,128)}), f32[8,1,2048]{2,1,0:T(1,128)S(1)}, u32[]{:S(2)}, u32[]{:S(2)}) %all-to-all-start.3) | async-done | bytes 65568 | tf_op jit(solution)/shard_map/all_to_all | solution.py:118
  218.8 11.5 collective-permute-done.13
  272.6 7.4 collective-permute-done.21
  285.2 12.8 %collective-permute-start.23 = (f32[8,64]{1,0:T(8,128)S(1)}, f32[8,64]{1,0:T(8,128)S(1)}, u32[]{:S(2)}, u32[]{:S(2)}) collective-permute-start(f32[8,64]{1,0:T(8,128)S(1)} %get-tuple-element.70), channel_id=1, source_target_pairs={{1,0},{2,1},{3,2},{4,3},{5,4},{6,5},{7,6},{8,7},{9,8},{10,9},{11,1... | collective-permute-start | bytes 6152 | tf_op jit(solution)/shard_map/ppermute | solution.py:18
  299.1 5.5 gather_fusion.2
  305.9 17.5 %all_to_all.193 = f32[8,1,2048]{2,1,0:T(1,128)S(1)} all-to-all(f32[8,1,2048]{2,1,0:T(1,128)S(1)} %reshape.363), channel_id=1, replica_groups=mesh['harm'=8,'space'=64] {'harm'}, dimensions={0} | all-to-all | bytes 131072 | tf_op jit(solution)/shard_map/all_to_all | solution.py:112
  327.7 5.4 all-to-all-start.5
  333.2 12.8 %all-to-all-done.5 = f32[8,1,2048]{2,1,0:T(1,128)S(1)} async-done(((f32[8,1,2048]{2,1,0:T(1,128)}), f32[8,1,2048]{2,1,0:T(1,128)S(1)}, u32[]{:S(2)}, u32[]{:S(2)}) %all-to-all-start.5) | async-done | bytes 65568 | tf_op jit(solution)/shard_map/all_to_all | solution.py:118
  350.7 11.5 collective-permute-done.24
  404.5 7.4 collective-permute-done.32
  417.7 12.4 %collective-permute-start.34 = (f32[8,64]{1,0:T(8,128)S(1)}, f32[8,64]{1,0:T(8,128)S(1)}, u32[]{:S(2)}, u32[]{:S(2)}) collective-permute-start(f32[8,64]{1,0:T(8,128)S(1)} %get-tuple-element.68), channel_id=1, source_target_pairs={{1,0},{2,1},{3,2},{4,3},{5,4},{6,5},{7,6},{8,7},{9,8},{10,9},{11,1... | collective-permute-start | bytes 6152 | tf_op jit(solution)/shard_map/ppermute | solution.py:18
  431.6 5.5 gather_fusion.3
  439.0 5.4 all-to-all-start.6
  444.4 13.0 %all-to-all-done.6 = f32[8,1,2048]{2,1,0:T(1,128)S(1)} async-done(((f32[8,1,2048]{2,1,0:T(1,128)}), f32[8,1,2048]{2,1,0:T(1,128)S(1)}, u32[]{:S(2)}, u32[]{:S(2)}) %all-to-all-start.6) | async-done | bytes 65568 | tf_op jit(solution)/shard_map/all_to_all | solution.py:112
  461.7 5.4 all-to-all-start.7
  467.2 12.8 %all-to-all-done.7 = f32[8,1,2048]{2,1,0:T(1,128)S(1)} async-done(((f32[8,1,2048]{2,1,0:T(1,128)}), f32[8,1,2048]{2,1,0:T(1,128)S(1)}, u32[]{:S(2)}, u32[]{:S(2)}) %all-to-all-start.7) | async-done | bytes 65568 | tf_op jit(solution)/shard_map/all_to_all | solution.py:118
  484.6 11.5 collective-permute-done.35
  538.5 7.4 collective-permute-done.43
  552.5 12.5 %collective-permute-start.45 = (f32[8,64]{1,0:T(8,128)S(1)}, f32[8,64]{1,0:T(8,128)S(1)}, u32[]{:S(2)}, u32[]{:S(2)}) collective-permute-start(f32[8,64]{1,0:T(8,128)S(1)} %get-tuple-element.66), channel_id=1, source_target_pairs={{1,0},{2,1},{3,2},{4,3},{5,4},{6,5},{7,6},{8,7},{9,8},{10,9},{11,1... | collective-permute-start | bytes 6152 | tf_op jit(solution)/shard_map/ppermute | solution.py:18
  566.4 5.5 gather_fusion.4
  573.8 5.4 all-to-all-start.8
  579.2 13.0 %all-to-all-done.8 = f32[8,1,2048]{2,1,0:T(1,128)S(1)} async-done(((f32[8,1,2048]{2,1,0:T(1,128)}), f32[8,1,2048]{2,1,0:T(1,128)S(1)}, u32[]{:S(2)}, u32[]{:S(2)}) %all-to-all-start.8) | async-done | bytes 65568 | tf_op jit(solution)/shard_map/all_to_all | solution.py:112
  596.5 5.4 all-to-all-start.9
  602.0 12.8 %all-to-all-done.9 = f32[8,1,2048]{2,1,0:T(1,128)S(1)} async-done(((f32[8,1,2048]{2,1,0:T(1,128)}), f32[8,1,2048]{2,1,0:T(1,128)S(1)}, u32[]{:S(2)}, u32[]{:S(2)}) %all-to-all-start.9) | async-done | bytes 65568 | tf_op jit(solution)/shard_map/all_to_all | solution.py:118
  619.5 11.5 collective-permute-done.46
  673.3 7.4 collective-permute-done.54
  687.9 12.4 %collective-permute-start.56 = (f32[8,64]{1,0:T(8,128)S(1)}, f32[8,64]{1,0:T(8,128)S(1)}, u32[]{:S(2)}, u32[]{:S(2)}) collective-permute-start(f32[8,64]{1,0:T(8,128)S(1)} %get-tuple-element.64), channel_id=1, source_target_pairs={{1,0},{2,1},{3,2},{4,3},{5,4},{6,5},{7,6},{8,7},{9,8},{10,9},{11,1... | collective-permute-start | bytes 6152 | tf_op jit(solution)/shard_map/ppermute | solution.py:18
  701.8 5.5 gather_fusion.5
  708.7 17.5 %all_to_all.194 = f32[8,1,2048]{2,1,0:T(1,128)S(1)} all-to-all(f32[8,1,2048]{2,1,0:T(1,128)S(1)} %reshape.375), channel_id=1, replica_groups=mesh['harm'=8,'space'=64] {'harm'}, dimensions={0} | all-to-all | bytes 131072 | tf_op jit(solution)/shard_map/all_to_all | solution.py:112
  730.4 5.4 all-to-all-start.11
  735.9 12.8 %all-to-all-done.11 = f32[8,1,2048]{2,1,0:T(1,128)S(1)} async-done(((f32[8,1,2048]{2,1,0:T(1,128)}), f32[8,1,2048]{2,1,0:T(1,128)S(1)}, u32[]{:S(2)}, u32[]{:S(2)}) %all-to-all-start.11) | async-done | bytes 65568 | tf_op jit(solution)/shard_map/all_to_all | solution.py:118
  753.4 11.5 collective-permute-done.57
  807.3 7.4 collective-permute-done.65
  822.4 12.6 %collective-permute-start.67 = (f32[8,64]{1,0:T(8,128)S(1)}, f32[8,64]{1,0:T(8,128)S(1)}, u32[]{:S(2)}, u32[]{:S(2)}) collective-permute-start(f32[8,64]{1,0:T(8,128)S(1)} %get-tuple-element.51), channel_id=1, source_target_pairs={{1,0},{2,1},{3,2},{4,3},{5,4},{6,5},{7,6},{8,7},{9,8},{10,9},{11,1... | collective-permute-start | bytes 6152 | tf_op jit(solution)/shard_map/ppermute | solution.py:18
  836.2 5.5 gather_fusion.6
  843.1 17.5 %all_to_all.195 = f32[8,1,2048]{2,1,0:T(1,128)S(1)} all-to-all(f32[8,1,2048]{2,1,0:T(1,128)S(1)} %reshape.379), channel_id=1, replica_groups=mesh['harm'=8,'space'=64] {'harm'}, dimensions={0} | all-to-all | bytes 131072 | tf_op jit(solution)/shard_map/all_to_all | solution.py:112
  864.9 5.4 all-to-all-start.13
  870.4 12.8 %all-to-all-done.13 = f32[8,1,2048]{2,1,0:T(1,128)S(1)} async-done(((f32[8,1,2048]{2,1,0:T(1,128)}), f32[8,1,2048]{2,1,0:T(1,128)S(1)}, u32[]{:S(2)}, u32[]{:S(2)}) %all-to-all-start.13) | async-done | bytes 65568 | tf_op jit(solution)/shard_map/all_to_all | solution.py:118
  887.9 11.5 collective-permute-done.68
  941.7 7.4 collective-permute-done.76
  957.5 12.4 %collective-permute-start.78 = (f32[8,64]{1,0:T(8,128)S(1)}, f32[8,64]{1,0:T(8,128)S(1)}, u32[]{:S(2)}, u32[]{:S(2)}) collective-permute-start(f32[8,64]{1,0:T(8,128)S(1)} %get-tuple-element.40), channel_id=1, source_target_pairs={{1,0},{2,1},{3,2},{4,3},{5,4},{6,5},{7,6},{8,7},{9,8},{10,9},{11,1... | collective-permute-start | bytes 6152 | tf_op jit(solution)/shard_map/ppermute | solution.py:18
  971.3 5.5 gather_fusion.7
  978.8 5.4 all-to-all-start.14
  985.6 11.6 all-to-all-done.14
  1001.5 5.4 all-to-all-start.15
  1007.2 12.6 %all-to-all-done.15 = f32[8,1,2048]{2,1,0:T(1,128)S(1)} async-done(((f32[8,1,2048]{2,1,0:T(1,128)}), f32[8,1,2048]{2,1,0:T(1,128)S(1)}, u32[]{:S(2)}, u32[]{:S(2)}) %all-to-all-start.15) | async-done | bytes 65568 | tf_op jit(solution)/shard_map/all_to_all | solution.py:118
  1024.5 11.5 collective-permute-done.79
  1078.4 7.4 collective-permute-done.87
  1095.6 11.7 %collective-permute-done.88 = f32[1]{0:T(128)} collective-permute-done((f32[1]{0:T(128)}, f32[1]{0:T(128)}, u32[]{:S(2)}, u32[]{:S(2)}) %collective-permute-start.88) | collective-permute-done | bytes 36 | tf_op jit(solution)/shard_map/ppermute | solution.py:76
  1114.7 5.3 collective-permute-start.90
  1156.2 6.3 collective-permute-done.96
  (521 shorter events, 503.5 us)
Async XLA Ops:
  1.4 18.8 %collective-permute-start = (f32[8,64]{1,0:T(8,128)S(1)}, f32[8,64]{1,0:T(8,128)S(1)}, u32[]{:S(2)}, u32[]{:S(2)}) collective-permute-start(f32[8,64]{1,0:T(8,128)S(1)} %get-tuple-element.75), channel_id=1, source_target_pairs={{0,1},{1,2},{2,3},{3,4},{4,5},{5,6},{6,7},{7,8},{8,9},{9,10},{10,1... | collective-permute-start | bytes 6152 | tf_op jit(solution)/shard_map/ppermute | solution.py:17
  3.3 16.9 %collective-permute-start.1 = (f32[8,64]{1,0:T(8,128)S(1)}, f32[8,64]{1,0:T(8,128)S(1)}, u32[]{:S(2)}, u32[]{:S(2)}) collective-permute-start(f32[8,64]{1,0:T(8,128)S(1)} %get-tuple-element.76), channel_id=1, source_target_pairs={{1,0},{2,1},{3,2},{4,3},{5,4},{6,5},{7,6},{8,7},{9,8},{10,9},{11,1... | collective-permute-start | bytes 6152 | tf_op jit(solution)/shard_map/ppermute | solution.py:18
  27.9 28.3 %all-to-all-start = ((f32[8,1,2048]{2,1,0:T(1,128)}), f32[8,1,2048]{2,1,0:T(1,128)S(1)}, u32[]{:S(2)}, u32[]{:S(2)}) async-start(f32[8,1,2048]{2,1,0:T(1,128)} %reshape.355), calls=%async_computation | async-start | bytes 131072 | tf_op jit(solution)/shard_map/all_to_all | solution.py:112
  61.0 18.3 %all-to-all-start.1 = ((f32[8,1,2048]{2,1,0:T(1,128)}), f32[8,1,2048]{2,1,0:T(1,128)S(1)}, u32[]{:S(2)}, u32[]{:S(2)}) async-start(f32[8,1,2048]{2,1,0:T(1,128)} %reshape.357), calls=%async_computation.1 | async-start | bytes 131072 | tf_op jit(solution)/shard_map/all_to_all | solution.py:118
  83.0 14.2 %collective-permute-start.2 = (f32[2]{0:T(128)S(1)}, f32[2]{0:T(128)S(1)}, u32[]{:S(2)}, u32[]{:S(2)}) collective-permute-start(f32[2]{0:T(128)S(1)} %pad_maximum_fusion.8), channel_id=1, source_target_pairs={{0,64},{64,0},{128,192},{192,128},{256,320},{320,256},{384,448},{4... | collective-permute-start | bytes 32 | tf_op jit(solution)/shard_map/ppermute | solution.py:76
  105.2 7.0 collective-permute-start.4
  120.7 7.0 collective-permute-start.7
  139.4 9.4 collective-permute-start.10
  151.4 14.4 %collective-permute-start.11 = (f32[8,64]{1,0:T(8,128)S(1)}, f32[8,64]{1,0:T(8,128)S(1)}, u32[]{:S(2)}, u32[]{:S(2)}) collective-permute-start(f32[8,64]{1,0:T(8,128)S(1)} %get-tuple-element.72), channel_id=1, source_target_pairs={{0,1},{1,2},{2,3},{3,4},{4,5},{5,6},{6,7},{7,8},{8,9},{9,10},{10,1... | collective-permute-start | bytes 6152 | tf_op jit(solution)/shard_map/ppermute | solution.py:17
  153.3 13.7 %collective-permute-start.12 = (f32[8,64]{1,0:T(8,128)S(1)}, f32[8,64]{1,0:T(8,128)S(1)}, u32[]{:S(2)}, u32[]{:S(2)}) collective-permute-start(f32[8,64]{1,0:T(8,128)S(1)} %get-tuple-element.73), channel_id=1, source_target_pairs={{1,0},{2,1},{3,2},{4,3},{5,4},{6,5},{7,6},{8,7},{9,8},{10,9},{11,1... | collective-permute-start | bytes 6152 | tf_op jit(solution)/shard_map/ppermute | solution.py:18
  195.8 18.3 %all-to-all-start.3 = ((f32[8,1,2048]{2,1,0:T(1,128)}), f32[8,1,2048]{2,1,0:T(1,128)S(1)}, u32[]{:S(2)}, u32[]{:S(2)}) async-start(f32[8,1,2048]{2,1,0:T(1,128)} %reshape.361), calls=%async_computation.3 | async-start | bytes 131072 | tf_op jit(solution)/shard_map/all_to_all | solution.py:118
  216.1 14.2 %collective-permute-start.13 = (f32[3]{0:T(128)S(1)}, f32[3]{0:T(128)S(1)}, u32[]{:S(2)}, u32[]{:S(2)}) collective-permute-start(f32[3]{0:T(128)S(1)} %pad_maximum_fusion.9), channel_id=1, source_target_pairs={{0,64},{64,0},{128,192},{192,128},{256,320},{320,256},{384,448},{4... | collective-permute-start | bytes 44 | tf_op jit(solution)/shard_map/ppermute | solution.py:76
  236.5 7.0 collective-permute-start.15
  251.9 7.0 collective-permute-start.18
  270.7 9.4 collective-permute-start.21
  283.3 14.9 %collective-permute-start.22 = (f32[8,64]{1,0:T(8,128)S(1)}, f32[8,64]{1,0:T(8,128)S(1)}, u32[]{:S(2)}, u32[]{:S(2)}) collective-permute-start(f32[8,64]{1,0:T(8,128)S(1)} %get-tuple-element.69), channel_id=1, source_target_pairs={{0,1},{1,2},{2,3},{3,4},{4,5},{5,6},{6,7},{7,8},{8,9},{9,10},{10,1... | collective-permute-start | bytes 6152 | tf_op jit(solution)/shard_map/ppermute | solution.py:17
  285.2 13.7 %collective-permute-start.23 = (f32[8,64]{1,0:T(8,128)S(1)}, f32[8,64]{1,0:T(8,128)S(1)}, u32[]{:S(2)}, u32[]{:S(2)}) collective-permute-start(f32[8,64]{1,0:T(8,128)S(1)} %get-tuple-element.70), channel_id=1, source_target_pairs={{1,0},{2,1},{3,2},{4,3},{5,4},{6,5},{7,6},{8,7},{9,8},{10,9},{11,1... | collective-permute-start | bytes 6152 | tf_op jit(solution)/shard_map/ppermute | solution.py:18
  327.7 18.3 %all-to-all-start.5 = ((f32[8,1,2048]{2,1,0:T(1,128)}), f32[8,1,2048]{2,1,0:T(1,128)S(1)}, u32[]{:S(2)}, u32[]{:S(2)}) async-start(f32[8,1,2048]{2,1,0:T(1,128)} %reshape.365), calls=%async_computation.5 | async-start | bytes 131072 | tf_op jit(solution)/shard_map/all_to_all | solution.py:118
  348.0 14.2 %collective-permute-start.24 = (f32[4]{0:T(128)S(1)}, f32[4]{0:T(128)S(1)}, u32[]{:S(2)}, u32[]{:S(2)}) collective-permute-start(f32[4]{0:T(128)S(1)} %pad_maximum_fusion.10), channel_id=1, source_target_pairs={{0,64},{64,0},{128,192},{192,128},{256,320},{320,256},{384,448},{4... | collective-permute-start | bytes 56 | tf_op jit(solution)/shard_map/ppermute | solution.py:76
  368.4 7.0 collective-permute-start.26
  383.8 7.0 collective-permute-start.29
  402.6 9.4 collective-permute-start.32
  415.8 14.4 %collective-permute-start.33 = (f32[8,64]{1,0:T(8,128)S(1)}, f32[8,64]{1,0:T(8,128)S(1)}, u32[]{:S(2)}, u32[]{:S(2)}) collective-permute-start(f32[8,64]{1,0:T(8,128)S(1)} %get-tuple-element.67), channel_id=1, source_target_pairs={{0,1},{1,2},{2,3},{3,4},{4,5},{5,6},{6,7},{7,8},{8,9},{9,10},{10,1... | collective-permute-start | bytes 6152 | tf_op jit(solution)/shard_map/ppermute | solution.py:17
  417.7 13.7 %collective-permute-start.34 = (f32[8,64]{1,0:T(8,128)S(1)}, f32[8,64]{1,0:T(8,128)S(1)}, u32[]{:S(2)}, u32[]{:S(2)}) collective-permute-start(f32[8,64]{1,0:T(8,128)S(1)} %get-tuple-element.68), channel_id=1, source_target_pairs={{1,0},{2,1},{3,2},{4,3},{5,4},{6,5},{7,6},{8,7},{9,8},{10,9},{11,1... | collective-permute-start | bytes 6152 | tf_op jit(solution)/shard_map/ppermute | solution.py:18
  439.0 18.3 %all-to-all-start.6 = ((f32[8,1,2048]{2,1,0:T(1,128)}), f32[8,1,2048]{2,1,0:T(1,128)S(1)}, u32[]{:S(2)}, u32[]{:S(2)}) async-start(f32[8,1,2048]{2,1,0:T(1,128)} %reshape.367), calls=%async_computation.6 | async-start | bytes 131072 | tf_op jit(solution)/shard_map/all_to_all | solution.py:112
  461.7 18.3 %all-to-all-start.7 = ((f32[8,1,2048]{2,1,0:T(1,128)}), f32[8,1,2048]{2,1,0:T(1,128)S(1)}, u32[]{:S(2)}, u32[]{:S(2)}) async-start(f32[8,1,2048]{2,1,0:T(1,128)} %reshape.369), calls=%async_computation.7 | async-start | bytes 131072 | tf_op jit(solution)/shard_map/all_to_all | solution.py:118
  482.0 14.2 %collective-permute-start.35 = (f32[5]{0:T(128)S(1)}, f32[5]{0:T(128)S(1)}, u32[]{:S(2)}, u32[]{:S(2)}) collective-permute-start(f32[5]{0:T(128)S(1)} %pad_maximum_fusion.11), channel_id=1, source_target_pairs={{0,64},{64,0},{128,192},{192,128},{256,320},{320,256},{384,448},{4... | collective-permute-start | bytes 68 | tf_op jit(solution)/shard_map/ppermute | solution.py:76
  502.4 7.0 collective-permute-start.37
  517.8 7.0 collective-permute-start.40
  536.6 9.4 collective-permute-start.43
  550.6 14.6 %collective-permute-start.44 = (f32[8,64]{1,0:T(8,128)S(1)}, f32[8,64]{1,0:T(8,128)S(1)}, u32[]{:S(2)}, u32[]{:S(2)}) collective-permute-start(f32[8,64]{1,0:T(8,128)S(1)} %get-tuple-element.65), channel_id=1, source_target_pairs={{0,1},{1,2},{2,3},{3,4},{4,5},{5,6},{6,7},{7,8},{8,9},{9,10},{10,1... | collective-permute-start | bytes 6152 | tf_op jit(solution)/shard_map/ppermute | solution.py:17
  552.5 13.7 %collective-permute-start.45 = (f32[8,64]{1,0:T(8,128)S(1)}, f32[8,64]{1,0:T(8,128)S(1)}, u32[]{:S(2)}, u32[]{:S(2)}) collective-permute-start(f32[8,64]{1,0:T(8,128)S(1)} %get-tuple-element.66), channel_id=1, source_target_pairs={{1,0},{2,1},{3,2},{4,3},{5,4},{6,5},{7,6},{8,7},{9,8},{10,9},{11,1... | collective-permute-start | bytes 6152 | tf_op jit(solution)/shard_map/ppermute | solution.py:18
  573.8 18.3 %all-to-all-start.8 = ((f32[8,1,2048]{2,1,0:T(1,128)}), f32[8,1,2048]{2,1,0:T(1,128)S(1)}, u32[]{:S(2)}, u32[]{:S(2)}) async-start(f32[8,1,2048]{2,1,0:T(1,128)} %reshape.371), calls=%async_computation.8 | async-start | bytes 131072 | tf_op jit(solution)/shard_map/all_to_all | solution.py:112
  596.5 18.3 %all-to-all-start.9 = ((f32[8,1,2048]{2,1,0:T(1,128)}), f32[8,1,2048]{2,1,0:T(1,128)S(1)}, u32[]{:S(2)}, u32[]{:S(2)}) async-start(f32[8,1,2048]{2,1,0:T(1,128)} %reshape.373), calls=%async_computation.9 | async-start | bytes 131072 | tf_op jit(solution)/shard_map/all_to_all | solution.py:118
  616.8 14.2 %collective-permute-start.46 = (f32[6]{0:T(128)S(1)}, f32[6]{0:T(128)S(1)}, u32[]{:S(2)}, u32[]{:S(2)}) collective-permute-start(f32[6]{0:T(128)S(1)} %pad_maximum_fusion.12), channel_id=1, source_target_pairs={{0,64},{64,0},{128,192},{192,128},{256,320},{320,256},{384,448},{4... | collective-permute-start | bytes 80 | tf_op jit(solution)/shard_map/ppermute | solution.py:76
  637.2 7.0 collective-permute-start.48
  652.6 7.0 collective-permute-start.51
  671.4 9.4 collective-permute-start.54
  686.0 14.4 %collective-permute-start.55 = (f32[8,64]{1,0:T(8,128)S(1)}, f32[8,64]{1,0:T(8,128)S(1)}, u32[]{:S(2)}, u32[]{:S(2)}) collective-permute-start(f32[8,64]{1,0:T(8,128)S(1)} %get-tuple-element.63), channel_id=1, source_target_pairs={{0,1},{1,2},{2,3},{3,4},{4,5},{5,6},{6,7},{7,8},{8,9},{9,10},{10,1... | collective-permute-start | bytes 6152 | tf_op jit(solution)/shard_map/ppermute | solution.py:17
  687.9 13.7 %collective-permute-start.56 = (f32[8,64]{1,0:T(8,128)S(1)}, f32[8,64]{1,0:T(8,128)S(1)}, u32[]{:S(2)}, u32[]{:S(2)}) collective-permute-start(f32[8,64]{1,0:T(8,128)S(1)} %get-tuple-element.64), channel_id=1, source_target_pairs={{1,0},{2,1},{3,2},{4,3},{5,4},{6,5},{7,6},{8,7},{9,8},{10,9},{11,1... | collective-permute-start | bytes 6152 | tf_op jit(solution)/shard_map/ppermute | solution.py:18
  730.4 18.3 %all-to-all-start.11 = ((f32[8,1,2048]{2,1,0:T(1,128)}), f32[8,1,2048]{2,1,0:T(1,128)S(1)}, u32[]{:S(2)}, u32[]{:S(2)}) async-start(f32[8,1,2048]{2,1,0:T(1,128)} %reshape.377), calls=%async_computation.11 | async-start | bytes 131072 | tf_op jit(solution)/shard_map/all_to_all | solution.py:118
  750.8 14.2 %collective-permute-start.57 = (f32[7]{0:T(128)S(1)}, f32[7]{0:T(128)S(1)}, u32[]{:S(2)}, u32[]{:S(2)}) collective-permute-start(f32[7]{0:T(128)S(1)} %pad_maximum_fusion.13), channel_id=1, source_target_pairs={{0,64},{64,0},{128,192},{192,128},{256,320},{320,256},{384,448},{4... | collective-permute-start | bytes 92 | tf_op jit(solution)/shard_map/ppermute | solution.py:76
  771.1 7.0 collective-permute-start.59
  786.6 7.0 collective-permute-start.62
  805.3 9.4 collective-permute-start.65
  820.4 14.6 %collective-permute-start.66 = (f32[8,64]{1,0:T(8,128)S(1)}, f32[8,64]{1,0:T(8,128)S(1)}, u32[]{:S(2)}, u32[]{:S(2)}) collective-permute-start(f32[8,64]{1,0:T(8,128)S(1)} %get-tuple-element.50), channel_id=1, source_target_pairs={{0,1},{1,2},{2,3},{3,4},{4,5},{5,6},{6,7},{7,8},{8,9},{9,10},{10,1... | collective-permute-start | bytes 6152 | tf_op jit(solution)/shard_map/ppermute | solution.py:17
  822.4 13.7 %collective-permute-start.67 = (f32[8,64]{1,0:T(8,128)S(1)}, f32[8,64]{1,0:T(8,128)S(1)}, u32[]{:S(2)}, u32[]{:S(2)}) collective-permute-start(f32[8,64]{1,0:T(8,128)S(1)} %get-tuple-element.51), channel_id=1, source_target_pairs={{1,0},{2,1},{3,2},{4,3},{5,4},{6,5},{7,6},{8,7},{9,8},{10,9},{11,1... | collective-permute-start | bytes 6152 | tf_op jit(solution)/shard_map/ppermute | solution.py:18
  864.9 18.3 %all-to-all-start.13 = ((f32[8,1,2048]{2,1,0:T(1,128)}), f32[8,1,2048]{2,1,0:T(1,128)S(1)}, u32[]{:S(2)}, u32[]{:S(2)}) async-start(f32[8,1,2048]{2,1,0:T(1,128)} %reshape.381), calls=%async_computation.13 | async-start | bytes 131072 | tf_op jit(solution)/shard_map/all_to_all | solution.py:118
  885.2 14.2 %collective-permute-start.68 = (f32[8]{0:T(128)S(1)}, f32[8]{0:T(128)S(1)}, u32[]{:S(2)}, u32[]{:S(2)}) collective-permute-start(f32[8]{0:T(128)S(1)} %pad_maximum_fusion.14), channel_id=1, source_target_pairs={{0,64},{64,0},{128,192},{192,128},{256,320},{320,256},{384,448},{4... | collective-permute-start | bytes 104 | tf_op jit(solution)/shard_map/ppermute | solution.py:76
  905.6 7.0 collective-permute-start.70
  921.0 7.0 collective-permute-start.73
  939.8 9.4 collective-permute-start.76
  955.6 14.4 %collective-permute-start.77 = (f32[8,64]{1,0:T(8,128)S(1)}, f32[8,64]{1,0:T(8,128)S(1)}, u32[]{:S(2)}, u32[]{:S(2)}) collective-permute-start(f32[8,64]{1,0:T(8,128)S(1)} %get-tuple-element.39), channel_id=1, source_target_pairs={{0,1},{1,2},{2,3},{3,4},{4,5},{5,6},{6,7},{7,8},{8,9},{9,10},{10,1... | collective-permute-start | bytes 6152 | tf_op jit(solution)/shard_map/ppermute | solution.py:17
  957.5 13.7 %collective-permute-start.78 = (f32[8,64]{1,0:T(8,128)S(1)}, f32[8,64]{1,0:T(8,128)S(1)}, u32[]{:S(2)}, u32[]{:S(2)}) collective-permute-start(f32[8,64]{1,0:T(8,128)S(1)} %get-tuple-element.40), channel_id=1, source_target_pairs={{1,0},{2,1},{3,2},{4,3},{5,4},{6,5},{7,6},{8,7},{9,8},{10,9},{11,1... | collective-permute-start | bytes 6152 | tf_op jit(solution)/shard_map/ppermute | solution.py:18
  978.8 18.3 %all-to-all-start.14 = ((f32[8,1,2048]{2,1,0:T(1,128)}), f32[8,1,2048]{2,1,0:T(1,128)S(1)}, u32[]{:S(2)}, u32[]{:S(2)}) async-start(f32[8,1,2048]{2,1,0:T(1,128)} %reshape.383), calls=%async_computation.14 | async-start | bytes 131072 | tf_op jit(solution)/shard_map/all_to_all | solution.py:112
  1001.5 18.3 %all-to-all-start.15 = ((f32[8,1,2048]{2,1,0:T(1,128)}), f32[8,1,2048]{2,1,0:T(1,128)S(1)}, u32[]{:S(2)}, u32[]{:S(2)}) async-start(f32[8,1,2048]{2,1,0:T(1,128)} %reshape.385), calls=%async_computation.15 | async-start | bytes 131072 | tf_op jit(solution)/shard_map/all_to_all | solution.py:118
  1021.9 14.2 %collective-permute-start.79 = (f32[9]{0:T(128)S(1)}, f32[9]{0:T(128)S(1)}, u32[]{:S(2)}, u32[]{:S(2)}) collective-permute-start(f32[9]{0:T(128)S(1)} %pad_maximum_fusion.15), channel_id=1, source_target_pairs={{0,64},{64,0},{128,192},{192,128},{256,320},{320,256},{384,448},{4... | collective-permute-start | bytes 116 | tf_op jit(solution)/shard_map/ppermute | solution.py:76
  1042.2 7.0 collective-permute-start.81
  1057.7 7.0 collective-permute-start.84
  1076.4 9.4 collective-permute-start.87
  1092.9 14.4 %collective-permute-start.88 = (f32[1]{0:T(128)}, f32[1]{0:T(128)}, u32[]{:S(2)}, u32[]{:S(2)}) collective-permute-start(f32[1]{0:T(128)} %bitcast.133), channel_id=1, source_target_pairs={{0,64},{64,0},{128,192},{192,128},{256,320},{320,256},{384,448},{4... | collective-permute-start | bytes 20 | tf_op jit(solution)/shard_map/ppermute | solution.py:76
  1114.7 7.1 collective-permute-start.90
  1132.2 7.1 collective-permute-start.93
  1153.0 9.5 collective-permute-start.96
  (51 other events, 254.3 us)

commit v2 on v1

--- a/solution.py
+++ b/solution.py
@@ -81,47 +81,56 @@
 def per_device(rhs_field, neighbors, nu_mean, nu_ripple, mass_coeff, eddy_coeff):
     block, nodes_own = rhs_field.shape
     harmonics = nu_ripple.shape[0]
-    halo_width = IF
-    harm_start = lax.axis_index("harm") * block
-    kernel = nu_ripple.at[0].add(nu_mean)
+    harm_count = lax.axis_size("harm")
+    harm_index = lax.axis_index("harm")
+    chunk = nodes_own // harm_count
+    devices = harm_count * lax.axis_size("space")
+    total_nodes = chunk * devices
+    reach = -(-IF // chunk)
+    block_index = lax.axis_index("space") * harm_count + harm_index
+    take = lambda array: lax.dynamic_slice_in_dim(array, harm_index * chunk, chunk, array.ndim - 1)
+    kernel = take(nu_ripple).at[0].add(take(nu_mean))
+    mass = take(mass_coeff)
+    eddy = take(eddy_coeff)
     cos_table, sin_table = fourier_tables(harmonics)
-    total_nodes = nodes_own * lax.axis_size("space")
-    relative = jnp.mod(neighbors - lax.axis_index("space") * nodes_own, total_nodes)
-    relative = jnp.where(relative >= total_nodes - halo_width, relative - total_nodes, relative)
-    ext_index = relative + halo_width
-    global_harm = harm_start + jnp.arange(block)
-    harm_order = (global_harm // 2 + 1).astype(jnp.float32)
-    sign_vals = jnp.where(global_harm % 2 == 0, 1.0, -1.0).astype(jnp.float32)
+    relative = jnp.mod(take(neighbors) - block_index * chunk, total_nodes)
+    relative = jnp.where(relative >= total_nodes - reach * chunk, relative - total_nodes, relative)
+    ext_index = relative + reach * chunk
+    all_harm = jnp.arange(harmonics)
+    harm_order = (all_harm // 2 + 1).astype(jnp.float32)
+    sign_vals = jnp.where(all_harm % 2 == 0, 1.0, -1.0).astype(jnp.float32)
     factor = 4.0 * harm_order / harmonics * sign_vals
-    node_share = nodes_own // lax.axis_size("harm")
-    kernel_use = lax.dynamic_slice_in_dim(
-        kernel, lax.axis_index("harm") * node_share, node_share, 2
-    )
-    kernel_flat = kernel_use.reshape(harmonics, -1)
+    kernel_flat = kernel.reshape(harmonics, -1)
     kernel_real = matmul_high(cos_table, kernel_flat)
     kernel_imag = -matmul_high(sin_table, kernel_flat)
 
-    def convolve_spectrum(spec_real, spec_imag, out_cos, out_sin):
+    def device_of(b):
+        b = b % devices
+        return (b % harm_count) * lax.axis_size("space") + b // harm_count
+
+    def shifted(vector_in, step):
+        pairs = [(device_of(b), device_of(b + step)) for b in range(devices)]
+        return lax.ppermute(vector_in, ("harm", "space"), pairs)
+
+    def operate(vector_in):
+        pieces = [shifted(vector_in, r) for r in range(reach, 0, -1)]
+        pieces += [vector_in] + [shifted(vector_in, -r) for r in range(1, reach + 1)]
+        extended = jnp.concatenate(pieces, axis=1)
+        gradients = vector_in[:, None, :] - extended[:, ext_index]
+        grad_flat = gradients.reshape(harmonics, -1)
+        spec_real = matmul_high(cos_table, grad_flat)
+        spec_imag = -matmul_high(sin_table, grad_flat)
         prod_real = spec_real * kernel_real - spec_imag * kernel_imag
         prod_imag = spec_real * kernel_imag + spec_imag * kernel_real
-        return (matmul_high(out_cos, prod_real) - matmul_high(out_sin, prod_imag)) / harmonics
-
-    def operate(vector_in):
-        extended = with_halo(vector_in, (("space", 1),), halo_width)
-        gradients = extended[:, None, halo_width : halo_width + nodes_own] - extended[:, ext_index]
-        spread = lax.all_to_all(gradients, "harm", split_axis=2, concat_axis=0, tiled=True)
-        spread_flat = spread.reshape(harmonics, -1)
-        spec_real = matmul_high(cos_table, spread_flat)
-        spec_imag = -matmul_high(sin_table, spread_flat)
-        fluxes = convolve_spectrum(spec_real, spec_imag, cos_table, sin_table)
-        fluxes = fluxes.reshape(spread.shape)
-        fluxes = lax.all_to_all(fluxes, "harm", split_axis=0, concat_axis=2, tiled=True)
+        fluxes = (matmul_high(cos_table, prod_real) - matmul_high(sin_table, prod_imag)) / harmonics
+        fluxes = fluxes.reshape(gradients.shape)
         return (
             jnp.sum(fluxes, axis=1)
-            + mass_coeff[None, :] * vector_in
-            + eddy_coeff[None, :] * factor[:, None] * swap_pairs(vector_in)
+            + mass[None, :] * vector_in
+            + eddy[None, :] * factor[:, None] * swap_pairs(vector_in)
         )
 
+    rhs_field = lax.all_to_all(rhs_field, "harm", split_axis=1, concat_axis=0, tiled=True)
     local_rows = lambda rows, other: jnp.sum(jnp.stack(rows) * other[None], axis=(1, 2))
     sums = all_sum(jnp.concatenate([local_rows([rhs_field], rhs_field), local_rows([rhs_field], image := operate(rhs_field))]))
     beta_norm = jnp.sqrt(sums[0])
@@ -151,7 +160,8 @@
         correction = correction + coeffs[j] * krylov[j]
         applied = applied + coeffs[j] * images[j]
     residual = rhs_field - applied
-    return (correction, residual)
+    both = lax.all_to_all(jnp.stack([correction, residual]), "harm", split_axis=1, concat_axis=2, tiled=True)
+    return (both[0], both[1])
 
 
 def solution(mesh):

time: 1180 us -> 1010 us (0.86); the launches traced: 1170 us -> 1010 us
  waiting for transfers between devices: 533 us -> 364 us
  starting transfers between devices: 388 us -> 525 us
  local copies, waits for them, and re-layouts: 85 us -> 21.4 us
  blocking collectives: 69.9 us -> 21.1 us
  other arithmetic: 39.1 us -> 26.5 us
    ppermute x81, starting transfers between devices: 196 us -> 343 us  [all_sum(): lax.ppermute(values, axis, [(i, i ^ stride) for i in range(count)])]
    all_to_all x12 -> x1, waiting for transfers between devices: 152 us -> 7.72 us  [per_device(): lax.all_to_all(rhs_field, 'harm', split_axis=1, concat_axis=0, tiled=True)]
    ppermute x81, waiting for transfers between devices: 373 us -> 310 us  [all_sum(): lax.ppermute(values, axis, [(i, i ^ stride) for i in range(count)])]
    all_to_all x12 -> x1, starting transfers between devices: 74.3 us -> 18 us  [per_device(): lax.all_to_all(rhs_field, 'harm', split_axis=1, concat_axis=0, tiled=True)]
    all_to_all x4 -> x1, blocking collectives: 69.9 us -> 21.1 us  [per_device(): lax.all_to_all(jnp.stack([correction, residual]), 'harm', split_axis=1, c...]
    ppermute x16 -> x32, starting transfers between devices: 118 us -> 164 us  [shifted(): return lax.ppermute(vector_in, ('harm', 'space'), pairs)]
    gather x16 -> x8, local copies, waits for them, and re-layouts: 47.9 us -> 5.83 us  [operate(): gradients = vector_in[:, None, :] - extended[:, ext_index]]
    ppermute x16 -> x32, waiting for transfers between devices: 7.35 us -> 46.6 us  [shifted(): return lax.ppermute(vector_in, ('harm', 'space'), pairs)]
  transfers between devices with their start and end apart: 109 -> 114, of which waited for: 100 -> 91; matrix products, arithmetic and copies ran while one was open for 0% -> 1% of each run, Pallas kernels for 0% -> 0%
where the time goes in v2:
time: 1010 us
  starting transfers between devices  525 us (52%)
  waiting for transfers between devices  364 us (36%)
  between operations  39.4 us (4%)
  other arithmetic  26.5 us (3%)
  local copies, waits for them, and re-layouts  21.4 us (2%)
  blocking collectives  21.1 us (2%)
  matrix products  12 us (1%)
    ppermute x81, starting transfers between devices, all_sum(): lax.ppermute(values, axis, [(i, i ^ stride) for i in range(count)])  343 us
    ppermute x81, waiting for transfers between devices, all_sum(): lax.ppermute(values, axis, [(i, i ^ stride) for i in range(count)])  310 us
    ppermute x32, starting transfers between devices, shifted(): return lax.ppermute(vector_in, ('harm', 'space'), pairs)  164 us
    ppermute x32, waiting for transfers between devices, shifted(): return lax.ppermute(vector_in, ('harm', 'space'), pairs)  46.6 us
    all_to_all x1, blocking collectives, per_device(): lax.all_to_all(jnp.stack([correction, residual]), 'harm', split_axis=1, c...  21.1 us
  transfers between devices with their start and end apart: 114, of which 91 were waited for; matrix products, arithmetic and copies ran while one was open for 1% of the time, Pallas kernels for 0%

profile of v2, /device:TPU:6, one launch (start us, length us, event | category | flops | bytes accessed | tf_op | source)
XLA Modules:
  0.0 1009.9 jit_solution(10012233702237796550)
XLA Ops:
  2.1 18.0 %all-to-all-start = ((f32[8,1,256]{2,1,0:T(1,128)}), f32[8,1,256]{2,1,0:T(1,128)S(1)}, u32[]{:S(2)}, u32[]{:S(2)}) async-start(f32[8,1,256]{2,1,0:T(1,128)} %reshape.5744), calls=%async_computation | async-start | bytes 16384 | tf_op jit(solution)/shard_map/all_to_all | solution.py:133
  25.2 7.7 all-to-all-done
  41.5 9.9 collective-permute-start.1
  61.6 8.7 collective-permute-start.4
  70.3 5.5 collective-permute-done.4
  84.0 17.9 %collective-permute-start.6 = (f32[2]{0:T(128)S(1)}, f32[2]{0:T(128)S(1)}, u32[]{:S(2)}, u32[]{:S(2)}) collective-permute-start(f32[2]{0:T(128)S(1)} %fusion.465), channel_id=1, source_target_pairs={{0,256},{64,320},{128,384},{192,448},{256,0},{320,64},{384,128},{4... | collective-permute-start | bytes 32 | tf_op jit(solution)/shard_map/ppermute | solution.py:76
  113.9 5.0 collective-permute-done.9
  132.6 7.4 collective-permute-done.12
  145.5 7.6 collective-permute-start.15
  153.2 6.9 collective-permute-start.14
  171.7 6.0 collective-permute-start.17
  177.8 8.1 collective-permute-done.17
  192.1 11.6 %collective-permute-start.19 = (f32[3]{0:T(128)S(1)}, f32[3]{0:T(128)S(1)}, u32[]{:S(2)}, u32[]{:S(2)}) collective-permute-start(f32[3]{0:T(128)S(1)} %add.2062), channel_id=1, source_target_pairs={{0,256},{64,320},{128,384},{192,448},{256,0},{320,64},{384,128},{4... | collective-permute-start | bytes 44 | tf_op jit(solution)/shard_map/ppermute | solution.py:76
  215.6 5.0 collective-permute-done.22
  234.4 7.4 collective-permute-done.25
  252.0 7.9 collective-permute-start.28
  260.0 6.6 collective-permute-start.27
  266.8 8.4 collective-permute-done.27
  278.5 5.7 collective-permute-start.30
  284.2 8.4 collective-permute-done.30
  298.8 16.5 %collective-permute-start.32 = (f32[4]{0:T(128)S(1)}, f32[4]{0:T(128)S(1)}, u32[]{:S(2)}, u32[]{:S(2)}) collective-permute-start(f32[4]{0:T(128)S(1)} %add.2082), channel_id=1, source_target_pairs={{0,256},{64,320},{128,384},{192,448},{256,0},{320,64},{384,128},{4... | collective-permute-start | bytes 56 | tf_op jit(solution)/shard_map/ppermute | solution.py:76
  327.3 5.0 collective-permute-done.35
  346.1 7.4 collective-permute-done.38
  363.8 6.1 collective-permute-start.41
  369.8 8.5 collective-permute-start.40
  378.5 6.6 collective-permute-done.40
  388.5 7.6 collective-permute-start.43
  396.0 6.6 collective-permute-done.43
  408.8 16.5 %collective-permute-start.45 = (f32[5]{0:T(128)S(1)}, f32[5]{0:T(128)S(1)}, u32[]{:S(2)}, u32[]{:S(2)}) collective-permute-start(f32[5]{0:T(128)S(1)} %add.2102), channel_id=1, source_target_pairs={{0,256},{64,320},{128,384},{192,448},{256,0},{320,64},{384,128},{4... | collective-permute-start | bytes 68 | tf_op jit(solution)/shard_map/ppermute | solution.py:76
  437.3 5.0 collective-permute-done.48
  456.1 7.4 collective-permute-done.51
  474.3 5.9 collective-permute-start.54
  480.2 8.8 collective-permute-start.53
  489.3 6.2 collective-permute-done.53
  498.8 7.7 collective-permute-start.56
  506.5 6.4 collective-permute-done.56
  519.1 16.5 %collective-permute-start.58 = (f32[6]{0:T(128)S(1)}, f32[6]{0:T(128)S(1)}, u32[]{:S(2)}, u32[]{:S(2)}) collective-permute-start(f32[6]{0:T(128)S(1)} %add.2122), channel_id=1, source_target_pairs={{0,256},{64,320},{128,384},{192,448},{256,0},{320,64},{384,128},{4... | collective-permute-start | bytes 80 | tf_op jit(solution)/shard_map/ppermute | solution.py:76
  547.6 5.0 collective-permute-done.61
  566.3 7.4 collective-permute-done.64
  585.2 6.1 collective-permute-start.67
  591.3 8.5 collective-permute-start.66
  600.0 6.5 collective-permute-done.66
  609.8 7.6 collective-permute-start.69
  617.4 6.6 collective-permute-done.69
  630.2 16.5 %collective-permute-start.71 = (f32[7]{0:T(128)S(1)}, f32[7]{0:T(128)S(1)}, u32[]{:S(2)}, u32[]{:S(2)}) collective-permute-start(f32[7]{0:T(128)S(1)} %add.2142), channel_id=1, source_target_pairs={{0,256},{64,320},{128,384},{192,448},{256,0},{320,64},{384,128},{4... | collective-permute-start | bytes 92 | tf_op jit(solution)/shard_map/ppermute | solution.py:76
  677.4 7.4 collective-permute-done.77
  697.0 5.9 collective-permute-start.80
  702.9 8.6 collective-permute-start.79
  711.7 6.4 collective-permute-done.79
  721.5 7.7 collective-permute-start.82
  729.2 6.4 collective-permute-done.82
  741.8 16.5 %collective-permute-start.84 = (f32[8]{0:T(128)S(1)}, f32[8]{0:T(128)S(1)}, u32[]{:S(2)}, u32[]{:S(2)}) collective-permute-start(f32[8]{0:T(128)S(1)} %add.2162), channel_id=1, source_target_pairs={{0,256},{64,320},{128,384},{192,448},{256,0},{320,64},{384,128},{4... | collective-permute-start | bytes 104 | tf_op jit(solution)/shard_map/ppermute | solution.py:76
  789.0 7.4 collective-permute-done.90
  809.3 6.1 collective-permute-start.93
  815.4 8.5 collective-permute-start.92
  824.1 6.5 collective-permute-done.92
  834.0 7.6 collective-permute-start.95
  841.6 6.6 collective-permute-done.95
  854.3 16.5 %collective-permute-start.97 = (f32[9]{0:T(128)S(1)}, f32[9]{0:T(128)S(1)}, u32[]{:S(2)}, u32[]{:S(2)}) collective-permute-start(f32[9]{0:T(128)S(1)} %add.2182), channel_id=1, source_target_pairs={{0,256},{64,320},{128,384},{192,448},{256,0},{320,64},{384,128},{4... | collective-permute-start | bytes 116 | tf_op jit(solution)/shard_map/ppermute | solution.py:76
  901.6 7.4 collective-permute-done.103
  921.4 9.3 collective-permute-done.104
  937.9 6.7 collective-permute-start.106
  978.9 6.1 collective-permute-done.112
  986.6 21.1 %all_to_all.34 = f32[8,1,512]{2,1,0:T(1,128)S(1)} all-to-all(f32[8,1,512]{2,1,0:T(1,128)S(1)} %reshape.5746), channel_id=1, replica_groups=mesh['harm'=8,'space'=64] {'harm'}, dimensions={0} | all-to-all | bytes 32768 | tf_op jit(solution)/shard_map/all_to_all | solution.py:163
  (493 shorter events, 422.5 us)
Async XLA Ops:
  2.1 30.9 %all-to-all-start = ((f32[8,1,256]{2,1,0:T(1,128)}), f32[8,1,256]{2,1,0:T(1,128)S(1)}, u32[]{:S(2)}, u32[]{:S(2)}) async-start(f32[8,1,256]{2,1,0:T(1,128)} %reshape.5744), calls=%async_computation | async-start | bytes 16384 | tf_op jit(solution)/shard_map/all_to_all | solution.py:133
  34.3 22.7 %collective-permute-start.3 = (f32[64,32]{0,1:T(8,128)S(1)}, f32[64,32]{0,1:T(8,128)S(1)}, u32[]{:S(2)}, u32[]{:S(2)}) collective-permute-start(f32[64,32]{0,1:T(8,128)S(1)} %copy.193), channel_id=1, source_target_pairs={{0,447},{64,511},{128,0},{192,64},{256,128},{320,192},{384,256},{4... | collective-permute-start | bytes 24584 | tf_op jit(solution)/shard_map/ppermute | solution.py:113
  36.8 20.2 %collective-permute-start.2 = (f32[64,32]{0,1:T(8,128)S(1)}, f32[64,32]{0,1:T(8,128)S(1)}, u32[]{:S(2)}, u32[]{:S(2)}) collective-permute-start(f32[64,32]{0,1:T(8,128)S(1)} %copy.193), channel_id=1, source_target_pairs={{0,511},{64,0},{128,64},{192,128},{256,192},{320,256},{384,320},{4... | collective-permute-start | bytes 24584 | tf_op jit(solution)/shard_map/ppermute | solution.py:113
  41.5 15.5 %collective-permute-start.1 = (f32[64,32]{0,1:T(8,128)S(1)}, f32[64,32]{0,1:T(8,128)S(1)}, u32[]{:S(2)}, u32[]{:S(2)}) collective-permute-start(f32[64,32]{0,1:T(8,128)S(1)} %copy.193), channel_id=1, source_target_pairs={{0,64},{64,128},{128,192},{192,256},{256,320},{320,384},{384,448},... | collective-permute-start | bytes 24584 | tf_op jit(solution)/shard_map/ppermute | solution.py:113
  61.6 14.2 %collective-permute-start.4 = (f32[2]{0:T(128)S(1)}, f32[2]{0:T(128)S(1)}, u32[]{:S(2)}, u32[]{:S(2)}) collective-permute-start(f32[2]{0:T(128)S(1)} %pad_maximum_fusion.1), channel_id=1, source_target_pairs={{0,64},{64,0},{128,192},{192,128},{256,320},{320,256},{384,448},{4... | collective-permute-start | bytes 32 | tf_op jit(solution)/shard_map/ppermute | solution.py:76
  84.0 19.4 %collective-permute-start.6 = (f32[2]{0:T(128)S(1)}, f32[2]{0:T(128)S(1)}, u32[]{:S(2)}, u32[]{:S(2)}) collective-permute-start(f32[2]{0:T(128)S(1)} %fusion.465), channel_id=1, source_target_pairs={{0,256},{64,320},{128,384},{192,448},{256,0},{320,64},{384,128},{4... | collective-permute-start | bytes 32 | tf_op jit(solution)/shard_map/ppermute | solution.py:76
  112.0 7.0 collective-permute-start.9
  130.7 9.4 collective-permute-start.12
  142.2 26.2 %collective-permute-start.16 = (f32[64,32]{0,1:T(8,128)S(1)}, f32[64,32]{0,1:T(8,128)S(1)}, u32[]{:S(2)}, u32[]{:S(2)}) collective-permute-start(f32[64,32]{0,1:T(8,128)S(1)} %fusion.206), channel_id=1, source_target_pairs={{0,447},{64,511},{128,0},{192,64},{256,128},{320,192},{384,256},{4... | collective-permute-start | bytes 24584 | tf_op jit(solution)/shard_map/ppermute | solution.py:113
  145.5 22.9 %collective-permute-start.15 = (f32[64,32]{0,1:T(8,128)S(1)}, f32[64,32]{0,1:T(8,128)S(1)}, u32[]{:S(2)}, u32[]{:S(2)}) collective-permute-start(f32[64,32]{0,1:T(8,128)S(1)} %fusion.206), channel_id=1, source_target_pairs={{0,511},{64,0},{128,64},{192,128},{256,192},{320,256},{384,320},{4... | collective-permute-start | bytes 24584 | tf_op jit(solution)/shard_map/ppermute | solution.py:113
  153.2 15.2 %collective-permute-start.14 = (f32[64,32]{0,1:T(8,128)S(1)}, f32[64,32]{0,1:T(8,128)S(1)}, u32[]{:S(2)}, u32[]{:S(2)}) collective-permute-start(f32[64,32]{0,1:T(8,128)S(1)} %fusion.206), channel_id=1, source_target_pairs={{0,64},{64,128},{128,192},{192,256},{256,320},{320,384},{384,448},... | collective-permute-start | bytes 24584 | tf_op jit(solution)/shard_map/ppermute | solution.py:113
  171.7 14.2 %collective-permute-start.17 = (f32[3]{0:T(128)S(1)}, f32[3]{0:T(128)S(1)}, u32[]{:S(2)}, u32[]{:S(2)}) collective-permute-start(f32[3]{0:T(128)S(1)} %pad_maximum_fusion.2), channel_id=1, source_target_pairs={{0,64},{64,0},{128,192},{192,128},{256,320},{320,256},{384,448},{4... | collective-permute-start | bytes 44 | tf_op jit(solution)/shard_map/ppermute | solution.py:76
  192.1 13.1 %collective-permute-start.19 = (f32[3]{0:T(128)S(1)}, f32[3]{0:T(128)S(1)}, u32[]{:S(2)}, u32[]{:S(2)}) collective-permute-start(f32[3]{0:T(128)S(1)} %add.2062), channel_id=1, source_target_pairs={{0,256},{64,320},{128,384},{192,448},{256,0},{320,64},{384,128},{4... | collective-permute-start | bytes 44 | tf_op jit(solution)/shard_map/ppermute | solution.py:76
  213.7 7.0 collective-permute-start.22
  232.5 9.4 collective-permute-start.25
  244.5 22.3 %collective-permute-start.26 = (f32[64,32]{0,1:T(8,128)S(1)}, f32[64,32]{0,1:T(8,128)S(1)}, u32[]{:S(2)}, u32[]{:S(2)}) collective-permute-start(f32[64,32]{0,1:T(8,128)S(1)} %multiply_subtract_fusion.11), channel_id=1, source_target_pairs={{0,128},{64,192},{128,256},{192,320},{256,384},{320,448},{384,1},{... | collective-permute-start | bytes 24584 | tf_op jit(solution)/shard_map/ppermute | solution.py:113
  248.1 27.1 %collective-permute-start.29 = (f32[64,32]{0,1:T(8,128)S(1)}, f32[64,32]{0,1:T(8,128)S(1)}, u32[]{:S(2)}, u32[]{:S(2)}) collective-permute-start(f32[64,32]{0,1:T(8,128)S(1)} %multiply_subtract_fusion.11), channel_id=1, source_target_pairs={{0,447},{64,511},{128,0},{192,64},{256,128},{320,192},{384,256},{4... | collective-permute-start | bytes 24584 | tf_op jit(solution)/shard_map/ppermute | solution.py:113
  252.0 23.2 %collective-permute-start.28 = (f32[64,32]{0,1:T(8,128)S(1)}, f32[64,32]{0,1:T(8,128)S(1)}, u32[]{:S(2)}, u32[]{:S(2)}) collective-permute-start(f32[64,32]{0,1:T(8,128)S(1)} %multiply_subtract_fusion.11), channel_id=1, source_target_pairs={{0,511},{64,0},{128,64},{192,128},{256,192},{320,256},{384,320},{4... | collective-permute-start | bytes 24584 | tf_op jit(solution)/shard_map/ppermute | solution.py:113
  260.0 15.2 %collective-permute-start.27 = (f32[64,32]{0,1:T(8,128)S(1)}, f32[64,32]{0,1:T(8,128)S(1)}, u32[]{:S(2)}, u32[]{:S(2)}) collective-permute-start(f32[64,32]{0,1:T(8,128)S(1)} %multiply_subtract_fusion.11), channel_id=1, source_target_pairs={{0,64},{64,128},{128,192},{192,256},{256,320},{320,384},{384,448},... | collective-permute-start | bytes 24584 | tf_op jit(solution)/shard_map/ppermute | solution.py:113
  278.5 14.2 %collective-permute-start.30 = (f32[4]{0:T(128)S(1)}, f32[4]{0:T(128)S(1)}, u32[]{:S(2)}, u32[]{:S(2)}) collective-permute-start(f32[4]{0:T(128)S(1)} %pad_maximum_fusion.3), channel_id=1, source_target_pairs={{0,64},{64,0},{128,192},{192,128},{256,320},{320,256},{384,448},{4... | collective-permute-start | bytes 56 | tf_op jit(solution)/shard_map/ppermute | solution.py:76
  298.8 18.0 %collective-permute-start.32 = (f32[4]{0:T(128)S(1)}, f32[4]{0:T(128)S(1)}, u32[]{:S(2)}, u32[]{:S(2)}) collective-permute-start(f32[4]{0:T(128)S(1)} %add.2082), channel_id=1, source_target_pairs={{0,256},{64,320},{128,384},{192,448},{256,0},{320,64},{384,128},{4... | collective-permute-start | bytes 56 | tf_op jit(solution)/shard_map/ppermute | solution.py:76
  325.4 7.0 collective-permute-start.35
  344.2 9.4 collective-permute-start.38
  356.8 21.7 %collective-permute-start.39 = (f32[64,32]{0,1:T(8,128)S(1)}, f32[64,32]{0,1:T(8,128)S(1)}, u32[]{:S(2)}, u32[]{:S(2)}) collective-permute-start(f32[64,32]{0,1:T(8,128)S(1)} %multiply_subtract_fusion.9), channel_id=1, source_target_pairs={{0,128},{64,192},{128,256},{192,320},{256,384},{320,448},{384,1},{... | collective-permute-start | bytes 24584 | tf_op jit(solution)/shard_map/ppermute | solution.py:113
  359.8 25.3 %collective-permute-start.42 = (f32[64,32]{0,1:T(8,128)S(1)}, f32[64,32]{0,1:T(8,128)S(1)}, u32[]{:S(2)}, u32[]{:S(2)}) collective-permute-start(f32[64,32]{0,1:T(8,128)S(1)} %multiply_subtract_fusion.9), channel_id=1, source_target_pairs={{0,447},{64,511},{128,0},{192,64},{256,128},{320,192},{384,256},{4... | collective-permute-start | bytes 24584 | tf_op jit(solution)/shard_map/ppermute | solution.py:113
  363.8 21.3 %collective-permute-start.41 = (f32[64,32]{0,1:T(8,128)S(1)}, f32[64,32]{0,1:T(8,128)S(1)}, u32[]{:S(2)}, u32[]{:S(2)}) collective-permute-start(f32[64,32]{0,1:T(8,128)S(1)} %multiply_subtract_fusion.9), channel_id=1, source_target_pairs={{0,511},{64,0},{128,64},{192,128},{256,192},{320,256},{384,320},{4... | collective-permute-start | bytes 24584 | tf_op jit(solution)/shard_map/ppermute | solution.py:113
  369.8 15.2 %collective-permute-start.40 = (f32[64,32]{0,1:T(8,128)S(1)}, f32[64,32]{0,1:T(8,128)S(1)}, u32[]{:S(2)}, u32[]{:S(2)}) collective-permute-start(f32[64,32]{0,1:T(8,128)S(1)} %multiply_subtract_fusion.9), channel_id=1, source_target_pairs={{0,64},{64,128},{128,192},{192,256},{256,320},{320,384},{384,448},... | collective-permute-start | bytes 24584 | tf_op jit(solution)/shard_map/ppermute | solution.py:113
  388.5 14.2 %collective-permute-start.43 = (f32[5]{0:T(128)S(1)}, f32[5]{0:T(128)S(1)}, u32[]{:S(2)}, u32[]{:S(2)}) collective-permute-start(f32[5]{0:T(128)S(1)} %pad_maximum_fusion.4), channel_id=1, source_target_pairs={{0,64},{64,0},{128,192},{192,128},{256,320},{320,256},{384,448},{4... | collective-permute-start | bytes 68 | tf_op jit(solution)/shard_map/ppermute | solution.py:76
  408.8 18.0 %collective-permute-start.45 = (f32[5]{0:T(128)S(1)}, f32[5]{0:T(128)S(1)}, u32[]{:S(2)}, u32[]{:S(2)}) collective-permute-start(f32[5]{0:T(128)S(1)} %add.2102), channel_id=1, source_target_pairs={{0,256},{64,320},{128,384},{192,448},{256,0},{320,64},{384,128},{4... | collective-permute-start | bytes 68 | tf_op jit(solution)/shard_map/ppermute | solution.py:76
  435.4 7.0 collective-permute-start.48
  454.2 9.4 collective-permute-start.51
  467.3 21.9 %collective-permute-start.52 = (f32[64,32]{0,1:T(8,128)S(1)}, f32[64,32]{0,1:T(8,128)S(1)}, u32[]{:S(2)}, u32[]{:S(2)}) collective-permute-start(f32[64,32]{0,1:T(8,128)S(1)} %multiply_subtract_fusion.7), channel_id=1, source_target_pairs={{0,128},{64,192},{128,256},{192,320},{256,384},{320,448},{384,1},{... | collective-permute-start | bytes 24584 | tf_op jit(solution)/shard_map/ppermute | solution.py:113
  470.4 25.1 %collective-permute-start.55 = (f32[64,32]{0,1:T(8,128)S(1)}, f32[64,32]{0,1:T(8,128)S(1)}, u32[]{:S(2)}, u32[]{:S(2)}) collective-permute-start(f32[64,32]{0,1:T(8,128)S(1)} %multiply_subtract_fusion.7), channel_id=1, source_target_pairs={{0,447},{64,511},{128,0},{192,64},{256,128},{320,192},{384,256},{4... | collective-permute-start | bytes 24584 | tf_op jit(solution)/shard_map/ppermute | solution.py:113
  474.3 21.2 %collective-permute-start.54 = (f32[64,32]{0,1:T(8,128)S(1)}, f32[64,32]{0,1:T(8,128)S(1)}, u32[]{:S(2)}, u32[]{:S(2)}) collective-permute-start(f32[64,32]{0,1:T(8,128)S(1)} %multiply_subtract_fusion.7), channel_id=1, source_target_pairs={{0,511},{64,0},{128,64},{192,128},{256,192},{320,256},{384,320},{4... | collective-permute-start | bytes 24584 | tf_op jit(solution)/shard_map/ppermute | solution.py:113
  480.2 15.2 %collective-permute-start.53 = (f32[64,32]{0,1:T(8,128)S(1)}, f32[64,32]{0,1:T(8,128)S(1)}, u32[]{:S(2)}, u32[]{:S(2)}) collective-permute-start(f32[64,32]{0,1:T(8,128)S(1)} %multiply_subtract_fusion.7), channel_id=1, source_target_pairs={{0,64},{64,128},{128,192},{192,256},{256,320},{320,384},{384,448},... | collective-permute-start | bytes 24584 | tf_op jit(solution)/shard_map/ppermute | solution.py:113
  498.8 14.2 %collective-permute-start.56 = (f32[6]{0:T(128)S(1)}, f32[6]{0:T(128)S(1)}, u32[]{:S(2)}, u32[]{:S(2)}) collective-permute-start(f32[6]{0:T(128)S(1)} %pad_maximum_fusion.5), channel_id=1, source_target_pairs={{0,64},{64,0},{128,192},{192,128},{256,320},{320,256},{384,448},{4... | collective-permute-start | bytes 80 | tf_op jit(solution)/shard_map/ppermute | solution.py:76
  519.1 18.1 %collective-permute-start.58 = (f32[6]{0:T(128)S(1)}, f32[6]{0:T(128)S(1)}, u32[]{:S(2)}, u32[]{:S(2)}) collective-permute-start(f32[6]{0:T(128)S(1)} %add.2122), channel_id=1, source_target_pairs={{0,256},{64,320},{128,384},{192,448},{256,0},{320,64},{384,128},{4... | collective-permute-start | bytes 80 | tf_op jit(solution)/shard_map/ppermute | solution.py:76
  545.7 7.0 collective-permute-start.61
  564.4 9.4 collective-permute-start.64
  578.3 21.7 %collective-permute-start.65 = (f32[64,32]{0,1:T(8,128)S(1)}, f32[64,32]{0,1:T(8,128)S(1)}, u32[]{:S(2)}, u32[]{:S(2)}) collective-permute-start(f32[64,32]{0,1:T(8,128)S(1)} %multiply_subtract_fusion.5), channel_id=1, source_target_pairs={{0,128},{64,192},{128,256},{192,320},{256,384},{320,448},{384,1},{... | collective-permute-start | bytes 24584 | tf_op jit(solution)/shard_map/ppermute | solution.py:113
  581.2 25.3 %collective-permute-start.68 = (f32[64,32]{0,1:T(8,128)S(1)}, f32[64,32]{0,1:T(8,128)S(1)}, u32[]{:S(2)}, u32[]{:S(2)}) collective-permute-start(f32[64,32]{0,1:T(8,128)S(1)} %multiply_subtract_fusion.5), channel_id=1, source_target_pairs={{0,447},{64,511},{128,0},{192,64},{256,128},{320,192},{384,256},{4... | collective-permute-start | bytes 24584 | tf_op jit(solution)/shard_map/ppermute | solution.py:113
  585.2 21.3 %collective-permute-start.67 = (f32[64,32]{0,1:T(8,128)S(1)}, f32[64,32]{0,1:T(8,128)S(1)}, u32[]{:S(2)}, u32[]{:S(2)}) collective-permute-start(f32[64,32]{0,1:T(8,128)S(1)} %multiply_subtract_fusion.5), channel_id=1, source_target_pairs={{0,511},{64,0},{128,64},{192,128},{256,192},{320,256},{384,320},{4... | collective-permute-start | bytes 24584 | tf_op jit(solution)/shard_map/ppermute | solution.py:113
  591.3 15.2 %collective-permute-start.66 = (f32[64,32]{0,1:T(8,128)S(1)}, f32[64,32]{0,1:T(8,128)S(1)}, u32[]{:S(2)}, u32[]{:S(2)}) collective-permute-start(f32[64,32]{0,1:T(8,128)S(1)} %multiply_subtract_fusion.5), channel_id=1, source_target_pairs={{0,64},{64,128},{128,192},{192,256},{256,320},{320,384},{384,448},... | collective-permute-start | bytes 24584 | tf_op jit(solution)/shard_map/ppermute | solution.py:113
  609.8 14.2 %collective-permute-start.69 = (f32[7]{0:T(128)S(1)}, f32[7]{0:T(128)S(1)}, u32[]{:S(2)}, u32[]{:S(2)}) collective-permute-start(f32[7]{0:T(128)S(1)} %pad_maximum_fusion.6), channel_id=1, source_target_pairs={{0,64},{64,0},{128,192},{192,128},{256,320},{320,256},{384,448},{4... | collective-permute-start | bytes 92 | tf_op jit(solution)/shard_map/ppermute | solution.py:76
  630.2 18.1 %collective-permute-start.71 = (f32[7]{0:T(128)S(1)}, f32[7]{0:T(128)S(1)}, u32[]{:S(2)}, u32[]{:S(2)}) collective-permute-start(f32[7]{0:T(128)S(1)} %add.2142), channel_id=1, source_target_pairs={{0,256},{64,320},{128,384},{192,448},{256,0},{320,64},{384,128},{4... | collective-permute-start | bytes 92 | tf_op jit(solution)/shard_map/ppermute | solution.py:76
  656.7 7.0 collective-permute-start.74
  675.5 9.4 collective-permute-start.77
  690.0 21.7 %collective-permute-start.78 = (f32[64,32]{0,1:T(8,128)S(1)}, f32[64,32]{0,1:T(8,128)S(1)}, u32[]{:S(2)}, u32[]{:S(2)}) collective-permute-start(f32[64,32]{0,1:T(8,128)S(1)} %multiply_subtract_fusion.3), channel_id=1, source_target_pairs={{0,128},{64,192},{128,256},{192,320},{256,384},{320,448},{384,1},{... | collective-permute-start | bytes 24584 | tf_op jit(solution)/shard_map/ppermute | solution.py:113
  693.0 25.1 %collective-permute-start.81 = (f32[64,32]{0,1:T(8,128)S(1)}, f32[64,32]{0,1:T(8,128)S(1)}, u32[]{:S(2)}, u32[]{:S(2)}) collective-permute-start(f32[64,32]{0,1:T(8,128)S(1)} %multiply_subtract_fusion.3), channel_id=1, source_target_pairs={{0,447},{64,511},{128,0},{192,64},{256,128},{320,192},{384,256},{4... | collective-permute-start | bytes 24584 | tf_op jit(solution)/shard_map/ppermute | solution.py:113
  697.0 21.2 %collective-permute-start.80 = (f32[64,32]{0,1:T(8,128)S(1)}, f32[64,32]{0,1:T(8,128)S(1)}, u32[]{:S(2)}, u32[]{:S(2)}) collective-permute-start(f32[64,32]{0,1:T(8,128)S(1)} %multiply_subtract_fusion.3), channel_id=1, source_target_pairs={{0,511},{64,0},{128,64},{192,128},{256,192},{320,256},{384,320},{4... | collective-permute-start | bytes 24584 | tf_op jit(solution)/shard_map/ppermute | solution.py:113
  702.9 15.2 %collective-permute-start.79 = (f32[64,32]{0,1:T(8,128)S(1)}, f32[64,32]{0,1:T(8,128)S(1)}, u32[]{:S(2)}, u32[]{:S(2)}) collective-permute-start(f32[64,32]{0,1:T(8,128)S(1)} %multiply_subtract_fusion.3), channel_id=1, source_target_pairs={{0,64},{64,128},{128,192},{192,256},{256,320},{320,384},{384,448},... | collective-permute-start | bytes 24584 | tf_op jit(solution)/shard_map/ppermute | solution.py:113
  721.5 14.2 %collective-permute-start.82 = (f32[8]{0:T(128)S(1)}, f32[8]{0:T(128)S(1)}, u32[]{:S(2)}, u32[]{:S(2)}) collective-permute-start(f32[8]{0:T(128)S(1)} %pad_maximum_fusion.7), channel_id=1, source_target_pairs={{0,64},{64,0},{128,192},{192,128},{256,320},{320,256},{384,448},{4... | collective-permute-start | bytes 104 | tf_op jit(solution)/shard_map/ppermute | solution.py:76
  741.8 18.1 %collective-permute-start.84 = (f32[8]{0:T(128)S(1)}, f32[8]{0:T(128)S(1)}, u32[]{:S(2)}, u32[]{:S(2)}) collective-permute-start(f32[8]{0:T(128)S(1)} %add.2162), channel_id=1, source_target_pairs={{0,256},{64,320},{128,384},{192,448},{256,0},{320,64},{384,128},{4... | collective-permute-start | bytes 104 | tf_op jit(solution)/shard_map/ppermute | solution.py:76
  768.3 7.0 collective-permute-start.87
  787.1 9.4 collective-permute-start.90
  802.3 21.7 %collective-permute-start.91 = (f32[64,32]{0,1:T(8,128)S(1)}, f32[64,32]{0,1:T(8,128)S(1)}, u32[]{:S(2)}, u32[]{:S(2)}) collective-permute-start(f32[64,32]{0,1:T(8,128)S(1)} %multiply_subtract_fusion.1), channel_id=1, source_target_pairs={{0,128},{64,192},{128,256},{192,320},{256,384},{320,448},{384,1},{... | collective-permute-start | bytes 24584 | tf_op jit(solution)/shard_map/ppermute | solution.py:113
  805.4 25.3 %collective-permute-start.94 = (f32[64,32]{0,1:T(8,128)S(1)}, f32[64,32]{0,1:T(8,128)S(1)}, u32[]{:S(2)}, u32[]{:S(2)}) collective-permute-start(f32[64,32]{0,1:T(8,128)S(1)} %multiply_subtract_fusion.1), channel_id=1, source_target_pairs={{0,447},{64,511},{128,0},{192,64},{256,128},{320,192},{384,256},{4... | collective-permute-start | bytes 24584 | tf_op jit(solution)/shard_map/ppermute | solution.py:113
  809.3 21.3 %collective-permute-start.93 = (f32[64,32]{0,1:T(8,128)S(1)}, f32[64,32]{0,1:T(8,128)S(1)}, u32[]{:S(2)}, u32[]{:S(2)}) collective-permute-start(f32[64,32]{0,1:T(8,128)S(1)} %multiply_subtract_fusion.1), channel_id=1, source_target_pairs={{0,511},{64,0},{128,64},{192,128},{256,192},{320,256},{384,320},{4... | collective-permute-start | bytes 24584 | tf_op jit(solution)/shard_map/ppermute | solution.py:113
  815.4 15.2 %collective-permute-start.92 = (f32[64,32]{0,1:T(8,128)S(1)}, f32[64,32]{0,1:T(8,128)S(1)}, u32[]{:S(2)}, u32[]{:S(2)}) collective-permute-start(f32[64,32]{0,1:T(8,128)S(1)} %multiply_subtract_fusion.1), channel_id=1, source_target_pairs={{0,64},{64,128},{128,192},{192,256},{256,320},{320,384},{384,448},... | collective-permute-start | bytes 24584 | tf_op jit(solution)/shard_map/ppermute | solution.py:113
  834.0 14.2 %collective-permute-start.95 = (f32[9]{0:T(128)S(1)}, f32[9]{0:T(128)S(1)}, u32[]{:S(2)}, u32[]{:S(2)}) collective-permute-start(f32[9]{0:T(128)S(1)} %pad_maximum_fusion.8), channel_id=1, source_target_pairs={{0,64},{64,0},{128,192},{192,128},{256,320},{320,256},{384,448},{4... | collective-permute-start | bytes 116 | tf_op jit(solution)/shard_map/ppermute | solution.py:76
  854.3 18.0 %collective-permute-start.97 = (f32[9]{0:T(128)S(1)}, f32[9]{0:T(128)S(1)}, u32[]{:S(2)}, u32[]{:S(2)}) collective-permute-start(f32[9]{0:T(128)S(1)} %add.2182), channel_id=1, source_target_pairs={{0,256},{64,320},{128,384},{192,448},{256,0},{320,64},{384,128},{4... | collective-permute-start | bytes 116 | tf_op jit(solution)/shard_map/ppermute | solution.py:76
  899.6 9.4 collective-permute-start.103
  916.3 14.3 %collective-permute-start.104 = (f32[1]{0:T(128)}, f32[1]{0:T(128)}, u32[]{:S(2)}, u32[]{:S(2)}) collective-permute-start(f32[1]{0:T(128)} %bitcast.139), channel_id=1, source_target_pairs={{0,64},{64,0},{128,192},{192,128},{256,320},{320,256},{384,448},{4... | collective-permute-start | bytes 20 | tf_op jit(solution)/shard_map/ppermute | solution.py:76
  975.7 9.3 collective-permute-start.112
  (54 other events, 266.9 us)

commit v3 on v1

--- a/solution.py
+++ b/solution.py
@@ -66,7 +66,7 @@
 
 
 def all_sum(values):
-    for axis in ("harm", "space"):
+    for axis in ("space",):
         count = lax.axis_size(axis)
         if count & (count - 1):
             values = lax.psum(values, axis)
@@ -81,47 +81,39 @@
 def per_device(rhs_field, neighbors, nu_mean, nu_ripple, mass_coeff, eddy_coeff):
     block, nodes_own = rhs_field.shape
     harmonics = nu_ripple.shape[0]
+    harm_index = lax.axis_index("harm")
     halo_width = IF
-    harm_start = lax.axis_index("harm") * block
     kernel = nu_ripple.at[0].add(nu_mean)
     cos_table, sin_table = fourier_tables(harmonics)
     total_nodes = nodes_own * lax.axis_size("space")
     relative = jnp.mod(neighbors - lax.axis_index("space") * nodes_own, total_nodes)
     relative = jnp.where(relative >= total_nodes - halo_width, relative - total_nodes, relative)
     ext_index = relative + halo_width
-    global_harm = harm_start + jnp.arange(block)
-    harm_order = (global_harm // 2 + 1).astype(jnp.float32)
-    sign_vals = jnp.where(global_harm % 2 == 0, 1.0, -1.0).astype(jnp.float32)
+    all_harm = jnp.arange(harmonics)
+    harm_order = (all_harm // 2 + 1).astype(jnp.float32)
+    sign_vals = jnp.where(all_harm % 2 == 0, 1.0, -1.0).astype(jnp.float32)
     factor = 4.0 * harm_order / harmonics * sign_vals
-    node_share = nodes_own // lax.axis_size("harm")
-    kernel_use = lax.dynamic_slice_in_dim(
-        kernel, lax.axis_index("harm") * node_share, node_share, 2
-    )
-    kernel_flat = kernel_use.reshape(harmonics, -1)
+    kernel_flat = kernel.reshape(harmonics, -1)
     kernel_real = matmul_high(cos_table, kernel_flat)
     kernel_imag = -matmul_high(sin_table, kernel_flat)
 
-    def convolve_spectrum(spec_real, spec_imag, out_cos, out_sin):
+    def operate(vector_in):
+        extended = with_halo(vector_in, (("space", 1),), halo_width)
+        gradients = vector_in[:, None, :] - extended[:, ext_index]
+        grad_flat = gradients.reshape(harmonics, -1)
+        spec_real = matmul_high(cos_table, grad_flat)
+        spec_imag = -matmul_high(sin_table, grad_flat)
         prod_real = spec_real * kernel_real - spec_imag * kernel_imag
         prod_imag = spec_real * kernel_imag + spec_imag * kernel_real
-        return (matmul_high(out_cos, prod_real) - matmul_high(out_sin, prod_imag)) / harmonics
-
-    def operate(vector_in):
-        extended = with_halo(vector_in, (("space", 1),), halo_width)
-        gradients = extended[:, None, halo_width : halo_width + nodes_own] - extended[:, ext_index]
-        spread = lax.all_to_all(gradients, "harm", split_axis=2, concat_axis=0, tiled=True)
-        spread_flat = spread.reshape(harmonics, -1)
-        spec_real = matmul_high(cos_table, spread_flat)
-        spec_imag = -matmul_high(sin_table, spread_flat)
-        fluxes = convolve_spectrum(spec_real, spec_imag, cos_table, sin_table)
-        fluxes = fluxes.reshape(spread.shape)
-        fluxes = lax.all_to_all(fluxes, "harm", split_axis=0, concat_axis=2, tiled=True)
+        fluxes = (matmul_high(cos_table, prod_real) - matmul_high(sin_table, prod_imag)) / harmonics
+        fluxes = fluxes.reshape(gradients.shape)
         return (
             jnp.sum(fluxes, axis=1)
             + mass_coeff[None, :] * vector_in
             + eddy_coeff[None, :] * factor[:, None] * swap_pairs(vector_in)
         )
 
+    rhs_field = lax.all_gather(rhs_field, "harm", axis=0, tiled=True)
     local_rows = lambda rows, other: jnp.sum(jnp.stack(rows) * other[None], axis=(1, 2))
     sums = all_sum(jnp.concatenate([local_rows([rhs_field], rhs_field), local_rows([rhs_field], image := operate(rhs_field))]))
     beta_norm = jnp.sqrt(sums[0])
@@ -151,7 +143,8 @@
         correction = correction + coeffs[j] * krylov[j]
         applied = applied + coeffs[j] * images[j]
     residual = rhs_field - applied
-    return (correction, residual)
+    own = lambda array: lax.dynamic_slice_in_dim(array, harm_index * block, block, 0)
+    return (own(correction), own(residual))
 
 
 def solution(mesh):

time: 1180 us -> 700 us (0.59)
  waiting for transfers between devices: 533 us -> 197 us
  starting transfers between devices: 388 us -> 247 us
  matrix products: 11.4 us -> 35.5 us
  local copies, waits for them, and re-layouts: 85 us -> 69 us
    ppermute x81 -> x54, waiting for transfers between devices: 373 us -> 197 us  [all_sum(): lax.ppermute(values, axis, [(i, i ^ stride) for i in range(count)])]
    all_to_all x12 -> x0, waiting for transfers between devices: 152 us -> none  [the longest x8 102 us: operate(): lax.all_to_all(fluxes, 'harm', split_axis=0, concat_axis=2, tiled=True)]
    all_to_all x12 -> x0, starting transfers between devices: 74.3 us -> none  [the longest x8 42.9 us: operate(): lax.all_to_all(fluxes, 'harm', split_axis=0, concat_axis=2, tiled=True)]
    all_to_all x4 -> x0, blocking collectives: 69.9 us -> none  [operate(): lax.all_to_all(gradients, 'harm', split_axis=2, concat_axis=0, tiled=True)]
    all_gather x0 -> x1, blocking collectives: none -> 66.3 us  [per_device(): rhs_field = lax.all_gather(rhs_field, 'harm', axis=0, tiled=True)]
    ppermute x81 -> x54, starting transfers between devices: 196 us -> 132 us  [all_sum(): lax.ppermute(values, axis, [(i, i ^ stride) for i in range(count)])]
    dot_general x34, matrix products: 11.4 us -> 35.5 us  [matmul_high(): jnp.dot(left, right, precision=lax.Precision.HIGHEST, preferred_element_t...]
    all_to_all x16 -> x0, other arithmetic: 12.8 us -> none  [the longest x8 6.38 us: operate(): lax.all_to_all(fluxes, 'harm', split_axis=0, concat_axis=2, tiled=True)]
  transfers between devices with their start and end apart: 109 -> 70, of which waited for: 100 -> 55; matrix products, arithmetic and copies ran while one was open for 0% -> 2% of each run, Pallas kernels for 0% -> 0%
where the time goes in v3:
time: 700 us; the launch traced here: 688 us
  starting transfers between devices  247 us (35%)
  waiting for transfers between devices  197 us (28%)
  local copies, waits for them, and re-layouts  69 us (10%)
  blocking collectives  66.3 us (9%)
  between operations  38 us (5%)
  matrix products  35.5 us (5%)
  other arithmetic  34.9 us (5%)
    ppermute x54, waiting for transfers between devices, all_sum(): lax.ppermute(values, axis, [(i, i ^ stride) for i in range(count)])  197 us
    ppermute x54, starting transfers between devices, all_sum(): lax.ppermute(values, axis, [(i, i ^ stride) for i in range(count)])  132 us
    ppermute x8, starting transfers between devices, with_halo(): after = lax.ppermute(leading, axis, down)  99.7 us
    all_gather x1, blocking collectives, per_device(): rhs_field = lax.all_gather(rhs_field, 'harm', axis=0, tiled=True)  66.3 us
    gather x8, local copies, waits for them, and re-layouts, operate(): gradients = vector_in[:, None, :] - extended[:, ext_index]  43.7 us
    dot_general x34, matrix products, matmul_high(): jnp.dot(left, right, precision=lax.Precision.HIGHEST, preferred_element_t...  35.5 us
    ppermute x8, starting transfers between devices, with_halo(): before = lax.ppermute(last, axis, up)  15.3 us
  transfers between devices with their start and end apart: 70, of which 55 were waited for; matrix products, arithmetic and copies ran while one was open for 2% of the time, Pallas kernels for 0%

profile of v3, /device:TPU:6, one launch (start us, length us, event | category | flops | bytes accessed | tf_op | source)
XLA Modules:
  0.0 688.1 jit_solution(13016184789733953150)
XLA Ops:
  1.3 66.3 %all_gather.3 = f32[64,256]{1,0:T(8,128)S(1)} all-gather(f32[8,256]{1,0:T(8,128)S(1)} %copy-done.19), channel_id=1, replica_groups=mesh['harm'=8,'space'=64] {'harm'}, dimensions={0}, use_global_device_ids=true | all-gather | bytes 73728 | tf_op jit(solution)/shard_map/all_gather | solution.py:116
  69.6 12.4 %collective-permute-start.1 = (f32[64,64]{0,1:T(8,128)S(1)}, f32[64,64]{0,1:T(8,128)S(1)}, u32[]{:S(2)}, u32[]{:S(2)}) collective-permute-start(f32[64,64]{0,1:T(8,128)S(1)} %get-tuple-element.47), channel_id=1, source_target_pairs={{1,0},{2,1},{3,2},{4,3},{5,4},{6,5},{7,6},{8,7},{9,8},{10,9},{11,1... | collective-permute-start | bytes 49160 | tf_op jit(solution)/shard_map/ppermute | solution.py:18
  84.1 5.5 gather_fusion
  103.2 3.5 collective-permute-done.3
  110.0 5.0 collective-permute-done.4
  117.0 3.5 collective-permute-done.5
  122.5 4.4 collective-permute-done.6
  126.9 4.6 collective-permute-start.7
  131.5 4.8 collective-permute-done.7
  140.9 12.4 %collective-permute-start.9 = (f32[64,64]{1,0:T(8,128)S(1)}, f32[64,64]{1,0:T(8,128)S(1)}, u32[]{:S(2)}, u32[]{:S(2)}) collective-permute-start(f32[64,64]{1,0:T(8,128)S(1)} %get-tuple-element.83), channel_id=1, source_target_pairs={{1,0},{2,1},{3,2},{4,3},{5,4},{6,5},{7,6},{8,7},{9,8},{10,9},{11,1... | collective-permute-start | bytes 49160 | tf_op jit(solution)/shard_map/ppermute | solution.py:18
  155.1 5.5 gather_fusion.1
  171.8 3.5 collective-permute-done.11
  177.3 5.0 collective-permute-done.12
  184.2 3.5 collective-permute-done.13
  189.7 4.4 collective-permute-done.14
  194.1 5.1 collective-permute-start.15
  199.2 4.3 collective-permute-done.15
  208.7 12.8 %collective-permute-start.17 = (f32[64,64]{1,0:T(8,128)S(1)}, f32[64,64]{1,0:T(8,128)S(1)}, u32[]{:S(2)}, u32[]{:S(2)}) collective-permute-start(f32[64,64]{1,0:T(8,128)S(1)} %get-tuple-element.80), channel_id=1, source_target_pairs={{1,0},{2,1},{3,2},{4,3},{5,4},{6,5},{7,6},{8,7},{9,8},{10,9},{11,1... | collective-permute-start | bytes 49160 | tf_op jit(solution)/shard_map/ppermute | solution.py:18
  223.7 5.5 gather_fusion.2
  240.9 3.5 collective-permute-done.19
  246.4 5.0 collective-permute-done.20
  253.4 3.5 collective-permute-done.21
  258.8 4.4 collective-permute-done.22
  263.2 4.3 collective-permute-start.23
  267.5 5.1 collective-permute-done.23
  278.5 12.4 %collective-permute-start.25 = (f32[64,64]{1,0:T(8,128)S(1)}, f32[64,64]{1,0:T(8,128)S(1)}, u32[]{:S(2)}, u32[]{:S(2)}) collective-permute-start(f32[64,64]{1,0:T(8,128)S(1)} %get-tuple-element.78), channel_id=1, source_target_pairs={{1,0},{2,1},{3,2},{4,3},{5,4},{6,5},{7,6},{8,7},{9,8},{10,9},{11,1... | collective-permute-start | bytes 49160 | tf_op jit(solution)/shard_map/ppermute | solution.py:18
  293.7 5.5 gather_fusion.3
  312.1 3.5 collective-permute-done.27
  317.5 5.0 collective-permute-done.28
  324.5 3.5 collective-permute-done.29
  329.9 4.4 collective-permute-done.30
  334.4 4.1 collective-permute-start.31
  338.5 5.3 collective-permute-done.31
  350.3 12.5 %collective-permute-start.33 = (f32[64,64]{1,0:T(8,128)S(1)}, f32[64,64]{1,0:T(8,128)S(1)}, u32[]{:S(2)}, u32[]{:S(2)}) collective-permute-start(f32[64,64]{1,0:T(8,128)S(1)} %get-tuple-element.76), channel_id=1, source_target_pairs={{1,0},{2,1},{3,2},{4,3},{5,4},{6,5},{7,6},{8,7},{9,8},{10,9},{11,1... | collective-permute-start | bytes 49160 | tf_op jit(solution)/shard_map/ppermute | solution.py:18
  365.1 5.5 gather_fusion.4
  382.6 3.5 collective-permute-done.35
  388.0 5.0 collective-permute-done.36
  395.0 3.5 collective-permute-done.37
  400.5 4.4 collective-permute-done.38
  404.9 4.5 collective-permute-start.39
  409.4 4.8 collective-permute-done.39
  422.2 12.4 %collective-permute-start.41 = (f32[64,64]{1,0:T(8,128)S(1)}, f32[64,64]{1,0:T(8,128)S(1)}, u32[]{:S(2)}, u32[]{:S(2)}) collective-permute-start(f32[64,64]{1,0:T(8,128)S(1)} %get-tuple-element.74), channel_id=1, source_target_pairs={{1,0},{2,1},{3,2},{4,3},{5,4},{6,5},{7,6},{8,7},{9,8},{10,9},{11,1... | collective-permute-start | bytes 49160 | tf_op jit(solution)/shard_map/ppermute | solution.py:18
  437.3 5.5 gather_fusion.5
  454.9 3.5 collective-permute-done.43
  460.3 5.0 collective-permute-done.44
  467.3 3.5 collective-permute-done.45
  472.7 4.4 collective-permute-done.46
  477.2 4.1 collective-permute-start.47
  481.3 5.2 collective-permute-done.47
  495.1 12.6 %collective-permute-start.49 = (f32[64,64]{1,0:T(8,128)S(1)}, f32[64,64]{1,0:T(8,128)S(1)}, u32[]{:S(2)}, u32[]{:S(2)}) collective-permute-start(f32[64,64]{1,0:T(8,128)S(1)} %get-tuple-element.58), channel_id=1, source_target_pairs={{1,0},{2,1},{3,2},{4,3},{5,4},{6,5},{7,6},{8,7},{9,8},{10,9},{11,1... | collective-permute-start | bytes 49160 | tf_op jit(solution)/shard_map/ppermute | solution.py:18
  511.0 5.5 gather_fusion.6
  529.5 3.5 collective-permute-done.51
  535.0 5.0 collective-permute-done.52
  541.9 3.5 collective-permute-done.53
  547.4 4.4 collective-permute-done.54
  555.2 6.0 collective-permute-done.55
  571.1 12.4 %collective-permute-start.57 = (f32[64,64]{1,0:T(8,128)S(1)}, f32[64,64]{1,0:T(8,128)S(1)}, u32[]{:S(2)}, u32[]{:S(2)}) collective-permute-start(f32[64,64]{1,0:T(8,128)S(1)} %get-tuple-element.51), channel_id=1, source_target_pairs={{1,0},{2,1},{3,2},{4,3},{5,4},{6,5},{7,6},{8,7},{9,8},{10,9},{11,1... | collective-permute-start | bytes 49160 | tf_op jit(solution)/shard_map/ppermute | solution.py:18
  585.6 5.5 gather_fusion.7
  609.4 5.0 collective-permute-done.60
  621.8 4.4 collective-permute-done.62
  626.3 4.7 collective-permute-start.63
  631.0 4.6 collective-permute-done.63
  653.4 3.6 collective-permute-start.66
  673.9 6.0 collective-permute-start.69
  (354 shorter events, 234.1 us)
Async XLA Ops:
  67.7 16.4 %collective-permute-start = (f32[64,64]{0,1:T(8,128)S(1)}, f32[64,64]{0,1:T(8,128)S(1)}, u32[]{:S(2)}, u32[]{:S(2)}) collective-permute-start(f32[64,64]{0,1:T(8,128)S(1)} %get-tuple-element.46), channel_id=1, source_target_pairs={{0,1},{1,2},{2,3},{3,4},{4,5},{5,6},{6,7},{7,8},{8,9},{9,10},{10,1... | collective-permute-start | bytes 49160 | tf_op jit(solution)/shard_map/ppermute | solution.py:17
  69.6 14.5 %collective-permute-start.1 = (f32[64,64]{0,1:T(8,128)S(1)}, f32[64,64]{0,1:T(8,128)S(1)}, u32[]{:S(2)}, u32[]{:S(2)}) collective-permute-start(f32[64,64]{0,1:T(8,128)S(1)} %get-tuple-element.47), channel_id=1, source_target_pairs={{1,0},{2,1},{3,2},{4,3},{5,4},{6,5},{7,6},{8,7},{9,8},{10,9},{11,1... | collective-permute-start | bytes 49160 | tf_op jit(solution)/shard_map/ppermute | solution.py:18
  96.9 3.0 collective-permute-start.2
  101.3 5.5 collective-permute-start.3
  108.1 7.0 %collective-permute-start.4 = (f32[2]{0:T(128)S(1)}, f32[2]{0:T(128)S(1)}, u32[]{:S(2)}, u32[]{:S(2)}) collective-permute-start(f32[2]{0:T(128)S(1)} %fusion.350), channel_id=1, source_target_pairs={{0,4},{1,5},{2,6},{3,7},{4,0},{5,1},{6,2},{7,3},{8,12},{9,13},{10,... | collective-permute-start | bytes 32 | tf_op jit(solution)/shard_map/ppermute | solution.py:76
  115.1 5.5 collective-permute-start.5
  120.5 6.3 collective-permute-start.6
  126.9 9.4 %collective-permute-start.7 = (f32[2]{0:T(128)S(1)}, f32[2]{0:T(128)S(1)}, u32[]{:S(2)}, u32[]{:S(2)}) collective-permute-start(f32[2]{0:T(128)S(1)} %add.533), channel_id=1, source_target_pairs={{0,32},{1,33},{2,34},{3,35},{4,36},{5,37},{6,38},{7,39},{8,40},{9,... | collective-permute-start | bytes 32 | tf_op jit(solution)/shard_map/ppermute | solution.py:76
  139.0 15.4 %collective-permute-start.8 = (f32[64,64]{1,0:T(8,128)S(1)}, f32[64,64]{1,0:T(8,128)S(1)}, u32[]{:S(2)}, u32[]{:S(2)}) collective-permute-start(f32[64,64]{1,0:T(8,128)S(1)} %get-tuple-element.82), channel_id=1, source_target_pairs={{0,1},{1,2},{2,3},{3,4},{4,5},{5,6},{6,7},{7,8},{8,9},{9,10},{10,1... | collective-permute-start | bytes 49160 | tf_op jit(solution)/shard_map/ppermute | solution.py:17
  140.9 13.9 %collective-permute-start.9 = (f32[64,64]{1,0:T(8,128)S(1)}, f32[64,64]{1,0:T(8,128)S(1)}, u32[]{:S(2)}, u32[]{:S(2)}) collective-permute-start(f32[64,64]{1,0:T(8,128)S(1)} %get-tuple-element.83), channel_id=1, source_target_pairs={{1,0},{2,1},{3,2},{4,3},{5,4},{6,5},{7,6},{8,7},{9,8},{10,9},{11,1... | collective-permute-start | bytes 49160 | tf_op jit(solution)/shard_map/ppermute | solution.py:18
  166.1 3.0 collective-permute-start.10
  169.9 5.5 collective-permute-start.11
  175.3 7.0 %collective-permute-start.12 = (f32[3]{0:T(128)S(1)}, f32[3]{0:T(128)S(1)}, u32[]{:S(2)}, u32[]{:S(2)}) collective-permute-start(f32[3]{0:T(128)S(1)} %add.539), channel_id=1, source_target_pairs={{0,4},{1,5},{2,6},{3,7},{4,0},{5,1},{6,2},{7,3},{8,12},{9,13},{10,... | collective-permute-start | bytes 44 | tf_op jit(solution)/shard_map/ppermute | solution.py:76
  182.3 5.5 collective-permute-start.13
  187.8 6.3 collective-permute-start.14
  194.1 9.4 %collective-permute-start.15 = (f32[3]{0:T(128)S(1)}, f32[3]{0:T(128)S(1)}, u32[]{:S(2)}, u32[]{:S(2)}) collective-permute-start(f32[3]{0:T(128)S(1)} %add.542), channel_id=1, source_target_pairs={{0,32},{1,33},{2,34},{3,35},{4,36},{5,37},{6,38},{7,39},{8,40},{9,... | collective-permute-start | bytes 44 | tf_op jit(solution)/shard_map/ppermute | solution.py:76
  206.8 16.7 %collective-permute-start.16 = (f32[64,64]{1,0:T(8,128)S(1)}, f32[64,64]{1,0:T(8,128)S(1)}, u32[]{:S(2)}, u32[]{:S(2)}) collective-permute-start(f32[64,64]{1,0:T(8,128)S(1)} %get-tuple-element.79), channel_id=1, source_target_pairs={{0,1},{1,2},{2,3},{3,4},{4,5},{5,6},{6,7},{7,8},{8,9},{9,10},{10,1... | collective-permute-start | bytes 49160 | tf_op jit(solution)/shard_map/ppermute | solution.py:17
  208.7 14.8 %collective-permute-start.17 = (f32[64,64]{1,0:T(8,128)S(1)}, f32[64,64]{1,0:T(8,128)S(1)}, u32[]{:S(2)}, u32[]{:S(2)}) collective-permute-start(f32[64,64]{1,0:T(8,128)S(1)} %get-tuple-element.80), channel_id=1, source_target_pairs={{1,0},{2,1},{3,2},{4,3},{5,4},{6,5},{7,6},{8,7},{9,8},{10,9},{11,1... | collective-permute-start | bytes 49160 | tf_op jit(solution)/shard_map/ppermute | solution.py:18
  239.0 5.5 collective-permute-start.19
  244.5 7.0 %collective-permute-start.20 = (f32[4]{0:T(128)S(1)}, f32[4]{0:T(128)S(1)}, u32[]{:S(2)}, u32[]{:S(2)}) collective-permute-start(f32[4]{0:T(128)S(1)} %add.550), channel_id=1, source_target_pairs={{0,4},{1,5},{2,6},{3,7},{4,0},{5,1},{6,2},{7,3},{8,12},{9,13},{10,... | collective-permute-start | bytes 56 | tf_op jit(solution)/shard_map/ppermute | solution.py:76
  251.4 5.5 collective-permute-start.21
  256.9 6.3 collective-permute-start.22
  263.2 9.4 %collective-permute-start.23 = (f32[4]{0:T(128)S(1)}, f32[4]{0:T(128)S(1)}, u32[]{:S(2)}, u32[]{:S(2)}) collective-permute-start(f32[4]{0:T(128)S(1)} %add.553), channel_id=1, source_target_pairs={{0,32},{1,33},{2,34},{3,35},{4,36},{5,37},{6,38},{7,39},{8,40},{9,... | collective-permute-start | bytes 56 | tf_op jit(solution)/shard_map/ppermute | solution.py:76
  276.6 16.9 %collective-permute-start.24 = (f32[64,64]{1,0:T(8,128)S(1)}, f32[64,64]{1,0:T(8,128)S(1)}, u32[]{:S(2)}, u32[]{:S(2)}) collective-permute-start(f32[64,64]{1,0:T(8,128)S(1)} %get-tuple-element.77), channel_id=1, source_target_pairs={{0,1},{1,2},{2,3},{3,4},{4,5},{5,6},{6,7},{7,8},{8,9},{9,10},{10,1... | collective-permute-start | bytes 49160 | tf_op jit(solution)/shard_map/ppermute | solution.py:17
  278.5 14.9 %collective-permute-start.25 = (f32[64,64]{1,0:T(8,128)S(1)}, f32[64,64]{1,0:T(8,128)S(1)}, u32[]{:S(2)}, u32[]{:S(2)}) collective-permute-start(f32[64,64]{1,0:T(8,128)S(1)} %get-tuple-element.78), channel_id=1, source_target_pairs={{1,0},{2,1},{3,2},{4,3},{5,4},{6,5},{7,6},{8,7},{9,8},{10,9},{11,1... | collective-permute-start | bytes 49160 | tf_op jit(solution)/shard_map/ppermute | solution.py:18
  310.2 5.5 collective-permute-start.27
  315.6 7.0 %collective-permute-start.28 = (f32[5]{0:T(128)S(1)}, f32[5]{0:T(128)S(1)}, u32[]{:S(2)}, u32[]{:S(2)}) collective-permute-start(f32[5]{0:T(128)S(1)} %add.561), channel_id=1, source_target_pairs={{0,4},{1,5},{2,6},{3,7},{4,0},{5,1},{6,2},{7,3},{8,12},{9,13},{10,... | collective-permute-start | bytes 68 | tf_op jit(solution)/shard_map/ppermute | solution.py:76
  322.6 5.5 collective-permute-start.29
  328.0 6.3 collective-permute-start.30
  334.4 9.4 %collective-permute-start.31 = (f32[5]{0:T(128)S(1)}, f32[5]{0:T(128)S(1)}, u32[]{:S(2)}, u32[]{:S(2)}) collective-permute-start(f32[5]{0:T(128)S(1)} %add.564), channel_id=1, source_target_pairs={{0,32},{1,33},{2,34},{3,35},{4,36},{5,37},{6,38},{7,39},{8,40},{9,... | collective-permute-start | bytes 68 | tf_op jit(solution)/shard_map/ppermute | solution.py:76
  348.4 16.4 %collective-permute-start.32 = (f32[64,64]{1,0:T(8,128)S(1)}, f32[64,64]{1,0:T(8,128)S(1)}, u32[]{:S(2)}, u32[]{:S(2)}) collective-permute-start(f32[64,64]{1,0:T(8,128)S(1)} %get-tuple-element.75), channel_id=1, source_target_pairs={{0,1},{1,2},{2,3},{3,4},{4,5},{5,6},{6,7},{7,8},{8,9},{9,10},{10,1... | collective-permute-start | bytes 49160 | tf_op jit(solution)/shard_map/ppermute | solution.py:17
  350.3 14.5 %collective-permute-start.33 = (f32[64,64]{1,0:T(8,128)S(1)}, f32[64,64]{1,0:T(8,128)S(1)}, u32[]{:S(2)}, u32[]{:S(2)}) collective-permute-start(f32[64,64]{1,0:T(8,128)S(1)} %get-tuple-element.76), channel_id=1, source_target_pairs={{1,0},{2,1},{3,2},{4,3},{5,4},{6,5},{7,6},{8,7},{9,8},{10,9},{11,1... | collective-permute-start | bytes 49160 | tf_op jit(solution)/shard_map/ppermute | solution.py:18
  380.7 5.5 collective-permute-start.35
  386.1 7.0 %collective-permute-start.36 = (f32[6]{0:T(128)S(1)}, f32[6]{0:T(128)S(1)}, u32[]{:S(2)}, u32[]{:S(2)}) collective-permute-start(f32[6]{0:T(128)S(1)} %add.572), channel_id=1, source_target_pairs={{0,4},{1,5},{2,6},{3,7},{4,0},{5,1},{6,2},{7,3},{8,12},{9,13},{10,... | collective-permute-start | bytes 80 | tf_op jit(solution)/shard_map/ppermute | solution.py:76
  393.1 5.5 collective-permute-start.37
  398.5 6.3 collective-permute-start.38
  404.9 9.4 %collective-permute-start.39 = (f32[6]{0:T(128)S(1)}, f32[6]{0:T(128)S(1)}, u32[]{:S(2)}, u32[]{:S(2)}) collective-permute-start(f32[6]{0:T(128)S(1)} %add.575), channel_id=1, source_target_pairs={{0,32},{1,33},{2,34},{3,35},{4,36},{5,37},{6,38},{7,39},{8,40},{9,... | collective-permute-start | bytes 80 | tf_op jit(solution)/shard_map/ppermute | solution.py:76
  420.2 16.8 %collective-permute-start.40 = (f32[64,64]{1,0:T(8,128)S(1)}, f32[64,64]{1,0:T(8,128)S(1)}, u32[]{:S(2)}, u32[]{:S(2)}) collective-permute-start(f32[64,64]{1,0:T(8,128)S(1)} %get-tuple-element.73), channel_id=1, source_target_pairs={{0,1},{1,2},{2,3},{3,4},{4,5},{5,6},{6,7},{7,8},{8,9},{9,10},{10,1... | collective-permute-start | bytes 49160 | tf_op jit(solution)/shard_map/ppermute | solution.py:17
  422.2 14.9 %collective-permute-start.41 = (f32[64,64]{1,0:T(8,128)S(1)}, f32[64,64]{1,0:T(8,128)S(1)}, u32[]{:S(2)}, u32[]{:S(2)}) collective-permute-start(f32[64,64]{1,0:T(8,128)S(1)} %get-tuple-element.74), channel_id=1, source_target_pairs={{1,0},{2,1},{3,2},{4,3},{5,4},{6,5},{7,6},{8,7},{9,8},{10,9},{11,1... | collective-permute-start | bytes 49160 | tf_op jit(solution)/shard_map/ppermute | solution.py:18
  452.9 5.5 collective-permute-start.43
  458.4 7.0 %collective-permute-start.44 = (f32[7]{0:T(128)S(1)}, f32[7]{0:T(128)S(1)}, u32[]{:S(2)}, u32[]{:S(2)}) collective-permute-start(f32[7]{0:T(128)S(1)} %add.583), channel_id=1, source_target_pairs={{0,4},{1,5},{2,6},{3,7},{4,0},{5,1},{6,2},{7,3},{8,12},{9,13},{10,... | collective-permute-start | bytes 92 | tf_op jit(solution)/shard_map/ppermute | solution.py:76
  465.4 5.5 collective-permute-start.45
  470.8 6.3 collective-permute-start.46
  477.2 9.4 %collective-permute-start.47 = (f32[7]{0:T(128)S(1)}, f32[7]{0:T(128)S(1)}, u32[]{:S(2)}, u32[]{:S(2)}) collective-permute-start(f32[7]{0:T(128)S(1)} %add.586), channel_id=1, source_target_pairs={{0,32},{1,33},{2,34},{3,35},{4,36},{5,37},{6,38},{7,39},{8,40},{9,... | collective-permute-start | bytes 92 | tf_op jit(solution)/shard_map/ppermute | solution.py:76
  493.1 17.6 %collective-permute-start.48 = (f32[64,64]{1,0:T(8,128)S(1)}, f32[64,64]{1,0:T(8,128)S(1)}, u32[]{:S(2)}, u32[]{:S(2)}) collective-permute-start(f32[64,64]{1,0:T(8,128)S(1)} %get-tuple-element.57), channel_id=1, source_target_pairs={{0,1},{1,2},{2,3},{3,4},{4,5},{5,6},{6,7},{7,8},{8,9},{9,10},{10,1... | collective-permute-start | bytes 49160 | tf_op jit(solution)/shard_map/ppermute | solution.py:17
  495.1 15.7 %collective-permute-start.49 = (f32[64,64]{1,0:T(8,128)S(1)}, f32[64,64]{1,0:T(8,128)S(1)}, u32[]{:S(2)}, u32[]{:S(2)}) collective-permute-start(f32[64,64]{1,0:T(8,128)S(1)} %get-tuple-element.58), channel_id=1, source_target_pairs={{1,0},{2,1},{3,2},{4,3},{5,4},{6,5},{7,6},{8,7},{9,8},{10,9},{11,1... | collective-permute-start | bytes 49160 | tf_op jit(solution)/shard_map/ppermute | solution.py:18
  527.6 5.5 collective-permute-start.51
  533.1 7.0 %collective-permute-start.52 = (f32[8]{0:T(128)S(1)}, f32[8]{0:T(128)S(1)}, u32[]{:S(2)}, u32[]{:S(2)}) collective-permute-start(f32[8]{0:T(128)S(1)} %add.594), channel_id=1, source_target_pairs={{0,4},{1,5},{2,6},{3,7},{4,0},{5,1},{6,2},{7,3},{8,12},{9,13},{10,... | collective-permute-start | bytes 104 | tf_op jit(solution)/shard_map/ppermute | solution.py:76
  540.0 5.5 collective-permute-start.53
  545.5 6.3 collective-permute-start.54
  551.8 9.4 %collective-permute-start.55 = (f32[8]{0:T(128)S(1)}, f32[8]{0:T(128)S(1)}, u32[]{:S(2)}, u32[]{:S(2)}) collective-permute-start(f32[8]{0:T(128)S(1)} %add.597), channel_id=1, source_target_pairs={{0,32},{1,33},{2,34},{3,35},{4,36},{5,37},{6,38},{7,39},{8,40},{9,... | collective-permute-start | bytes 104 | tf_op jit(solution)/shard_map/ppermute | solution.py:76
  569.1 16.2 %collective-permute-start.56 = (f32[64,64]{1,0:T(8,128)S(1)}, f32[64,64]{1,0:T(8,128)S(1)}, u32[]{:S(2)}, u32[]{:S(2)}) collective-permute-start(f32[64,64]{1,0:T(8,128)S(1)} %get-tuple-element.50), channel_id=1, source_target_pairs={{0,1},{1,2},{2,3},{3,4},{4,5},{5,6},{6,7},{7,8},{8,9},{9,10},{10,1... | collective-permute-start | bytes 49160 | tf_op jit(solution)/shard_map/ppermute | solution.py:17
  571.1 14.3 %collective-permute-start.57 = (f32[64,64]{1,0:T(8,128)S(1)}, f32[64,64]{1,0:T(8,128)S(1)}, u32[]{:S(2)}, u32[]{:S(2)}) collective-permute-start(f32[64,64]{1,0:T(8,128)S(1)} %get-tuple-element.51), channel_id=1, source_target_pairs={{1,0},{2,1},{3,2},{4,3},{5,4},{6,5},{7,6},{8,7},{9,8},{10,9},{11,1... | collective-permute-start | bytes 49160 | tf_op jit(solution)/shard_map/ppermute | solution.py:18
  602.0 5.5 collective-permute-start.59
  607.5 7.0 %collective-permute-start.60 = (f32[9]{0:T(128)S(1)}, f32[9]{0:T(128)S(1)}, u32[]{:S(2)}, u32[]{:S(2)}) collective-permute-start(f32[9]{0:T(128)S(1)} %add.605), channel_id=1, source_target_pairs={{0,4},{1,5},{2,6},{3,7},{4,0},{5,1},{6,2},{7,3},{8,12},{9,13},{10,... | collective-permute-start | bytes 116 | tf_op jit(solution)/shard_map/ppermute | solution.py:76
  614.5 5.5 collective-permute-start.61
  619.9 6.3 collective-permute-start.62
  626.3 9.4 %collective-permute-start.63 = (f32[9]{0:T(128)S(1)}, f32[9]{0:T(128)S(1)}, u32[]{:S(2)}, u32[]{:S(2)}) collective-permute-start(f32[9]{0:T(128)S(1)} %add.608), channel_id=1, source_target_pairs={{0,32},{1,33},{2,34},{3,35},{4,36},{5,37},{6,38},{7,39},{8,40},{9,... | collective-permute-start | bytes 116 | tf_op jit(solution)/shard_map/ppermute | solution.py:76
  642.9 3.2 collective-permute-start.64
  647.4 5.4 collective-permute-start.65
  653.4 6.9 %collective-permute-start.66 = (f32[1]{0:T(128)}, f32[1]{0:T(128)}, u32[]{:S(2)}, u32[]{:S(2)}) collective-permute-start(f32[1]{0:T(128)} %add.613), channel_id=1, source_target_pairs={{0,4},{1,5},{2,6},{3,7},{4,0},{5,1},{6,2},{7,3},{8,12},{9,13},{10,... | collective-permute-start | bytes 20 | tf_op jit(solution)/shard_map/ppermute | solution.py:76
  660.9 5.4 collective-permute-start.67
  667.0 6.3 collective-permute-start.68
  673.9 9.3 %collective-permute-start.69 = (f32[1]{0:T(128)}, f32[1]{0:T(128)}, u32[]{:S(2)}, u32[]{:S(2)}) collective-permute-start(f32[1]{0:T(128)} %add.616), channel_id=1, source_target_pairs={{0,32},{1,33},{2,34},{3,35},{4,36},{5,37},{6,38},{7,39},{8,40},{9,... | collective-permute-start | bytes 20 | tf_op jit(solution)/shard_map/ppermute | solution.py:76
  (28 other events, 253.4 us)

commit v4 on v3

--- a/solution.py
+++ b/solution.py
@@ -97,8 +97,14 @@
     kernel_real = matmul_high(cos_table, kernel_flat)
     kernel_imag = -matmul_high(sin_table, kernel_flat)
 
-    def operate(vector_in):
-        extended = with_halo(vector_in, (("space", 1),), halo_width)
+    def extend(vector_in):
+        return with_halo(vector_in, (("space", 1),), halo_width)
+
+    def inner(extended):
+        return lax.slice_in_dim(extended, halo_width, halo_width + nodes_own, axis=1)
+
+    def operate(extended):
+        vector_in = inner(extended)
         gradients = vector_in[:, None, :] - extended[:, ext_index]
         grad_flat = gradients.reshape(harmonics, -1)
         spec_real = matmul_high(cos_table, grad_flat)
@@ -115,26 +121,40 @@
 
     rhs_field = lax.all_gather(rhs_field, "harm", axis=0, tiled=True)
     local_rows = lambda rows, other: jnp.sum(jnp.stack(rows) * other[None], axis=(1, 2))
-    sums = all_sum(jnp.concatenate([local_rows([rhs_field], rhs_field), local_rows([rhs_field], image := operate(rhs_field))]))
+    rhs_ext = extend(rhs_field)
+    image = operate(rhs_ext)
+    image_ext = extend(image)
+    sums = all_sum(jnp.concatenate([local_rows([rhs_field], rhs_field), local_rows([rhs_field], image)]))
     beta_norm = jnp.sqrt(sums[0])
-    krylov = [rhs_field / beta_norm]
+    krylov_ext = [rhs_ext / beta_norm]
+    krylov = [inner(krylov_ext[0])]
     images = [image / beta_norm]
     columns = [[sums[1] / beta_norm / beta_norm]]
-    ortho = images[0] - columns[0][0] * krylov[0]
+    ortho_ext = image_ext / beta_norm - columns[0][0] * krylov_ext[0]
     for j in range(1, ITERS):
-        image = operate(ortho)
+        ortho = inner(ortho_ext)
+        image = operate(ortho_ext)
+        last = j + 1 == ITERS
+        if not last:
+            image_ext = extend(image)
         sums = all_sum(
             jnp.concatenate([local_rows([ortho], ortho), local_rows(krylov + [ortho], image)])
         )
         length = jnp.sqrt(sums[0])
         columns[j - 1].append(length)
-        krylov.append(ortho / length)
+        krylov_ext.append(ortho_ext / length)
+        krylov.append(inner(krylov_ext[j]))
         images.append(image / length)
         projected = [sums[1 + i] / length for i in range(j)] + [sums[1 + j] / length / length]
         columns.append(projected)
-        ortho = images[j]
-        for i in range(j + 1):
-            ortho = ortho - projected[i] * krylov[i]
+        if last:
+            ortho = images[j]
+            for i in range(j + 1):
+                ortho = ortho - projected[i] * krylov[i]
+        else:
+            ortho_ext = image_ext / length
+            for i in range(j + 1):
+                ortho_ext = ortho_ext - projected[i] * krylov_ext[i]
     columns[ITERS - 1].append(jnp.sqrt(all_sum(jnp.sum(ortho * ortho)[None])[0]))
     coeffs = least_squares(columns, beta_norm)
     correction = coeffs[0] * krylov[0]

time: 700 us -> 682 us (0.974)
  starting transfers between devices: 247 us -> 197 us
  local copies, waits for them, and re-layouts: 69 us -> 91.2 us
  waiting for transfers between devices: 197 us -> 206 us
    ppermute x8, starting transfers between devices: 99.7 us -> 52.1 us  [with_halo(): after = lax.ppermute(leading, axis, down)]
    ppermute x8, waiting for transfers between devices: 0.02 us -> 9.15 us  [with_halo(): before = lax.ppermute(last, axis, up)]
    unnamed x56 -> x93, local copies, waits for them, and re-layouts: 9 us -> 16.2 us
  transfers between devices with their start and end apart: 70 -> 70, of which waited for: 55 -> 54; matrix products, arithmetic and copies ran while one was open for 2% -> 4% of each run, Pallas kernels for 0% -> 0%
where the time goes in v4:
time: 682 us; the launch traced here: 670 us
  waiting for transfers between devices  206 us (30%)
  starting transfers between devices  197 us (29%)
  local copies, waits for them, and re-layouts  91.2 us (13%)
  blocking collectives  66.3 us (10%)
  between operations  37.6 us (6%)
  matrix products  37.3 us (5%)
  other arithmetic  34.1 us (5%)
    ppermute x54, waiting for transfers between devices, all_sum(): lax.ppermute(values, axis, [(i, i ^ stride) for i in range(count)])  197 us
    ppermute x54, starting transfers between devices, all_sum(): lax.ppermute(values, axis, [(i, i ^ stride) for i in range(count)])  130 us
    all_gather x1, blocking collectives, per_device(): rhs_field = lax.all_gather(rhs_field, 'harm', axis=0, tiled=True)  66.3 us
    ppermute x8, starting transfers between devices, with_halo(): after = lax.ppermute(leading, axis, down)  52.1 us
    gather x8, local copies, waits for them, and re-layouts, operate(): gradients = vector_in[:, None, :] - extended[:, ext_index]  48 us
    dot_general x34, matrix products, matmul_high(): jnp.dot(left, right, precision=lax.Precision.HIGHEST, preferred_element_t...  37.3 us
    unnamed x93, local copies, waits for them, and re-layouts  16.2 us
    ppermute x8, starting transfers between devices, with_halo(): before = lax.ppermute(last, axis, up)  15.4 us
  transfers between devices with their start and end apart: 70, of which 54 were waited for; matrix products, arithmetic and copies ran while one was open for 4% of the time, Pallas kernels for 0%

profile of v4, /device:TPU:6, one launch (start us, length us, event | category | flops | bytes accessed | tf_op | source)
XLA Modules:
  0.0 669.8 jit_solution(14481352433028725167)
XLA Ops:
  1.3 66.3 %all_gather.3 = f32[64,256]{1,0:T(8,128)S(1)} all-gather(f32[8,256]{1,0:T(8,128)S(1)} %copy-done.34), channel_id=1, replica_groups=mesh['harm'=8,'space'=64] {'harm'}, dimensions={0}, use_global_device_ids=true | all-gather | bytes 73728 | tf_op jit(solution)/shard_map/all_gather | solution.py:122
  75.9 9.1 %collective-permute-done = f32[64,64]{0,1:T(8,128)S(1)} collective-permute-done((f32[64,64]{0,1:T(8,128)S(1)}, f32[64,64]{0,1:T(8,128)S(1)}, u32[]{:S(2)}, u32[]{:S(2)}) %collective-permute-start) | collective-permute-done | bytes 16416 | tf_op jit(solution)/shard_map/ppermute | solution.py:17
  85.1 5.5 gather_fusion
  109.5 3.5 collective-permute-done.3
  116.4 5.0 collective-permute-done.4
  123.3 3.5 collective-permute-done.5
  128.8 4.4 collective-permute-done.6
  133.2 5.1 collective-permute-start.7
  138.3 4.3 collective-permute-done.7
  144.6 5.5 gather_fusion.1
  156.9 6.6 collective-permute-start.17
  171.9 3.5 collective-permute-done.11
  177.4 5.0 collective-permute-done.12
  184.3 3.5 collective-permute-done.13
  190.3 4.4 collective-permute-done.14
  194.7 5.1 collective-permute-start.15
  199.8 4.3 collective-permute-done.15
  207.6 5.5 gather_fusion.2
  219.6 6.6 collective-permute-start.25
  234.7 3.5 collective-permute-done.19
  240.1 5.0 collective-permute-done.20
  247.1 3.5 collective-permute-done.21
  252.5 4.4 collective-permute-done.22
  257.0 5.1 collective-permute-start.23
  262.1 4.2 collective-permute-done.23
  269.9 5.5 gather_fusion.3
  281.8 6.6 collective-permute-start.33
  297.9 3.5 collective-permute-done.27
  303.3 5.0 collective-permute-done.28
  310.3 3.5 collective-permute-done.29
  315.7 4.4 collective-permute-done.30
  320.2 5.4 collective-permute-start.31
  325.5 4.0 collective-permute-done.31
  333.7 5.5 gather_fusion.4
  347.4 6.6 collective-permute-start.41
  363.3 3.5 collective-permute-done.35
  368.7 5.0 collective-permute-done.36
  375.7 3.5 collective-permute-done.37
  381.1 4.4 collective-permute-done.38
  385.6 5.1 collective-permute-start.39
  390.7 4.3 collective-permute-done.39
  401.7 5.5 gather_fusion.5
  422.0 6.6 collective-permute-start.49
  440.4 3.5 collective-permute-done.43
  445.8 5.0 collective-permute-done.44
  452.8 3.5 collective-permute-done.45
  458.2 4.4 collective-permute-done.46
  462.7 5.3 collective-permute-start.47
  468.0 4.0 collective-permute-done.47
  477.6 7.6 %gather_fusion.6 = f32[2048,64]{1,0:T(8,128)} fusion(f32[64,384]{0,1:T(8,128)S(1)} %get-tuple-element.59, s32[2048]{0:T(1024)S(1)} %broadcast_clamp_fusion), kind=kCustom, calls=%fused_computation.6 | custom fusion | bytes 1056768 | tf_op jit(solution)/shard_map/gather | solution.py:108
  501.8 12.5 %collective-permute-start.57 = (f32[64,64]{0,1:T(8,128)S(1)}, f32[64,64]{0,1:T(8,128)S(1)}, u32[]{:S(2)}, u32[]{:S(2)}) collective-permute-start(f32[64,64]{0,1:T(8,128)S(1)} %get-tuple-element.77), channel_id=1, source_target_pairs={{1,0},{2,1},{3,2},{4,3},{5,4},{6,5},{7,6},{8,7},{9,8},{10,9},{11,1... | collective-permute-start | bytes 49160 | tf_op jit(solution)/shard_map/ppermute | solution.py:18
  518.9 3.5 collective-permute-done.51
  524.3 5.0 collective-permute-done.52
  531.3 3.5 collective-permute-done.53
  536.7 4.4 collective-permute-done.54
  543.1 7.4 %collective-permute-done.55 = f32[8]{0:T(128)S(1)} collective-permute-done((f32[8]{0:T(128)S(1)}, f32[8]{0:T(128)S(1)}, u32[]{:S(2)}, u32[]{:S(2)}) %collective-permute-start.55) | collective-permute-done | bytes 64 | tf_op jit(solution)/shard_map/ppermute | solution.py:76
  557.4 7.6 %gather_fusion.7 = f32[2048,64]{1,0:T(8,128)} fusion(f32[64,384]{0,1:T(8,128)S(1)} %fusion.110, s32[2048]{0:T(1024)S(1)} %broadcast_clamp_fusion), kind=kCustom, calls=%fused_computation.7 | custom fusion | bytes 1056768 | tf_op jit(solution)/shard_map/gather | solution.py:108
  584.9 3.5 collective-permute-done.59
  590.4 5.0 collective-permute-done.60
  597.3 3.5 collective-permute-done.61
  602.8 4.4 collective-permute-done.62
  609.1 7.4 %collective-permute-done.63 = f32[9]{0:T(128)S(1)} collective-permute-done((f32[9]{0:T(128)S(1)}, f32[9]{0:T(128)S(1)}, u32[]{:S(2)}, u32[]{:S(2)}) %collective-permute-start.63) | collective-permute-done | bytes 68 | tf_op jit(solution)/shard_map/ppermute | solution.py:76
  637.6 3.7 collective-permute-done.66
  658.1 6.1 collective-permute-done.69
  (402 shorter events, 250.2 us)
Async XLA Ops:
  67.7 8.2 %collective-permute-start.1 = (f32[64,64]{0,1:T(8,128)S(1)}, f32[64,64]{0,1:T(8,128)S(1)}, u32[]{:S(2)}, u32[]{:S(2)}) collective-permute-start(f32[64,64]{0,1:T(8,128)S(1)} %get-tuple-element.91), channel_id=1, source_target_pairs={{1,0},{2,1},{3,2},{4,3},{5,4},{6,5},{7,6},{8,7},{9,8},{10,9},{11,1... | collective-permute-start | bytes 49160 | tf_op jit(solution)/shard_map/ppermute | solution.py:18
  71.1 13.9 %collective-permute-start = (f32[64,64]{0,1:T(8,128)S(1)}, f32[64,64]{0,1:T(8,128)S(1)}, u32[]{:S(2)}, u32[]{:S(2)}) collective-permute-start(f32[64,64]{0,1:T(8,128)S(1)} %get-tuple-element.90), channel_id=1, source_target_pairs={{0,1},{1,2},{2,3},{3,4},{4,5},{5,6},{6,7},{7,8},{8,9},{9,10},{10,1... | collective-permute-start | bytes 49160 | tf_op jit(solution)/shard_map/ppermute | solution.py:17
  96.7 47.8 %collective-permute-start.9 = (f32[64,64]{0,1:T(8,128)S(1)}, f32[64,64]{0,1:T(8,128)S(1)}, u32[]{:S(2)}, u32[]{:S(2)}) collective-permute-start(f32[64,64]{0,1:T(8,128)S(1)} %get-tuple-element.89), channel_id=1, source_target_pairs={{1,0},{2,1},{3,2},{4,3},{5,4},{6,5},{7,6},{8,7},{9,8},{10,9},{11,1... | collective-permute-start | bytes 49160 | tf_op jit(solution)/shard_map/ppermute | solution.py:18
  99.9 44.6 %collective-permute-start.8 = (f32[64,64]{0,1:T(8,128)S(1)}, f32[64,64]{0,1:T(8,128)S(1)}, u32[]{:S(2)}, u32[]{:S(2)}) collective-permute-start(f32[64,64]{0,1:T(8,128)S(1)} %get-tuple-element.88), channel_id=1, source_target_pairs={{0,1},{1,2},{2,3},{3,4},{4,5},{5,6},{6,7},{7,8},{8,9},{9,10},{10,1... | collective-permute-start | bytes 49160 | tf_op jit(solution)/shard_map/ppermute | solution.py:17
  107.6 5.5 collective-permute-start.3
  114.4 7.0 %collective-permute-start.4 = (f32[2]{0:T(128)S(1)}, f32[2]{0:T(128)S(1)}, u32[]{:S(2)}, u32[]{:S(2)}) collective-permute-start(f32[2]{0:T(128)S(1)} %fusion.376), channel_id=1, source_target_pairs={{0,4},{1,5},{2,6},{3,7},{4,0},{5,1},{6,2},{7,3},{8,12},{9,13},{10,... | collective-permute-start | bytes 32 | tf_op jit(solution)/shard_map/ppermute | solution.py:76
  121.4 5.5 collective-permute-start.5
  126.8 6.3 collective-permute-start.6
  133.2 9.4 %collective-permute-start.7 = (f32[2]{0:T(128)S(1)}, f32[2]{0:T(128)S(1)}, u32[]{:S(2)}, u32[]{:S(2)}) collective-permute-start(f32[2]{0:T(128)S(1)} %add.533), channel_id=1, source_target_pairs={{0,32},{1,33},{2,34},{3,35},{4,36},{5,37},{6,38},{7,39},{8,40},{9,... | collective-permute-start | bytes 32 | tf_op jit(solution)/shard_map/ppermute | solution.py:76
  156.9 50.6 %collective-permute-start.17 = (f32[64,64]{0,1:T(8,128)S(1)}, f32[64,64]{0,1:T(8,128)S(1)}, u32[]{:S(2)}, u32[]{:S(2)}) collective-permute-start(f32[64,64]{0,1:T(8,128)S(1)} %get-tuple-element.87), channel_id=1, source_target_pairs={{1,0},{2,1},{3,2},{4,3},{5,4},{6,5},{7,6},{8,7},{9,8},{10,9},{11,1... | collective-permute-start | bytes 49160 | tf_op jit(solution)/shard_map/ppermute | solution.py:18
  163.5 44.0 %collective-permute-start.16 = (f32[64,64]{0,1:T(8,128)S(1)}, f32[64,64]{0,1:T(8,128)S(1)}, u32[]{:S(2)}, u32[]{:S(2)}) collective-permute-start(f32[64,64]{0,1:T(8,128)S(1)} %get-tuple-element.86), channel_id=1, source_target_pairs={{0,1},{1,2},{2,3},{3,4},{4,5},{5,6},{6,7},{7,8},{8,9},{9,10},{10,1... | collective-permute-start | bytes 49160 | tf_op jit(solution)/shard_map/ppermute | solution.py:17
  170.0 5.5 collective-permute-start.11
  175.5 7.0 %collective-permute-start.12 = (f32[3]{0:T(128)S(1)}, f32[3]{0:T(128)S(1)}, u32[]{:S(2)}, u32[]{:S(2)}) collective-permute-start(f32[3]{0:T(128)S(1)} %add.539), channel_id=1, source_target_pairs={{0,4},{1,5},{2,6},{3,7},{4,0},{5,1},{6,2},{7,3},{8,12},{9,13},{10,... | collective-permute-start | bytes 44 | tf_op jit(solution)/shard_map/ppermute | solution.py:76
  182.4 5.5 collective-permute-start.13
  187.9 6.8 %collective-permute-start.14 = (f32[3]{0:T(128)S(1)}, f32[3]{0:T(128)S(1)}, u32[]{:S(2)}, u32[]{:S(2)}) collective-permute-start(f32[3]{0:T(128)S(1)} %add.541), channel_id=1, source_target_pairs={{0,16},{1,17},{2,18},{3,19},{4,20},{5,21},{6,22},{7,23},{8,24},{9,... | collective-permute-start | bytes 44 | tf_op jit(solution)/shard_map/ppermute | solution.py:76
  194.7 9.4 %collective-permute-start.15 = (f32[3]{0:T(128)S(1)}, f32[3]{0:T(128)S(1)}, u32[]{:S(2)}, u32[]{:S(2)}) collective-permute-start(f32[3]{0:T(128)S(1)} %add.542), channel_id=1, source_target_pairs={{0,32},{1,33},{2,34},{3,35},{4,36},{5,37},{6,38},{7,39},{8,40},{9,... | collective-permute-start | bytes 44 | tf_op jit(solution)/shard_map/ppermute | solution.py:76
  219.6 50.2 %collective-permute-start.25 = (f32[64,64]{0,1:T(8,128)S(1)}, f32[64,64]{0,1:T(8,128)S(1)}, u32[]{:S(2)}, u32[]{:S(2)}) collective-permute-start(f32[64,64]{0,1:T(8,128)S(1)} %get-tuple-element.85), channel_id=1, source_target_pairs={{1,0},{2,1},{3,2},{4,3},{5,4},{6,5},{7,6},{8,7},{9,8},{10,9},{11,1... | collective-permute-start | bytes 49160 | tf_op jit(solution)/shard_map/ppermute | solution.py:18
  226.2 43.6 %collective-permute-start.24 = (f32[64,64]{0,1:T(8,128)S(1)}, f32[64,64]{0,1:T(8,128)S(1)}, u32[]{:S(2)}, u32[]{:S(2)}) collective-permute-start(f32[64,64]{0,1:T(8,128)S(1)} %get-tuple-element.84), channel_id=1, source_target_pairs={{0,1},{1,2},{2,3},{3,4},{4,5},{5,6},{6,7},{7,8},{8,9},{9,10},{10,1... | collective-permute-start | bytes 49160 | tf_op jit(solution)/shard_map/ppermute | solution.py:17
  229.0 3.0 collective-permute-start.18
  232.8 5.5 collective-permute-start.19
  238.2 7.0 %collective-permute-start.20 = (f32[4]{0:T(128)S(1)}, f32[4]{0:T(128)S(1)}, u32[]{:S(2)}, u32[]{:S(2)}) collective-permute-start(f32[4]{0:T(128)S(1)} %add.550), channel_id=1, source_target_pairs={{0,4},{1,5},{2,6},{3,7},{4,0},{5,1},{6,2},{7,3},{8,12},{9,13},{10,... | collective-permute-start | bytes 56 | tf_op jit(solution)/shard_map/ppermute | solution.py:76
  245.2 5.5 collective-permute-start.21
  250.6 6.3 collective-permute-start.22
  257.0 9.4 %collective-permute-start.23 = (f32[4]{0:T(128)S(1)}, f32[4]{0:T(128)S(1)}, u32[]{:S(2)}, u32[]{:S(2)}) collective-permute-start(f32[4]{0:T(128)S(1)} %add.553), channel_id=1, source_target_pairs={{0,32},{1,33},{2,34},{3,35},{4,36},{5,37},{6,38},{7,39},{8,40},{9,... | collective-permute-start | bytes 56 | tf_op jit(solution)/shard_map/ppermute | solution.py:76
  281.8 51.7 %collective-permute-start.33 = (f32[64,64]{0,1:T(8,128)S(1)}, f32[64,64]{0,1:T(8,128)S(1)}, u32[]{:S(2)}, u32[]{:S(2)}) collective-permute-start(f32[64,64]{0,1:T(8,128)S(1)} %get-tuple-element.83), channel_id=1, source_target_pairs={{1,0},{2,1},{3,2},{4,3},{5,4},{6,5},{7,6},{8,7},{9,8},{10,9},{11,1... | collective-permute-start | bytes 49160 | tf_op jit(solution)/shard_map/ppermute | solution.py:18
  288.4 45.1 %collective-permute-start.32 = (f32[64,64]{0,1:T(8,128)S(1)}, f32[64,64]{0,1:T(8,128)S(1)}, u32[]{:S(2)}, u32[]{:S(2)}) collective-permute-start(f32[64,64]{0,1:T(8,128)S(1)} %get-tuple-element.82), channel_id=1, source_target_pairs={{0,1},{1,2},{2,3},{3,4},{4,5},{5,6},{6,7},{7,8},{8,9},{9,10},{10,1... | collective-permute-start | bytes 49160 | tf_op jit(solution)/shard_map/ppermute | solution.py:17
  295.9 5.5 collective-permute-start.27
  301.4 7.0 %collective-permute-start.28 = (f32[5]{0:T(128)S(1)}, f32[5]{0:T(128)S(1)}, u32[]{:S(2)}, u32[]{:S(2)}) collective-permute-start(f32[5]{0:T(128)S(1)} %add.561), channel_id=1, source_target_pairs={{0,4},{1,5},{2,6},{3,7},{4,0},{5,1},{6,2},{7,3},{8,12},{9,13},{10,... | collective-permute-start | bytes 68 | tf_op jit(solution)/shard_map/ppermute | solution.py:76
  308.4 5.5 collective-permute-start.29
  313.8 6.3 collective-permute-start.30
  320.2 9.4 %collective-permute-start.31 = (f32[5]{0:T(128)S(1)}, f32[5]{0:T(128)S(1)}, u32[]{:S(2)}, u32[]{:S(2)}) collective-permute-start(f32[5]{0:T(128)S(1)} %add.564), channel_id=1, source_target_pairs={{0,32},{1,33},{2,34},{3,35},{4,36},{5,37},{6,38},{7,39},{8,40},{9,... | collective-permute-start | bytes 68 | tf_op jit(solution)/shard_map/ppermute | solution.py:76
  347.4 52.9 %collective-permute-start.41 = (f32[64,64]{0,1:T(8,128)S(1)}, f32[64,64]{0,1:T(8,128)S(1)}, u32[]{:S(2)}, u32[]{:S(2)}) collective-permute-start(f32[64,64]{0,1:T(8,128)S(1)} %get-tuple-element.81), channel_id=1, source_target_pairs={{1,0},{2,1},{3,2},{4,3},{5,4},{6,5},{7,6},{8,7},{9,8},{10,9},{11,1... | collective-permute-start | bytes 49160 | tf_op jit(solution)/shard_map/ppermute | solution.py:18
  354.0 46.3 %collective-permute-start.40 = (f32[64,64]{0,1:T(8,128)S(1)}, f32[64,64]{0,1:T(8,128)S(1)}, u32[]{:S(2)}, u32[]{:S(2)}) collective-permute-start(f32[64,64]{0,1:T(8,128)S(1)} %get-tuple-element.80), channel_id=1, source_target_pairs={{0,1},{1,2},{2,3},{3,4},{4,5},{5,6},{6,7},{7,8},{8,9},{9,10},{10,1... | collective-permute-start | bytes 49160 | tf_op jit(solution)/shard_map/ppermute | solution.py:17
  361.4 5.5 collective-permute-start.35
  366.8 7.0 %collective-permute-start.36 = (f32[6]{0:T(128)S(1)}, f32[6]{0:T(128)S(1)}, u32[]{:S(2)}, u32[]{:S(2)}) collective-permute-start(f32[6]{0:T(128)S(1)} %add.572), channel_id=1, source_target_pairs={{0,4},{1,5},{2,6},{3,7},{4,0},{5,1},{6,2},{7,3},{8,12},{9,13},{10,... | collective-permute-start | bytes 80 | tf_op jit(solution)/shard_map/ppermute | solution.py:76
  373.8 5.5 collective-permute-start.37
  379.2 6.3 collective-permute-start.38
  385.6 9.4 %collective-permute-start.39 = (f32[6]{0:T(128)S(1)}, f32[6]{0:T(128)S(1)}, u32[]{:S(2)}, u32[]{:S(2)}) collective-permute-start(f32[6]{0:T(128)S(1)} %add.575), channel_id=1, source_target_pairs={{0,32},{1,33},{2,34},{3,35},{4,36},{5,37},{6,38},{7,39},{8,40},{9,... | collective-permute-start | bytes 80 | tf_op jit(solution)/shard_map/ppermute | solution.py:76
  422.0 55.4 %collective-permute-start.49 = (f32[64,64]{0,1:T(8,128)S(1)}, f32[64,64]{0,1:T(8,128)S(1)}, u32[]{:S(2)}, u32[]{:S(2)}) collective-permute-start(f32[64,64]{0,1:T(8,128)S(1)} %get-tuple-element.79), channel_id=1, source_target_pairs={{1,0},{2,1},{3,2},{4,3},{5,4},{6,5},{7,6},{8,7},{9,8},{10,9},{11,1... | collective-permute-start | bytes 49160 | tf_op jit(solution)/shard_map/ppermute | solution.py:18
  428.6 48.9 %collective-permute-start.48 = (f32[64,64]{0,1:T(8,128)S(1)}, f32[64,64]{0,1:T(8,128)S(1)}, u32[]{:S(2)}, u32[]{:S(2)}) collective-permute-start(f32[64,64]{0,1:T(8,128)S(1)} %get-tuple-element.78), channel_id=1, source_target_pairs={{0,1},{1,2},{2,3},{3,4},{4,5},{5,6},{6,7},{7,8},{8,9},{9,10},{10,1... | collective-permute-start | bytes 49160 | tf_op jit(solution)/shard_map/ppermute | solution.py:17
  438.5 5.5 collective-permute-start.43
  443.9 7.0 %collective-permute-start.44 = (f32[7]{0:T(128)S(1)}, f32[7]{0:T(128)S(1)}, u32[]{:S(2)}, u32[]{:S(2)}) collective-permute-start(f32[7]{0:T(128)S(1)} %add.583), channel_id=1, source_target_pairs={{0,4},{1,5},{2,6},{3,7},{4,0},{5,1},{6,2},{7,3},{8,12},{9,13},{10,... | collective-permute-start | bytes 92 | tf_op jit(solution)/shard_map/ppermute | solution.py:76
  450.9 5.5 collective-permute-start.45
  456.3 6.3 collective-permute-start.46
  462.7 9.4 %collective-permute-start.47 = (f32[7]{0:T(128)S(1)}, f32[7]{0:T(128)S(1)}, u32[]{:S(2)}, u32[]{:S(2)}) collective-permute-start(f32[7]{0:T(128)S(1)} %add.586), channel_id=1, source_target_pairs={{0,32},{1,33},{2,34},{3,35},{4,36},{5,37},{6,38},{7,39},{8,40},{9,... | collective-permute-start | bytes 92 | tf_op jit(solution)/shard_map/ppermute | solution.py:76
  499.8 16.4 %collective-permute-start.50 = (f32[8]{0:T(128)S(1)}, f32[8]{0:T(128)S(1)}, u32[]{:S(2)}, u32[]{:S(2)}) collective-permute-start(f32[8]{0:T(128)S(1)} %pad_maximum_fusion.7), channel_id=1, source_target_pairs={{0,1},{1,0},{2,3},{3,2},{4,5},{5,4},{6,7},{7,6},{8,9},{9,8},{10,11... | collective-permute-start | bytes 104 | tf_op jit(solution)/shard_map/ppermute | solution.py:76
  501.8 55.4 %collective-permute-start.57 = (f32[64,64]{0,1:T(8,128)S(1)}, f32[64,64]{0,1:T(8,128)S(1)}, u32[]{:S(2)}, u32[]{:S(2)}) collective-permute-start(f32[64,64]{0,1:T(8,128)S(1)} %get-tuple-element.77), channel_id=1, source_target_pairs={{1,0},{2,1},{3,2},{4,3},{5,4},{6,5},{7,6},{8,7},{9,8},{10,9},{11,1... | collective-permute-start | bytes 49160 | tf_op jit(solution)/shard_map/ppermute | solution.py:18
  514.3 42.9 %collective-permute-start.56 = (f32[64,64]{0,1:T(8,128)S(1)}, f32[64,64]{0,1:T(8,128)S(1)}, u32[]{:S(2)}, u32[]{:S(2)}) collective-permute-start(f32[64,64]{0,1:T(8,128)S(1)} %get-tuple-element.76), channel_id=1, source_target_pairs={{0,1},{1,2},{2,3},{3,4},{4,5},{5,6},{6,7},{7,8},{8,9},{9,10},{10,1... | collective-permute-start | bytes 49160 | tf_op jit(solution)/shard_map/ppermute | solution.py:17
  516.9 5.5 collective-permute-start.51
  522.4 7.0 %collective-permute-start.52 = (f32[8]{0:T(128)S(1)}, f32[8]{0:T(128)S(1)}, u32[]{:S(2)}, u32[]{:S(2)}) collective-permute-start(f32[8]{0:T(128)S(1)} %add.594), channel_id=1, source_target_pairs={{0,4},{1,5},{2,6},{3,7},{4,0},{5,1},{6,2},{7,3},{8,12},{9,13},{10,... | collective-permute-start | bytes 104 | tf_op jit(solution)/shard_map/ppermute | solution.py:76
  529.3 5.5 collective-permute-start.53
  534.8 6.3 collective-permute-start.54
  541.2 9.4 %collective-permute-start.55 = (f32[8]{0:T(128)S(1)}, f32[8]{0:T(128)S(1)}, u32[]{:S(2)}, u32[]{:S(2)}) collective-permute-start(f32[8]{0:T(128)S(1)} %add.597), channel_id=1, source_target_pairs={{0,32},{1,33},{2,34},{3,35},{4,36},{5,37},{6,38},{7,39},{8,40},{9,... | collective-permute-start | bytes 104 | tf_op jit(solution)/shard_map/ppermute | solution.py:76
  583.0 5.5 collective-permute-start.59
  588.4 7.0 %collective-permute-start.60 = (f32[9]{0:T(128)S(1)}, f32[9]{0:T(128)S(1)}, u32[]{:S(2)}, u32[]{:S(2)}) collective-permute-start(f32[9]{0:T(128)S(1)} %add.605), channel_id=1, source_target_pairs={{0,4},{1,5},{2,6},{3,7},{4,0},{5,1},{6,2},{7,3},{8,12},{9,13},{10,... | collective-permute-start | bytes 116 | tf_op jit(solution)/shard_map/ppermute | solution.py:76
  595.4 5.5 collective-permute-start.61
  600.9 6.3 collective-permute-start.62
  607.2 9.4 %collective-permute-start.63 = (f32[9]{0:T(128)S(1)}, f32[9]{0:T(128)S(1)}, u32[]{:S(2)}, u32[]{:S(2)}) collective-permute-start(f32[9]{0:T(128)S(1)} %add.608), channel_id=1, source_target_pairs={{0,32},{1,33},{2,34},{3,35},{4,36},{5,37},{6,38},{7,39},{8,40},{9,... | collective-permute-start | bytes 116 | tf_op jit(solution)/shard_map/ppermute | solution.py:76
  623.8 3.3 collective-permute-start.64
  628.3 5.4 collective-permute-start.65
  634.4 6.9 %collective-permute-start.66 = (f32[1]{0:T(128)}, f32[1]{0:T(128)}, u32[]{:S(2)}, u32[]{:S(2)}) collective-permute-start(f32[1]{0:T(128)} %add.613), channel_id=1, source_target_pairs={{0,4},{1,5},{2,6},{3,7},{4,0},{5,1},{6,2},{7,3},{8,12},{9,13},{10,... | collective-permute-start | bytes 20 | tf_op jit(solution)/shard_map/ppermute | solution.py:76
  641.9 5.4 collective-permute-start.67
  647.9 6.3 collective-permute-start.68
  654.9 9.3 %collective-permute-start.69 = (f32[1]{0:T(128)}, f32[1]{0:T(128)}, u32[]{:S(2)}, u32[]{:S(2)}) collective-permute-start(f32[1]{0:T(128)} %add.616), channel_id=1, source_target_pairs={{0,32},{1,33},{2,34},{3,35},{4,36},{5,37},{6,38},{7,39},{8,40},{9,... | collective-permute-start | bytes 20 | tf_op jit(solution)/shard_map/ppermute | solution.py:76
  (44 other events, 737.2 us)

commit v5 on v4

--- a/solution.py
+++ b/solution.py
@@ -89,6 +89,7 @@
     relative = jnp.mod(neighbors - lax.axis_index("space") * nodes_own, total_nodes)
     relative = jnp.where(relative >= total_nodes - halo_width, relative - total_nodes, relative)
     ext_index = relative + halo_width
+    select = (ext_index.reshape(1, -1) == jnp.arange(nodes_own + 2 * halo_width)[:, None]).astype(jnp.float32)
     all_harm = jnp.arange(harmonics)
     harm_order = (all_harm // 2 + 1).astype(jnp.float32)
     sign_vals = jnp.where(all_harm % 2 == 0, 1.0, -1.0).astype(jnp.float32)
@@ -105,7 +106,8 @@
 
     def operate(extended):
         vector_in = inner(extended)
-        gradients = vector_in[:, None, :] - extended[:, ext_index]
+        gathered = matmul_high(extended, select).reshape(harmonics, -1, nodes_own)
+        gradients = vector_in[:, None, :] - gathered
         grad_flat = gradients.reshape(harmonics, -1)
         spec_real = matmul_high(cos_table, grad_flat)
         spec_imag = -matmul_high(sin_table, grad_flat)

time: 682 us -> 603 us (0.88)
  local copies, waits for them, and re-layouts: 91.2 us -> 23 us
    gather x8 -> x0, local copies, waits for them, and re-layouts: 48 us -> none  [operate(): gradients = vector_in[:, None, :] - extended[:, ext_index]]
    unnamed x93 -> x49, local copies, waits for them, and re-layouts: 16.2 us -> 9.92 us
    dot_general x34 -> x42, matrix products: 37.3 us -> 35 us  [matmul_high(): jnp.dot(left, right, precision=lax.Precision.HIGHEST, preferred_element_t...]
where the time goes in v5:
time: 603 us; the launch traced here: 594 us
  waiting for transfers between devices  206 us (34%)
  starting transfers between devices  197 us (33%)
  blocking collectives  66.3 us (11%)
  between operations  37.9 us (6%)
  matrix products  35 us (6%)
  other arithmetic  29.1 us (5%)
  local copies, waits for them, and re-layouts  23 us (4%)
    ppermute x54, waiting for transfers between devices, all_sum(): lax.ppermute(values, axis, [(i, i ^ stride) for i in range(count)])  196 us
    ppermute x54, starting transfers between devices, all_sum(): lax.ppermute(values, axis, [(i, i ^ stride) for i in range(count)])  130 us
    all_gather x1, blocking collectives, per_device(): rhs_field = lax.all_gather(rhs_field, 'harm', axis=0, tiled=True)  66.3 us
    ppermute x8, starting transfers between devices, with_halo(): after = lax.ppermute(leading, axis, down)  51.6 us
    dot_general x42, matrix products, matmul_high(): jnp.dot(left, right, precision=lax.Precision.HIGHEST, preferred_element_t...  35 us
    ppermute x8, starting transfers between devices, with_halo(): before = lax.ppermute(last, axis, up)  15.4 us
  transfers between devices with their start and end apart: 70, of which 54 were waited for; matrix products, arithmetic and copies ran while one was open for 4% of the time, Pallas kernels for 0%

profile of v5, /device:TPU:6, one launch (start us, length us, event | category | flops | bytes accessed | tf_op | source)
XLA Modules:
  0.0 594.2 jit_solution(2548696434519355967)
XLA Ops:
  1.3 66.3 %all_gather.3 = f32[64,256]{1,0:T(8,128)S(1)} all-gather(f32[8,256]{1,0:T(8,128)S(1)} %copy-done.9), channel_id=1, replica_groups=mesh['harm'=8,'space'=64] {'harm'}, dimensions={0}, use_global_device_ids=true | all-gather | bytes 73728 | tf_op jit(solution)/shard_map/all_gather | solution.py:124
  67.7 3.4 collective-permute-start.1
  75.3 9.7 %collective-permute-done = f32[64,64]{1,0:T(8,128)S(1)} collective-permute-done((f32[64,64]{1,0:T(8,128)S(1)}, f32[64,64]{1,0:T(8,128)S(1)}, u32[]{:S(2)}, u32[]{:S(2)}) %collective-permute-start) | collective-permute-done | bytes 16416 | tf_op jit(solution)/shard_map/ppermute | solution.py:17
  90.9 2.7 collective-permute-start.9
  103.2 3.5 collective-permute-done.3
  110.0 5.0 collective-permute-done.4
  117.0 3.5 collective-permute-done.5
  122.4 4.4 collective-permute-done.6
  126.9 5.6 collective-permute-start.7
  132.5 3.7 collective-permute-done.7
  145.2 6.6 %collective-permute-start.17 = (f32[64,64]{1,0:T(8,128)S(1)}, f32[64,64]{1,0:T(8,128)S(1)}, u32[]{:S(2)}, u32[]{:S(2)}) collective-permute-start(f32[64,64]{1,0:T(8,128)S(1)} %get-tuple-element.82), channel_id=1, source_target_pairs={{1,0},{2,1},{3,2},{4,3},{5,4},{6,5},{7,6},{8,7},{9,8},{10,9},{11,1... | collective-permute-start | bytes 49160 | tf_op jit(solution)/shard_map/ppermute | solution.py:18
  160.2 3.5 collective-permute-done.11
  165.7 5.0 collective-permute-done.12
  172.6 3.5 collective-permute-done.13
  178.1 4.4 collective-permute-done.14
  182.5 5.1 collective-permute-start.15
  187.6 4.3 collective-permute-done.15
  201.3 6.6 %collective-permute-start.25 = (f32[64,64]{1,0:T(8,128)S(1)}, f32[64,64]{1,0:T(8,128)S(1)}, u32[]{:S(2)}, u32[]{:S(2)}) collective-permute-start(f32[64,64]{1,0:T(8,128)S(1)} %get-tuple-element.80), channel_id=1, source_target_pairs={{1,0},{2,1},{3,2},{4,3},{5,4},{6,5},{7,6},{8,7},{9,8},{10,9},{11,1... | collective-permute-start | bytes 49160 | tf_op jit(solution)/shard_map/ppermute | solution.py:18
  216.5 3.5 collective-permute-done.19
  221.9 5.0 collective-permute-done.20
  228.9 3.5 collective-permute-done.21
  234.3 4.4 collective-permute-done.22
  238.8 5.3 collective-permute-start.23
  244.1 4.1 collective-permute-done.23
  257.6 6.6 %collective-permute-start.33 = (f32[64,64]{1,0:T(8,128)S(1)}, f32[64,64]{1,0:T(8,128)S(1)}, u32[]{:S(2)}, u32[]{:S(2)}) collective-permute-start(f32[64,64]{1,0:T(8,128)S(1)} %get-tuple-element.78), channel_id=1, source_target_pairs={{1,0},{2,1},{3,2},{4,3},{5,4},{6,5},{7,6},{8,7},{9,8},{10,9},{11,1... | collective-permute-start | bytes 49160 | tf_op jit(solution)/shard_map/ppermute | solution.py:18
  272.8 3.5 collective-permute-done.27
  278.2 5.0 collective-permute-done.28
  285.2 3.5 collective-permute-done.29
  290.6 4.4 collective-permute-done.30
  295.1 5.1 collective-permute-start.31
  300.2 4.3 collective-permute-done.31
  314.5 6.6 %collective-permute-start.41 = (f32[64,64]{1,0:T(8,128)S(1)}, f32[64,64]{1,0:T(8,128)S(1)}, u32[]{:S(2)}, u32[]{:S(2)}) collective-permute-start(f32[64,64]{1,0:T(8,128)S(1)} %get-tuple-element.76), channel_id=1, source_target_pairs={{1,0},{2,1},{3,2},{4,3},{5,4},{6,5},{7,6},{8,7},{9,8},{10,9},{11,1... | collective-permute-start | bytes 49160 | tf_op jit(solution)/shard_map/ppermute | solution.py:18
  330.5 3.5 collective-permute-done.35
  335.9 5.0 collective-permute-done.36
  342.9 3.5 collective-permute-done.37
  348.3 4.4 collective-permute-done.38
  352.8 5.3 collective-permute-start.39
  358.1 4.0 collective-permute-done.39
  373.6 6.6 %collective-permute-start.49 = (f32[64,64]{1,0:T(8,128)S(1)}, f32[64,64]{1,0:T(8,128)S(1)}, u32[]{:S(2)}, u32[]{:S(2)}) collective-permute-start(f32[64,64]{1,0:T(8,128)S(1)} %get-tuple-element.74), channel_id=1, source_target_pairs={{1,0},{2,1},{3,2},{4,3},{5,4},{6,5},{7,6},{8,7},{9,8},{10,9},{11,1... | collective-permute-start | bytes 49160 | tf_op jit(solution)/shard_map/ppermute | solution.py:18
  390.2 3.5 collective-permute-done.43
  395.7 5.0 collective-permute-done.44
  402.6 3.5 collective-permute-done.45
  408.1 4.4 collective-permute-done.46
  412.5 5.1 collective-permute-start.47
  417.6 4.3 collective-permute-done.47
  439.7 12.5 %collective-permute-start.57 = (f32[64,64]{1,0:T(8,128)S(1)}, f32[64,64]{1,0:T(8,128)S(1)}, u32[]{:S(2)}, u32[]{:S(2)}) collective-permute-start(f32[64,64]{1,0:T(8,128)S(1)} %get-tuple-element.72), channel_id=1, source_target_pairs={{1,0},{2,1},{3,2},{4,3},{5,4},{6,5},{7,6},{8,7},{9,8},{10,9},{11,1... | collective-permute-start | bytes 49160 | tf_op jit(solution)/shard_map/ppermute | solution.py:18
  456.8 3.5 collective-permute-done.51
  462.3 5.0 collective-permute-done.52
  469.2 3.5 collective-permute-done.53
  474.7 4.4 collective-permute-done.54
  481.3 7.2 %collective-permute-done.55 = f32[8]{0:T(128)S(1)} collective-permute-done((f32[8]{0:T(128)S(1)}, f32[8]{0:T(128)S(1)}, u32[]{:S(2)}, u32[]{:S(2)}) %collective-permute-start.55) | collective-permute-done | bytes 64 | tf_op jit(solution)/shard_map/ppermute | solution.py:76
  510.1 3.5 collective-permute-done.59
  515.5 5.0 collective-permute-done.60
  522.5 3.5 collective-permute-done.61
  528.0 4.4 collective-permute-done.62
  534.3 7.4 %collective-permute-done.63 = f32[9]{0:T(128)S(1)} collective-permute-done((f32[9]{0:T(128)S(1)}, f32[9]{0:T(128)S(1)}, u32[]{:S(2)}, u32[]{:S(2)}) %collective-permute-start.63) | collective-permute-done | bytes 68 | tf_op jit(solution)/shard_map/ppermute | solution.py:76
  553.5 3.2 collective-permute-start.65
  559.6 3.2 collective-permute-start.66
  562.8 3.7 collective-permute-done.66
  567.2 3.2 collective-permute-start.67
  573.3 3.2 collective-permute-start.68
  576.5 3.1 collective-permute-done.68
  580.3 3.2 collective-permute-start.69
  583.5 6.1 %collective-permute-done.69 = f32[1]{0:T(128)} collective-permute-done((f32[1]{0:T(128)}, f32[1]{0:T(128)}, u32[]{:S(2)}, u32[]{:S(2)}) %collective-permute-start.69) | collective-permute-done | bytes 36 | tf_op jit(solution)/shard_map/ppermute | solution.py:76
  (330 shorter events, 196.7 us)
Async XLA Ops:
  67.7 7.6 %collective-permute-start.1 = (f32[64,64]{1,0:T(8,128)S(1)}, f32[64,64]{1,0:T(8,128)S(1)}, u32[]{:S(2)}, u32[]{:S(2)}) collective-permute-start(f32[64,64]{1,0:T(8,128)S(1)} %get-tuple-element.86), channel_id=1, source_target_pairs={{1,0},{2,1},{3,2},{4,3},{5,4},{6,5},{7,6},{8,7},{9,8},{10,9},{11,1... | collective-permute-start | bytes 49160 | tf_op jit(solution)/shard_map/ppermute | solution.py:18
  71.1 13.9 %collective-permute-start = (f32[64,64]{1,0:T(8,128)S(1)}, f32[64,64]{1,0:T(8,128)S(1)}, u32[]{:S(2)}, u32[]{:S(2)}) collective-permute-start(f32[64,64]{1,0:T(8,128)S(1)} %get-tuple-element.85), channel_id=1, source_target_pairs={{0,1},{1,2},{2,3},{3,4},{4,5},{5,6},{6,7},{7,8},{8,9},{9,10},{10,1... | collective-permute-start | bytes 49160 | tf_op jit(solution)/shard_map/ppermute | solution.py:17
  90.9 47.3 %collective-permute-start.9 = (f32[64,64]{1,0:T(8,128)S(1)}, f32[64,64]{1,0:T(8,128)S(1)}, u32[]{:S(2)}, u32[]{:S(2)}) collective-permute-start(f32[64,64]{1,0:T(8,128)S(1)} %get-tuple-element.84), channel_id=1, source_target_pairs={{1,0},{2,1},{3,2},{4,3},{5,4},{6,5},{7,6},{8,7},{9,8},{10,9},{11,1... | collective-permute-start | bytes 49160 | tf_op jit(solution)/shard_map/ppermute | solution.py:18
  93.6 44.6 %collective-permute-start.8 = (f32[64,64]{1,0:T(8,128)S(1)}, f32[64,64]{1,0:T(8,128)S(1)}, u32[]{:S(2)}, u32[]{:S(2)}) collective-permute-start(f32[64,64]{1,0:T(8,128)S(1)} %get-tuple-element.83), channel_id=1, source_target_pairs={{0,1},{1,2},{2,3},{3,4},{4,5},{5,6},{6,7},{7,8},{8,9},{9,10},{10,1... | collective-permute-start | bytes 49160 | tf_op jit(solution)/shard_map/ppermute | solution.py:17
  101.3 5.5 collective-permute-start.3
  108.1 7.0 %collective-permute-start.4 = (f32[2]{0:T(128)S(1)}, f32[2]{0:T(128)S(1)}, u32[]{:S(2)}, u32[]{:S(2)}) collective-permute-start(f32[2]{0:T(128)S(1)} %fusion.411), channel_id=1, source_target_pairs={{0,4},{1,5},{2,6},{3,7},{4,0},{5,1},{6,2},{7,3},{8,12},{9,13},{10,... | collective-permute-start | bytes 32 | tf_op jit(solution)/shard_map/ppermute | solution.py:76
  115.1 5.5 collective-permute-start.5
  120.5 6.3 %collective-permute-start.6 = (f32[2]{0:T(128)S(1)}, f32[2]{0:T(128)S(1)}, u32[]{:S(2)}, u32[]{:S(2)}) collective-permute-start(f32[2]{0:T(128)S(1)} %add.516), channel_id=1, source_target_pairs={{0,16},{1,17},{2,18},{3,19},{4,20},{5,21},{6,22},{7,23},{8,24},{9,... | collective-permute-start | bytes 32 | tf_op jit(solution)/shard_map/ppermute | solution.py:76
  126.9 9.4 %collective-permute-start.7 = (f32[2]{0:T(128)S(1)}, f32[2]{0:T(128)S(1)}, u32[]{:S(2)}, u32[]{:S(2)}) collective-permute-start(f32[2]{0:T(128)S(1)} %add.517), channel_id=1, source_target_pairs={{0,32},{1,33},{2,34},{3,35},{4,36},{5,37},{6,38},{7,39},{8,40},{9,... | collective-permute-start | bytes 32 | tf_op jit(solution)/shard_map/ppermute | solution.py:76
  145.2 50.0 %collective-permute-start.17 = (f32[64,64]{1,0:T(8,128)S(1)}, f32[64,64]{1,0:T(8,128)S(1)}, u32[]{:S(2)}, u32[]{:S(2)}) collective-permute-start(f32[64,64]{1,0:T(8,128)S(1)} %get-tuple-element.82), channel_id=1, source_target_pairs={{1,0},{2,1},{3,2},{4,3},{5,4},{6,5},{7,6},{8,7},{9,8},{10,9},{11,1... | collective-permute-start | bytes 49160 | tf_op jit(solution)/shard_map/ppermute | solution.py:18
  151.8 43.4 %collective-permute-start.16 = (f32[64,64]{1,0:T(8,128)S(1)}, f32[64,64]{1,0:T(8,128)S(1)}, u32[]{:S(2)}, u32[]{:S(2)}) collective-permute-start(f32[64,64]{1,0:T(8,128)S(1)} %get-tuple-element.81), channel_id=1, source_target_pairs={{0,1},{1,2},{2,3},{3,4},{4,5},{5,6},{6,7},{7,8},{8,9},{9,10},{10,1... | collective-permute-start | bytes 49160 | tf_op jit(solution)/shard_map/ppermute | solution.py:17
  158.3 5.5 collective-permute-start.11
  163.8 7.0 %collective-permute-start.12 = (f32[3]{0:T(128)S(1)}, f32[3]{0:T(128)S(1)}, u32[]{:S(2)}, u32[]{:S(2)}) collective-permute-start(f32[3]{0:T(128)S(1)} %add.523), channel_id=1, source_target_pairs={{0,4},{1,5},{2,6},{3,7},{4,0},{5,1},{6,2},{7,3},{8,12},{9,13},{10,... | collective-permute-start | bytes 44 | tf_op jit(solution)/shard_map/ppermute | solution.py:76
  170.7 5.5 collective-permute-start.13
  176.2 6.3 %collective-permute-start.14 = (f32[3]{0:T(128)S(1)}, f32[3]{0:T(128)S(1)}, u32[]{:S(2)}, u32[]{:S(2)}) collective-permute-start(f32[3]{0:T(128)S(1)} %add.525), channel_id=1, source_target_pairs={{0,16},{1,17},{2,18},{3,19},{4,20},{5,21},{6,22},{7,23},{8,24},{9,... | collective-permute-start | bytes 44 | tf_op jit(solution)/shard_map/ppermute | solution.py:76
  182.5 9.4 %collective-permute-start.15 = (f32[3]{0:T(128)S(1)}, f32[3]{0:T(128)S(1)}, u32[]{:S(2)}, u32[]{:S(2)}) collective-permute-start(f32[3]{0:T(128)S(1)} %add.526), channel_id=1, source_target_pairs={{0,32},{1,33},{2,34},{3,35},{4,36},{5,37},{6,38},{7,39},{8,40},{9,... | collective-permute-start | bytes 44 | tf_op jit(solution)/shard_map/ppermute | solution.py:76
  201.3 50.2 %collective-permute-start.25 = (f32[64,64]{1,0:T(8,128)S(1)}, f32[64,64]{1,0:T(8,128)S(1)}, u32[]{:S(2)}, u32[]{:S(2)}) collective-permute-start(f32[64,64]{1,0:T(8,128)S(1)} %get-tuple-element.80), channel_id=1, source_target_pairs={{1,0},{2,1},{3,2},{4,3},{5,4},{6,5},{7,6},{8,7},{9,8},{10,9},{11,1... | collective-permute-start | bytes 49160 | tf_op jit(solution)/shard_map/ppermute | solution.py:18
  207.9 43.6 %collective-permute-start.24 = (f32[64,64]{1,0:T(8,128)S(1)}, f32[64,64]{1,0:T(8,128)S(1)}, u32[]{:S(2)}, u32[]{:S(2)}) collective-permute-start(f32[64,64]{1,0:T(8,128)S(1)} %get-tuple-element.79), channel_id=1, source_target_pairs={{0,1},{1,2},{2,3},{3,4},{4,5},{5,6},{6,7},{7,8},{8,9},{9,10},{10,1... | collective-permute-start | bytes 49160 | tf_op jit(solution)/shard_map/ppermute | solution.py:17
  210.8 3.0 collective-permute-start.18
  214.5 5.5 collective-permute-start.19
  220.0 7.0 %collective-permute-start.20 = (f32[4]{0:T(128)S(1)}, f32[4]{0:T(128)S(1)}, u32[]{:S(2)}, u32[]{:S(2)}) collective-permute-start(f32[4]{0:T(128)S(1)} %add.534), channel_id=1, source_target_pairs={{0,4},{1,5},{2,6},{3,7},{4,0},{5,1},{6,2},{7,3},{8,12},{9,13},{10,... | collective-permute-start | bytes 56 | tf_op jit(solution)/shard_map/ppermute | solution.py:76
  226.9 5.5 collective-permute-start.21
  232.4 6.3 %collective-permute-start.22 = (f32[4]{0:T(128)S(1)}, f32[4]{0:T(128)S(1)}, u32[]{:S(2)}, u32[]{:S(2)}) collective-permute-start(f32[4]{0:T(128)S(1)} %add.536), channel_id=1, source_target_pairs={{0,16},{1,17},{2,18},{3,19},{4,20},{5,21},{6,22},{7,23},{8,24},{9,... | collective-permute-start | bytes 56 | tf_op jit(solution)/shard_map/ppermute | solution.py:76
  238.8 9.4 %collective-permute-start.23 = (f32[4]{0:T(128)S(1)}, f32[4]{0:T(128)S(1)}, u32[]{:S(2)}, u32[]{:S(2)}) collective-permute-start(f32[4]{0:T(128)S(1)} %add.537), channel_id=1, source_target_pairs={{0,32},{1,33},{2,34},{3,35},{4,36},{5,37},{6,38},{7,39},{8,40},{9,... | collective-permute-start | bytes 56 | tf_op jit(solution)/shard_map/ppermute | solution.py:76
  257.6 50.9 %collective-permute-start.33 = (f32[64,64]{1,0:T(8,128)S(1)}, f32[64,64]{1,0:T(8,128)S(1)}, u32[]{:S(2)}, u32[]{:S(2)}) collective-permute-start(f32[64,64]{1,0:T(8,128)S(1)} %get-tuple-element.78), channel_id=1, source_target_pairs={{1,0},{2,1},{3,2},{4,3},{5,4},{6,5},{7,6},{8,7},{9,8},{10,9},{11,1... | collective-permute-start | bytes 49160 | tf_op jit(solution)/shard_map/ppermute | solution.py:18
  264.2 44.2 %collective-permute-start.32 = (f32[64,64]{1,0:T(8,128)S(1)}, f32[64,64]{1,0:T(8,128)S(1)}, u32[]{:S(2)}, u32[]{:S(2)}) collective-permute-start(f32[64,64]{1,0:T(8,128)S(1)} %get-tuple-element.77), channel_id=1, source_target_pairs={{0,1},{1,2},{2,3},{3,4},{4,5},{5,6},{6,7},{7,8},{8,9},{9,10},{10,1... | collective-permute-start | bytes 49160 | tf_op jit(solution)/shard_map/ppermute | solution.py:17
  270.8 5.5 collective-permute-start.27
  276.3 7.0 %collective-permute-start.28 = (f32[5]{0:T(128)S(1)}, f32[5]{0:T(128)S(1)}, u32[]{:S(2)}, u32[]{:S(2)}) collective-permute-start(f32[5]{0:T(128)S(1)} %add.545), channel_id=1, source_target_pairs={{0,4},{1,5},{2,6},{3,7},{4,0},{5,1},{6,2},{7,3},{8,12},{9,13},{10,... | collective-permute-start | bytes 68 | tf_op jit(solution)/shard_map/ppermute | solution.py:76
  283.3 5.5 collective-permute-start.29
  288.7 6.3 %collective-permute-start.30 = (f32[5]{0:T(128)S(1)}, f32[5]{0:T(128)S(1)}, u32[]{:S(2)}, u32[]{:S(2)}) collective-permute-start(f32[5]{0:T(128)S(1)} %add.547), channel_id=1, source_target_pairs={{0,16},{1,17},{2,18},{3,19},{4,20},{5,21},{6,22},{7,23},{8,24},{9,... | collective-permute-start | bytes 68 | tf_op jit(solution)/shard_map/ppermute | solution.py:76
  295.1 9.4 %collective-permute-start.31 = (f32[5]{0:T(128)S(1)}, f32[5]{0:T(128)S(1)}, u32[]{:S(2)}, u32[]{:S(2)}) collective-permute-start(f32[5]{0:T(128)S(1)} %add.548), channel_id=1, source_target_pairs={{0,32},{1,33},{2,34},{3,35},{4,36},{5,37},{6,38},{7,39},{8,40},{9,... | collective-permute-start | bytes 68 | tf_op jit(solution)/shard_map/ppermute | solution.py:76
  314.5 53.0 %collective-permute-start.41 = (f32[64,64]{1,0:T(8,128)S(1)}, f32[64,64]{1,0:T(8,128)S(1)}, u32[]{:S(2)}, u32[]{:S(2)}) collective-permute-start(f32[64,64]{1,0:T(8,128)S(1)} %get-tuple-element.76), channel_id=1, source_target_pairs={{1,0},{2,1},{3,2},{4,3},{5,4},{6,5},{7,6},{8,7},{9,8},{10,9},{11,1... | collective-permute-start | bytes 49160 | tf_op jit(solution)/shard_map/ppermute | solution.py:18
  321.1 46.4 %collective-permute-start.40 = (f32[64,64]{1,0:T(8,128)S(1)}, f32[64,64]{1,0:T(8,128)S(1)}, u32[]{:S(2)}, u32[]{:S(2)}) collective-permute-start(f32[64,64]{1,0:T(8,128)S(1)} %get-tuple-element.75), channel_id=1, source_target_pairs={{0,1},{1,2},{2,3},{3,4},{4,5},{5,6},{6,7},{7,8},{8,9},{9,10},{10,1... | collective-permute-start | bytes 49160 | tf_op jit(solution)/shard_map/ppermute | solution.py:17
  328.6 5.5 collective-permute-start.35
  334.0 7.0 %collective-permute-start.36 = (f32[6]{0:T(128)S(1)}, f32[6]{0:T(128)S(1)}, u32[]{:S(2)}, u32[]{:S(2)}) collective-permute-start(f32[6]{0:T(128)S(1)} %add.556), channel_id=1, source_target_pairs={{0,4},{1,5},{2,6},{3,7},{4,0},{5,1},{6,2},{7,3},{8,12},{9,13},{10,... | collective-permute-start | bytes 80 | tf_op jit(solution)/shard_map/ppermute | solution.py:76
  341.0 5.5 collective-permute-start.37
  346.4 6.3 %collective-permute-start.38 = (f32[6]{0:T(128)S(1)}, f32[6]{0:T(128)S(1)}, u32[]{:S(2)}, u32[]{:S(2)}) collective-permute-start(f32[6]{0:T(128)S(1)} %add.558), channel_id=1, source_target_pairs={{0,16},{1,17},{2,18},{3,19},{4,20},{5,21},{6,22},{7,23},{8,24},{9,... | collective-permute-start | bytes 80 | tf_op jit(solution)/shard_map/ppermute | solution.py:76
  352.8 9.4 %collective-permute-start.39 = (f32[6]{0:T(128)S(1)}, f32[6]{0:T(128)S(1)}, u32[]{:S(2)}, u32[]{:S(2)}) collective-permute-start(f32[6]{0:T(128)S(1)} %add.559), channel_id=1, source_target_pairs={{0,32},{1,33},{2,34},{3,35},{4,36},{5,37},{6,38},{7,39},{8,40},{9,... | collective-permute-start | bytes 80 | tf_op jit(solution)/shard_map/ppermute | solution.py:76
  373.6 53.5 %collective-permute-start.49 = (f32[64,64]{1,0:T(8,128)S(1)}, f32[64,64]{1,0:T(8,128)S(1)}, u32[]{:S(2)}, u32[]{:S(2)}) collective-permute-start(f32[64,64]{1,0:T(8,128)S(1)} %get-tuple-element.74), channel_id=1, source_target_pairs={{1,0},{2,1},{3,2},{4,3},{5,4},{6,5},{7,6},{8,7},{9,8},{10,9},{11,1... | collective-permute-start | bytes 49160 | tf_op jit(solution)/shard_map/ppermute | solution.py:18
  380.2 46.9 %collective-permute-start.48 = (f32[64,64]{1,0:T(8,128)S(1)}, f32[64,64]{1,0:T(8,128)S(1)}, u32[]{:S(2)}, u32[]{:S(2)}) collective-permute-start(f32[64,64]{1,0:T(8,128)S(1)} %get-tuple-element.73), channel_id=1, source_target_pairs={{0,1},{1,2},{2,3},{3,4},{4,5},{5,6},{6,7},{7,8},{8,9},{9,10},{10,1... | collective-permute-start | bytes 49160 | tf_op jit(solution)/shard_map/ppermute | solution.py:17
  388.3 5.5 collective-permute-start.43
  393.8 7.0 %collective-permute-start.44 = (f32[7]{0:T(128)S(1)}, f32[7]{0:T(128)S(1)}, u32[]{:S(2)}, u32[]{:S(2)}) collective-permute-start(f32[7]{0:T(128)S(1)} %add.567), channel_id=1, source_target_pairs={{0,4},{1,5},{2,6},{3,7},{4,0},{5,1},{6,2},{7,3},{8,12},{9,13},{10,... | collective-permute-start | bytes 92 | tf_op jit(solution)/shard_map/ppermute | solution.py:76
  400.7 5.5 collective-permute-start.45
  406.2 6.3 %collective-permute-start.46 = (f32[7]{0:T(128)S(1)}, f32[7]{0:T(128)S(1)}, u32[]{:S(2)}, u32[]{:S(2)}) collective-permute-start(f32[7]{0:T(128)S(1)} %add.569), channel_id=1, source_target_pairs={{0,16},{1,17},{2,18},{3,19},{4,20},{5,21},{6,22},{7,23},{8,24},{9,... | collective-permute-start | bytes 92 | tf_op jit(solution)/shard_map/ppermute | solution.py:76
  412.5 9.4 %collective-permute-start.47 = (f32[7]{0:T(128)S(1)}, f32[7]{0:T(128)S(1)}, u32[]{:S(2)}, u32[]{:S(2)}) collective-permute-start(f32[7]{0:T(128)S(1)} %add.570), channel_id=1, source_target_pairs={{0,32},{1,33},{2,34},{3,35},{4,36},{5,37},{6,38},{7,39},{8,40},{9,... | collective-permute-start | bytes 92 | tf_op jit(solution)/shard_map/ppermute | solution.py:76
  437.8 16.4 %collective-permute-start.50 = (f32[8]{0:T(128)S(1)}, f32[8]{0:T(128)S(1)}, u32[]{:S(2)}, u32[]{:S(2)}) collective-permute-start(f32[8]{0:T(128)S(1)} %pad_maximum_fusion.8), channel_id=1, source_target_pairs={{0,1},{1,0},{2,3},{3,2},{4,5},{5,4},{6,7},{7,6},{8,9},{9,8},{10,11... | collective-permute-start | bytes 104 | tf_op jit(solution)/shard_map/ppermute | solution.py:76
  439.7 56.1 %collective-permute-start.57 = (f32[64,64]{1,0:T(8,128)S(1)}, f32[64,64]{1,0:T(8,128)S(1)}, u32[]{:S(2)}, u32[]{:S(2)}) collective-permute-start(f32[64,64]{1,0:T(8,128)S(1)} %get-tuple-element.72), channel_id=1, source_target_pairs={{1,0},{2,1},{3,2},{4,3},{5,4},{6,5},{7,6},{8,7},{9,8},{10,9},{11,1... | collective-permute-start | bytes 49160 | tf_op jit(solution)/shard_map/ppermute | solution.py:18
  452.2 43.5 %collective-permute-start.56 = (f32[64,64]{1,0:T(8,128)S(1)}, f32[64,64]{1,0:T(8,128)S(1)}, u32[]{:S(2)}, u32[]{:S(2)}) collective-permute-start(f32[64,64]{1,0:T(8,128)S(1)} %get-tuple-element.71), channel_id=1, source_target_pairs={{0,1},{1,2},{2,3},{3,4},{4,5},{5,6},{6,7},{7,8},{8,9},{9,10},{10,1... | collective-permute-start | bytes 49160 | tf_op jit(solution)/shard_map/ppermute | solution.py:17
  454.9 5.5 collective-permute-start.51
  460.3 7.0 %collective-permute-start.52 = (f32[8]{0:T(128)S(1)}, f32[8]{0:T(128)S(1)}, u32[]{:S(2)}, u32[]{:S(2)}) collective-permute-start(f32[8]{0:T(128)S(1)} %add.578), channel_id=1, source_target_pairs={{0,4},{1,5},{2,6},{3,7},{4,0},{5,1},{6,2},{7,3},{8,12},{9,13},{10,... | collective-permute-start | bytes 104 | tf_op jit(solution)/shard_map/ppermute | solution.py:76
  467.3 5.5 collective-permute-start.53
  472.8 6.3 %collective-permute-start.54 = (f32[8]{0:T(128)S(1)}, f32[8]{0:T(128)S(1)}, u32[]{:S(2)}, u32[]{:S(2)}) collective-permute-start(f32[8]{0:T(128)S(1)} %add.580), channel_id=1, source_target_pairs={{0,16},{1,17},{2,18},{3,19},{4,20},{5,21},{6,22},{7,23},{8,24},{9,... | collective-permute-start | bytes 104 | tf_op jit(solution)/shard_map/ppermute | solution.py:76
  479.1 9.4 %collective-permute-start.55 = (f32[8]{0:T(128)S(1)}, f32[8]{0:T(128)S(1)}, u32[]{:S(2)}, u32[]{:S(2)}) collective-permute-start(f32[8]{0:T(128)S(1)} %add.581), channel_id=1, source_target_pairs={{0,32},{1,33},{2,34},{3,35},{4,36},{5,37},{6,38},{7,39},{8,40},{9,... | collective-permute-start | bytes 104 | tf_op jit(solution)/shard_map/ppermute | solution.py:76
  508.2 5.5 collective-permute-start.59
  513.6 7.0 %collective-permute-start.60 = (f32[9]{0:T(128)S(1)}, f32[9]{0:T(128)S(1)}, u32[]{:S(2)}, u32[]{:S(2)}) collective-permute-start(f32[9]{0:T(128)S(1)} %add.589), channel_id=1, source_target_pairs={{0,4},{1,5},{2,6},{3,7},{4,0},{5,1},{6,2},{7,3},{8,12},{9,13},{10,... | collective-permute-start | bytes 116 | tf_op jit(solution)/shard_map/ppermute | solution.py:76
  520.6 5.5 collective-permute-start.61
  526.0 6.3 %collective-permute-start.62 = (f32[9]{0:T(128)S(1)}, f32[9]{0:T(128)S(1)}, u32[]{:S(2)}, u32[]{:S(2)}) collective-permute-start(f32[9]{0:T(128)S(1)} %add.591), channel_id=1, source_target_pairs={{0,16},{1,17},{2,18},{3,19},{4,20},{5,21},{6,22},{7,23},{8,24},{9,... | collective-permute-start | bytes 116 | tf_op jit(solution)/shard_map/ppermute | solution.py:76
  532.4 9.4 %collective-permute-start.63 = (f32[9]{0:T(128)S(1)}, f32[9]{0:T(128)S(1)}, u32[]{:S(2)}, u32[]{:S(2)}) collective-permute-start(f32[9]{0:T(128)S(1)} %add.592), channel_id=1, source_target_pairs={{0,32},{1,33},{2,34},{3,35},{4,36},{5,37},{6,38},{7,39},{8,40},{9,... | collective-permute-start | bytes 116 | tf_op jit(solution)/shard_map/ppermute | solution.py:76
  549.0 3.2 collective-permute-start.64
  553.5 5.4 collective-permute-start.65
  559.6 6.9 %collective-permute-start.66 = (f32[1]{0:T(128)}, f32[1]{0:T(128)}, u32[]{:S(2)}, u32[]{:S(2)}) collective-permute-start(f32[1]{0:T(128)} %add.597), channel_id=1, source_target_pairs={{0,4},{1,5},{2,6},{3,7},{4,0},{5,1},{6,2},{7,3},{8,12},{9,13},{10,... | collective-permute-start | bytes 20 | tf_op jit(solution)/shard_map/ppermute | solution.py:76
  567.2 5.4 collective-permute-start.67
  573.3 6.3 %collective-permute-start.68 = (f32[1]{0:T(128)}, f32[1]{0:T(128)}, u32[]{:S(2)}, u32[]{:S(2)}) collective-permute-start(f32[1]{0:T(128)} %add.599), channel_id=1, source_target_pairs={{0,16},{1,17},{2,18},{3,19},{4,20},{5,21},{6,22},{7,23},{8,24},{9,... | collective-permute-start | bytes 20 | tf_op jit(solution)/shard_map/ppermute | solution.py:76
  580.3 9.3 %collective-permute-start.69 = (f32[1]{0:T(128)}, f32[1]{0:T(128)}, u32[]{:S(2)}, u32[]{:S(2)}) collective-permute-start(f32[1]{0:T(128)} %add.600), channel_id=1, source_target_pairs={{0,32},{1,33},{2,34},{3,35},{4,36},{5,37},{6,38},{7,39},{8,40},{9,... | collective-permute-start | bytes 20 | tf_op jit(solution)/shard_map/ppermute | solution.py:76
  (18 other events, 536.8 us)

commit v6 on v5

--- a/solution.py
+++ b/solution.py
@@ -78,6 +78,17 @@
     return values
 
 
+def gather_harmonics(values, position):
+    count = lax.axis_size("harm")
+    stride = 1
+    while stride < count:
+        other = lax.ppermute(values, "harm", [(i, i ^ stride) for i in range(count)])
+        low = (position // stride) % 2 == 0
+        values = jnp.where(low, jnp.concatenate([values, other]), jnp.concatenate([other, values]))
+        stride *= 2
+    return values
+
+
 def per_device(rhs_field, neighbors, nu_mean, nu_ripple, mass_coeff, eddy_coeff):
     block, nodes_own = rhs_field.shape
     harmonics = nu_ripple.shape[0]
@@ -121,7 +132,7 @@
             + eddy_coeff[None, :] * factor[:, None] * swap_pairs(vector_in)
         )
 
-    rhs_field = lax.all_gather(rhs_field, "harm", axis=0, tiled=True)
+    rhs_field = gather_harmonics(rhs_field, harm_index)
     local_rows = lambda rows, other: jnp.sum(jnp.stack(rows) * other[None], axis=(1, 2))
     rhs_ext = extend(rhs_field)
     image = operate(rhs_ext)

time: 603 us -> 571 us (0.947)
  blocking collectives: 66.3 us -> 0 us
  starting transfers between devices: 197 us -> 223 us
  waiting for transfers between devices: 206 us -> 215 us
    all_gather x1 -> x0, blocking collectives: 66.3 us -> none  [per_device(): rhs_field = lax.all_gather(rhs_field, 'harm', axis=0, tiled=True)]
    ppermute x0 -> x3, starting transfers between devices: none -> 22.4 us  [gather_harmonics(): lax.ppermute(values, 'harm', [(i, i ^ stride) for i in range(count)])]
    ppermute x0 -> x3, waiting for transfers between devices: none -> 6.08 us  [gather_harmonics(): lax.ppermute(values, 'harm', [(i, i ^ stride) for i in range(count)])]
  transfers between devices with their start and end apart: 70 -> 73, of which waited for: 54 -> 56; matrix products, arithmetic and copies ran while one was open for 4% -> 5% of each run, Pallas kernels for 0% -> 0%
where the time goes in v6:
time: 571 us; the launch traced here: 563 us
  starting transfers between devices  223 us (39%)
  waiting for transfers between devices  215 us (38%)
  between operations  37.2 us (7%)
  matrix products  35 us (6%)
  other arithmetic  29.9 us (5%)
  local copies, waits for them, and re-layouts  23 us (4%)
    ppermute x54, waiting for transfers between devices, all_sum(): lax.ppermute(values, axis, [(i, i ^ stride) for i in range(count)])  198 us
    ppermute x54, starting transfers between devices, all_sum(): lax.ppermute(values, axis, [(i, i ^ stride) for i in range(count)])  129 us
    ppermute x8, starting transfers between devices, with_halo(): after = lax.ppermute(leading, axis, down)  55.3 us
    dot_general x42, matrix products, matmul_high(): jnp.dot(left, right, precision=lax.Precision.HIGHEST, preferred_element_t...  35 us
    ppermute x3, starting transfers between devices, gather_harmonics(): lax.ppermute(values, 'harm', [(i, i ^ stride) for i in range(count)])  22.4 us
    ppermute x8, starting transfers between devices, with_halo(): before = lax.ppermute(last, axis, up)  15.9 us
  transfers between devices with their start and end apart: 73, of which 56 were waited for; matrix products, arithmetic and copies ran while one was open for 5% of the time, Pallas kernels for 0%

profile of v6, /device:TPU:6, one launch (start us, length us, event | category | flops | bytes accessed | tf_op | source)
XLA Modules:
  0.0 562.8 jit_solution(4392263974458709273)
XLA Ops:
  1.3 15.7 %collective-permute-start = (f32[8,256]{1,0:T(8,128)S(1)}, f32[8,256]{1,0:T(8,128)S(1)}, u32[]{:S(2)}, u32[]{:S(2)}) collective-permute-start(f32[8,256]{1,0:T(8,128)S(1)} %copy-done.11), channel_id=1, source_target_pairs={{0,64},{64,0},{128,192},{192,128},{256,320},{320,256},{384,448},{4... | collective-permute-start | bytes 24584 | tf_op jit(solution)/shard_map/ppermute | solution.py:85
  24.4 4.0 collective-permute-start.2
  28.4 3.2 collective-permute-done.2
  31.8 8.4 %collective-permute-start.4 = (f32[64,64]{1,0:T(8,128)S(1)}, f32[64,64]{1,0:T(8,128)S(1)}, u32[]{:S(2)}, u32[]{:S(2)}) collective-permute-start(f32[64,64]{1,0:T(8,128)S(1)} %get-tuple-element.83), channel_id=1, source_target_pairs={{1,0},{2,1},{3,2},{4,3},{5,4},{6,5},{7,6},{8,7},{9,8},{10,9},{11,1... | collective-permute-start | bytes 49160 | tf_op jit(solution)/shard_map/ppermute | solution.py:18
  43.3 10.8 %collective-permute-done.3 = f32[64,64]{1,0:T(8,128)S(1)} collective-permute-done((f32[64,64]{1,0:T(8,128)S(1)}, f32[64,64]{1,0:T(8,128)S(1)}, u32[]{:S(2)}, u32[]{:S(2)}) %collective-permute-start.3) | collective-permute-done | bytes 16416 | tf_op jit(solution)/shard_map/ppermute | solution.py:17
  72.2 3.5 collective-permute-done.6
  79.0 5.0 collective-permute-done.7
  86.0 3.5 collective-permute-done.8
  91.4 4.4 collective-permute-done.9
  95.9 4.8 collective-permute-start.10
  100.7 4.6 collective-permute-done.10
  114.2 6.1 %collective-permute-start.20 = (f32[64,64]{1,0:T(8,128)S(1)}, f32[64,64]{1,0:T(8,128)S(1)}, u32[]{:S(2)}, u32[]{:S(2)}) collective-permute-start(f32[64,64]{1,0:T(8,128)S(1)} %get-tuple-element.79), channel_id=1, source_target_pairs={{1,0},{2,1},{3,2},{4,3},{5,4},{6,5},{7,6},{8,7},{9,8},{10,9},{11,1... | collective-permute-start | bytes 49160 | tf_op jit(solution)/shard_map/ppermute | solution.py:18
  128.7 3.5 collective-permute-done.14
  134.2 5.0 collective-permute-done.15
  141.1 3.5 collective-permute-done.16
  146.6 4.4 collective-permute-done.17
  151.0 5.1 collective-permute-start.18
  156.1 4.3 collective-permute-done.18
  169.9 6.6 %collective-permute-start.28 = (f32[64,64]{1,0:T(8,128)S(1)}, f32[64,64]{1,0:T(8,128)S(1)}, u32[]{:S(2)}, u32[]{:S(2)}) collective-permute-start(f32[64,64]{1,0:T(8,128)S(1)} %get-tuple-element.77), channel_id=1, source_target_pairs={{1,0},{2,1},{3,2},{4,3},{5,4},{6,5},{7,6},{8,7},{9,8},{10,9},{11,1... | collective-permute-start | bytes 49160 | tf_op jit(solution)/shard_map/ppermute | solution.py:18
  185.0 3.5 collective-permute-done.22
  190.5 5.0 collective-permute-done.23
  197.5 3.5 collective-permute-done.24
  202.9 4.4 collective-permute-done.25
  207.4 5.3 collective-permute-start.26
  212.7 4.0 collective-permute-done.26
  226.2 6.6 %collective-permute-start.36 = (f32[64,64]{1,0:T(8,128)S(1)}, f32[64,64]{1,0:T(8,128)S(1)}, u32[]{:S(2)}, u32[]{:S(2)}) collective-permute-start(f32[64,64]{1,0:T(8,128)S(1)} %get-tuple-element.75), channel_id=1, source_target_pairs={{1,0},{2,1},{3,2},{4,3},{5,4},{6,5},{7,6},{8,7},{9,8},{10,9},{11,1... | collective-permute-start | bytes 49160 | tf_op jit(solution)/shard_map/ppermute | solution.py:18
  241.3 3.5 collective-permute-done.30
  246.7 5.0 collective-permute-done.31
  253.7 3.5 collective-permute-done.32
  259.2 4.4 collective-permute-done.33
  263.6 5.1 collective-permute-start.34
  268.7 4.2 collective-permute-done.34
  283.1 6.6 %collective-permute-start.44 = (f32[64,64]{1,0:T(8,128)S(1)}, f32[64,64]{1,0:T(8,128)S(1)}, u32[]{:S(2)}, u32[]{:S(2)}) collective-permute-start(f32[64,64]{1,0:T(8,128)S(1)} %get-tuple-element.73), channel_id=1, source_target_pairs={{1,0},{2,1},{3,2},{4,3},{5,4},{6,5},{7,6},{8,7},{9,8},{10,9},{11,1... | collective-permute-start | bytes 49160 | tf_op jit(solution)/shard_map/ppermute | solution.py:18
  299.1 3.5 collective-permute-done.38
  304.5 5.0 collective-permute-done.39
  311.5 3.5 collective-permute-done.40
  316.9 4.4 collective-permute-done.41
  321.4 5.5 collective-permute-start.42
  326.9 3.9 collective-permute-done.42
  342.3 6.6 %collective-permute-start.52 = (f32[64,64]{1,0:T(8,128)S(1)}, f32[64,64]{1,0:T(8,128)S(1)}, u32[]{:S(2)}, u32[]{:S(2)}) collective-permute-start(f32[64,64]{1,0:T(8,128)S(1)} %get-tuple-element.71), channel_id=1, source_target_pairs={{1,0},{2,1},{3,2},{4,3},{5,4},{6,5},{7,6},{8,7},{9,8},{10,9},{11,1... | collective-permute-start | bytes 49160 | tf_op jit(solution)/shard_map/ppermute | solution.py:18
  358.9 3.5 collective-permute-done.46
  364.4 5.0 collective-permute-done.47
  371.3 3.5 collective-permute-done.48
  376.8 4.4 collective-permute-done.49
  381.2 5.1 collective-permute-start.50
  386.3 4.3 collective-permute-done.50
  408.4 12.5 %collective-permute-start.60 = (f32[64,64]{1,0:T(8,128)S(1)}, f32[64,64]{1,0:T(8,128)S(1)}, u32[]{:S(2)}, u32[]{:S(2)}) collective-permute-start(f32[64,64]{1,0:T(8,128)S(1)} %get-tuple-element.69), channel_id=1, source_target_pairs={{1,0},{2,1},{3,2},{4,3},{5,4},{6,5},{7,6},{8,7},{9,8},{10,9},{11,1... | collective-permute-start | bytes 49160 | tf_op jit(solution)/shard_map/ppermute | solution.py:18
  425.5 3.5 collective-permute-done.54
  430.9 5.0 collective-permute-done.55
  437.9 3.5 collective-permute-done.56
  443.3 4.4 collective-permute-done.57
  449.9 7.3 %collective-permute-done.58 = f32[8]{0:T(128)S(1)} collective-permute-done((f32[8]{0:T(128)S(1)}, f32[8]{0:T(128)S(1)}, u32[]{:S(2)}, u32[]{:S(2)}) %collective-permute-start.58) | collective-permute-done | bytes 64 | tf_op jit(solution)/shard_map/ppermute | solution.py:76
  478.8 3.5 collective-permute-done.62
  484.3 5.0 collective-permute-done.63
  491.2 3.5 collective-permute-done.64
  496.7 4.4 collective-permute-done.65
  503.0 7.4 %collective-permute-done.66 = f32[9]{0:T(128)S(1)} collective-permute-done((f32[9]{0:T(128)S(1)}, f32[9]{0:T(128)S(1)}, u32[]{:S(2)}, u32[]{:S(2)}) %collective-permute-start.66) | collective-permute-done | bytes 68 | tf_op jit(solution)/shard_map/ppermute | solution.py:76
  528.4 3.2 collective-permute-start.69
  531.6 3.9 collective-permute-done.69
  536.0 3.2 collective-permute-start.70
  542.1 3.2 collective-permute-start.71
  545.3 3.3 collective-permute-done.71
  549.1 3.2 collective-permute-start.72
  552.4 6.3 %collective-permute-done.72 = f32[1]{0:T(128)} collective-permute-done((f32[1]{0:T(128)}, f32[1]{0:T(128)}, u32[]{:S(2)}, u32[]{:S(2)}) %collective-permute-start.72) | collective-permute-done | bytes 36 | tf_op jit(solution)/shard_map/ppermute | solution.py:76
  (342 shorter events, 209.1 us)
Async XLA Ops:
  1.3 17.4 %collective-permute-start = (f32[8,256]{1,0:T(8,128)S(1)}, f32[8,256]{1,0:T(8,128)S(1)}, u32[]{:S(2)}, u32[]{:S(2)}) collective-permute-start(f32[8,256]{1,0:T(8,128)S(1)} %copy-done.11), channel_id=1, source_target_pairs={{0,64},{64,0},{128,192},{192,128},{256,320},{320,256},{384,448},{4... | collective-permute-start | bytes 24584 | tf_op jit(solution)/shard_map/ppermute | solution.py:85
  18.8 5.6 %collective-permute-start.1 = (f32[16,256]{1,0:T(8,128)S(1)}, f32[16,256]{1,0:T(8,128)S(1)}, u32[]{:S(2)}, u32[]{:S(2)}) collective-permute-start(f32[16,256]{1,0:T(8,128)S(1)} %maximum_select_fusion.3), channel_id=1, source_target_pairs={{0,128},{64,192},{128,0},{192,64},{256,384},{320,448},{384,256},{4... | collective-permute-start | bytes 49160 | tf_op jit(solution)/shard_map/ppermute | solution.py:85
  24.4 7.3 %collective-permute-start.2 = (f32[32,256]{1,0:T(8,128)S(1)}, f32[32,256]{1,0:T(8,128)S(1)}, u32[]{:S(2)}, u32[]{:S(2)}) collective-permute-start(f32[32,256]{1,0:T(8,128)S(1)} %maximum_select_fusion.2), channel_id=1, source_target_pairs={{0,256},{64,320},{128,384},{192,448},{256,0},{320,64},{384,128},{4... | collective-permute-start | bytes 98312 | tf_op jit(solution)/shard_map/ppermute | solution.py:85
  31.8 11.6 %collective-permute-start.4 = (f32[64,64]{1,0:T(8,128)S(1)}, f32[64,64]{1,0:T(8,128)S(1)}, u32[]{:S(2)}, u32[]{:S(2)}) collective-permute-start(f32[64,64]{1,0:T(8,128)S(1)} %get-tuple-element.83), channel_id=1, source_target_pairs={{1,0},{2,1},{3,2},{4,3},{5,4},{6,5},{7,6},{8,7},{9,8},{10,9},{11,1... | collective-permute-start | bytes 49160 | tf_op jit(solution)/shard_map/ppermute | solution.py:18
  40.2 13.9 %collective-permute-start.3 = (f32[64,64]{1,0:T(8,128)S(1)}, f32[64,64]{1,0:T(8,128)S(1)}, u32[]{:S(2)}, u32[]{:S(2)}) collective-permute-start(f32[64,64]{1,0:T(8,128)S(1)} %get-tuple-element.82), channel_id=1, source_target_pairs={{0,1},{1,2},{2,3},{3,4},{4,5},{5,6},{6,7},{7,8},{8,9},{9,10},{10,1... | collective-permute-start | bytes 49160 | tf_op jit(solution)/shard_map/ppermute | solution.py:17
  59.4 47.7 %collective-permute-start.12 = (f32[64,64]{1,0:T(8,128)S(1)}, f32[64,64]{1,0:T(8,128)S(1)}, u32[]{:S(2)}, u32[]{:S(2)}) collective-permute-start(f32[64,64]{1,0:T(8,128)S(1)} %get-tuple-element.81), channel_id=1, source_target_pairs={{1,0},{2,1},{3,2},{4,3},{5,4},{6,5},{7,6},{8,7},{9,8},{10,9},{11,1... | collective-permute-start | bytes 49160 | tf_op jit(solution)/shard_map/ppermute | solution.py:18
  61.4 45.8 %collective-permute-start.11 = (f32[64,64]{1,0:T(8,128)S(1)}, f32[64,64]{1,0:T(8,128)S(1)}, u32[]{:S(2)}, u32[]{:S(2)}) collective-permute-start(f32[64,64]{1,0:T(8,128)S(1)} %get-tuple-element.80), channel_id=1, source_target_pairs={{0,1},{1,2},{2,3},{3,4},{4,5},{5,6},{6,7},{7,8},{8,9},{9,10},{10,1... | collective-permute-start | bytes 49160 | tf_op jit(solution)/shard_map/ppermute | solution.py:17
  70.3 5.5 collective-permute-start.6
  77.1 7.0 %collective-permute-start.7 = (f32[2]{0:T(128)S(1)}, f32[2]{0:T(128)S(1)}, u32[]{:S(2)}, u32[]{:S(2)}) collective-permute-start(f32[2]{0:T(128)S(1)} %fusion.422), channel_id=1, source_target_pairs={{0,4},{1,5},{2,6},{3,7},{4,0},{5,1},{6,2},{7,3},{8,12},{9,13},{10,... | collective-permute-start | bytes 32 | tf_op jit(solution)/shard_map/ppermute | solution.py:76
  84.1 5.5 collective-permute-start.8
  89.5 6.3 %collective-permute-start.9 = (f32[2]{0:T(128)S(1)}, f32[2]{0:T(128)S(1)}, u32[]{:S(2)}, u32[]{:S(2)}) collective-permute-start(f32[2]{0:T(128)S(1)} %add.552), channel_id=1, source_target_pairs={{0,16},{1,17},{2,18},{3,19},{4,20},{5,21},{6,22},{7,23},{8,24},{9,... | collective-permute-start | bytes 32 | tf_op jit(solution)/shard_map/ppermute | solution.py:76
  95.9 9.4 %collective-permute-start.10 = (f32[2]{0:T(128)S(1)}, f32[2]{0:T(128)S(1)}, u32[]{:S(2)}, u32[]{:S(2)}) collective-permute-start(f32[2]{0:T(128)S(1)} %add.553), channel_id=1, source_target_pairs={{0,32},{1,33},{2,34},{3,35},{4,36},{5,37},{6,38},{7,39},{8,40},{9,... | collective-permute-start | bytes 32 | tf_op jit(solution)/shard_map/ppermute | solution.py:76
  114.2 49.6 %collective-permute-start.20 = (f32[64,64]{1,0:T(8,128)S(1)}, f32[64,64]{1,0:T(8,128)S(1)}, u32[]{:S(2)}, u32[]{:S(2)}) collective-permute-start(f32[64,64]{1,0:T(8,128)S(1)} %get-tuple-element.79), channel_id=1, source_target_pairs={{1,0},{2,1},{3,2},{4,3},{5,4},{6,5},{7,6},{8,7},{9,8},{10,9},{11,1... | collective-permute-start | bytes 49160 | tf_op jit(solution)/shard_map/ppermute | solution.py:18
  120.3 43.5 %collective-permute-start.19 = (f32[64,64]{1,0:T(8,128)S(1)}, f32[64,64]{1,0:T(8,128)S(1)}, u32[]{:S(2)}, u32[]{:S(2)}) collective-permute-start(f32[64,64]{1,0:T(8,128)S(1)} %get-tuple-element.78), channel_id=1, source_target_pairs={{0,1},{1,2},{2,3},{3,4},{4,5},{5,6},{6,7},{7,8},{8,9},{9,10},{10,1... | collective-permute-start | bytes 49160 | tf_op jit(solution)/shard_map/ppermute | solution.py:17
  126.8 5.5 collective-permute-start.14
  132.3 7.0 %collective-permute-start.15 = (f32[3]{0:T(128)S(1)}, f32[3]{0:T(128)S(1)}, u32[]{:S(2)}, u32[]{:S(2)}) collective-permute-start(f32[3]{0:T(128)S(1)} %add.563), channel_id=1, source_target_pairs={{0,4},{1,5},{2,6},{3,7},{4,0},{5,1},{6,2},{7,3},{8,12},{9,13},{10,... | collective-permute-start | bytes 44 | tf_op jit(solution)/shard_map/ppermute | solution.py:76
  139.2 5.5 collective-permute-start.16
  144.7 6.3 %collective-permute-start.17 = (f32[3]{0:T(128)S(1)}, f32[3]{0:T(128)S(1)}, u32[]{:S(2)}, u32[]{:S(2)}) collective-permute-start(f32[3]{0:T(128)S(1)} %add.565), channel_id=1, source_target_pairs={{0,16},{1,17},{2,18},{3,19},{4,20},{5,21},{6,22},{7,23},{8,24},{9,... | collective-permute-start | bytes 44 | tf_op jit(solution)/shard_map/ppermute | solution.py:76
  151.0 9.4 %collective-permute-start.18 = (f32[3]{0:T(128)S(1)}, f32[3]{0:T(128)S(1)}, u32[]{:S(2)}, u32[]{:S(2)}) collective-permute-start(f32[3]{0:T(128)S(1)} %add.566), channel_id=1, source_target_pairs={{0,32},{1,33},{2,34},{3,35},{4,36},{5,37},{6,38},{7,39},{8,40},{9,... | collective-permute-start | bytes 44 | tf_op jit(solution)/shard_map/ppermute | solution.py:76
  169.9 50.2 %collective-permute-start.28 = (f32[64,64]{1,0:T(8,128)S(1)}, f32[64,64]{1,0:T(8,128)S(1)}, u32[]{:S(2)}, u32[]{:S(2)}) collective-permute-start(f32[64,64]{1,0:T(8,128)S(1)} %get-tuple-element.77), channel_id=1, source_target_pairs={{1,0},{2,1},{3,2},{4,3},{5,4},{6,5},{7,6},{8,7},{9,8},{10,9},{11,1... | collective-permute-start | bytes 49160 | tf_op jit(solution)/shard_map/ppermute | solution.py:18
  176.5 43.6 %collective-permute-start.27 = (f32[64,64]{1,0:T(8,128)S(1)}, f32[64,64]{1,0:T(8,128)S(1)}, u32[]{:S(2)}, u32[]{:S(2)}) collective-permute-start(f32[64,64]{1,0:T(8,128)S(1)} %get-tuple-element.76), channel_id=1, source_target_pairs={{0,1},{1,2},{2,3},{3,4},{4,5},{5,6},{6,7},{7,8},{8,9},{9,10},{10,1... | collective-permute-start | bytes 49160 | tf_op jit(solution)/shard_map/ppermute | solution.py:17
  183.1 5.5 collective-permute-start.22
  188.6 7.0 %collective-permute-start.23 = (f32[4]{0:T(128)S(1)}, f32[4]{0:T(128)S(1)}, u32[]{:S(2)}, u32[]{:S(2)}) collective-permute-start(f32[4]{0:T(128)S(1)} %add.574), channel_id=1, source_target_pairs={{0,4},{1,5},{2,6},{3,7},{4,0},{5,1},{6,2},{7,3},{8,12},{9,13},{10,... | collective-permute-start | bytes 56 | tf_op jit(solution)/shard_map/ppermute | solution.py:76
  195.5 5.5 collective-permute-start.24
  201.0 6.3 %collective-permute-start.25 = (f32[4]{0:T(128)S(1)}, f32[4]{0:T(128)S(1)}, u32[]{:S(2)}, u32[]{:S(2)}) collective-permute-start(f32[4]{0:T(128)S(1)} %add.576), channel_id=1, source_target_pairs={{0,16},{1,17},{2,18},{3,19},{4,20},{5,21},{6,22},{7,23},{8,24},{9,... | collective-permute-start | bytes 56 | tf_op jit(solution)/shard_map/ppermute | solution.py:76
  207.4 9.4 %collective-permute-start.26 = (f32[4]{0:T(128)S(1)}, f32[4]{0:T(128)S(1)}, u32[]{:S(2)}, u32[]{:S(2)}) collective-permute-start(f32[4]{0:T(128)S(1)} %add.577), channel_id=1, source_target_pairs={{0,32},{1,33},{2,34},{3,35},{4,36},{5,37},{6,38},{7,39},{8,40},{9,... | collective-permute-start | bytes 56 | tf_op jit(solution)/shard_map/ppermute | solution.py:76
  226.2 50.9 %collective-permute-start.36 = (f32[64,64]{1,0:T(8,128)S(1)}, f32[64,64]{1,0:T(8,128)S(1)}, u32[]{:S(2)}, u32[]{:S(2)}) collective-permute-start(f32[64,64]{1,0:T(8,128)S(1)} %get-tuple-element.75), channel_id=1, source_target_pairs={{1,0},{2,1},{3,2},{4,3},{5,4},{6,5},{7,6},{8,7},{9,8},{10,9},{11,1... | collective-permute-start | bytes 49160 | tf_op jit(solution)/shard_map/ppermute | solution.py:18
  232.7 44.3 %collective-permute-start.35 = (f32[64,64]{1,0:T(8,128)S(1)}, f32[64,64]{1,0:T(8,128)S(1)}, u32[]{:S(2)}, u32[]{:S(2)}) collective-permute-start(f32[64,64]{1,0:T(8,128)S(1)} %get-tuple-element.74), channel_id=1, source_target_pairs={{0,1},{1,2},{2,3},{3,4},{4,5},{5,6},{6,7},{7,8},{8,9},{9,10},{10,1... | collective-permute-start | bytes 49160 | tf_op jit(solution)/shard_map/ppermute | solution.py:17
  239.4 5.5 collective-permute-start.30
  244.8 7.0 %collective-permute-start.31 = (f32[5]{0:T(128)S(1)}, f32[5]{0:T(128)S(1)}, u32[]{:S(2)}, u32[]{:S(2)}) collective-permute-start(f32[5]{0:T(128)S(1)} %add.585), channel_id=1, source_target_pairs={{0,4},{1,5},{2,6},{3,7},{4,0},{5,1},{6,2},{7,3},{8,12},{9,13},{10,... | collective-permute-start | bytes 68 | tf_op jit(solution)/shard_map/ppermute | solution.py:76
  251.8 5.5 collective-permute-start.32
  257.2 6.3 %collective-permute-start.33 = (f32[5]{0:T(128)S(1)}, f32[5]{0:T(128)S(1)}, u32[]{:S(2)}, u32[]{:S(2)}) collective-permute-start(f32[5]{0:T(128)S(1)} %add.587), channel_id=1, source_target_pairs={{0,16},{1,17},{2,18},{3,19},{4,20},{5,21},{6,22},{7,23},{8,24},{9,... | collective-permute-start | bytes 68 | tf_op jit(solution)/shard_map/ppermute | solution.py:76
  263.6 9.4 %collective-permute-start.34 = (f32[5]{0:T(128)S(1)}, f32[5]{0:T(128)S(1)}, u32[]{:S(2)}, u32[]{:S(2)}) collective-permute-start(f32[5]{0:T(128)S(1)} %add.588), channel_id=1, source_target_pairs={{0,32},{1,33},{2,34},{3,35},{4,36},{5,37},{6,38},{7,39},{8,40},{9,... | collective-permute-start | bytes 68 | tf_op jit(solution)/shard_map/ppermute | solution.py:76
  283.1 53.1 %collective-permute-start.44 = (f32[64,64]{1,0:T(8,128)S(1)}, f32[64,64]{1,0:T(8,128)S(1)}, u32[]{:S(2)}, u32[]{:S(2)}) collective-permute-start(f32[64,64]{1,0:T(8,128)S(1)} %get-tuple-element.73), channel_id=1, source_target_pairs={{1,0},{2,1},{3,2},{4,3},{5,4},{6,5},{7,6},{8,7},{9,8},{10,9},{11,1... | collective-permute-start | bytes 49160 | tf_op jit(solution)/shard_map/ppermute | solution.py:18
  289.7 46.5 %collective-permute-start.43 = (f32[64,64]{1,0:T(8,128)S(1)}, f32[64,64]{1,0:T(8,128)S(1)}, u32[]{:S(2)}, u32[]{:S(2)}) collective-permute-start(f32[64,64]{1,0:T(8,128)S(1)} %get-tuple-element.72), channel_id=1, source_target_pairs={{0,1},{1,2},{2,3},{3,4},{4,5},{5,6},{6,7},{7,8},{8,9},{9,10},{10,1... | collective-permute-start | bytes 49160 | tf_op jit(solution)/shard_map/ppermute | solution.py:17
  297.1 5.5 collective-permute-start.38
  302.6 7.0 %collective-permute-start.39 = (f32[6]{0:T(128)S(1)}, f32[6]{0:T(128)S(1)}, u32[]{:S(2)}, u32[]{:S(2)}) collective-permute-start(f32[6]{0:T(128)S(1)} %add.596), channel_id=1, source_target_pairs={{0,4},{1,5},{2,6},{3,7},{4,0},{5,1},{6,2},{7,3},{8,12},{9,13},{10,... | collective-permute-start | bytes 80 | tf_op jit(solution)/shard_map/ppermute | solution.py:76
  309.6 5.5 collective-permute-start.40
  315.0 6.3 %collective-permute-start.41 = (f32[6]{0:T(128)S(1)}, f32[6]{0:T(128)S(1)}, u32[]{:S(2)}, u32[]{:S(2)}) collective-permute-start(f32[6]{0:T(128)S(1)} %add.598), channel_id=1, source_target_pairs={{0,16},{1,17},{2,18},{3,19},{4,20},{5,21},{6,22},{7,23},{8,24},{9,... | collective-permute-start | bytes 80 | tf_op jit(solution)/shard_map/ppermute | solution.py:76
  321.4 9.4 %collective-permute-start.42 = (f32[6]{0:T(128)S(1)}, f32[6]{0:T(128)S(1)}, u32[]{:S(2)}, u32[]{:S(2)}) collective-permute-start(f32[6]{0:T(128)S(1)} %add.599), channel_id=1, source_target_pairs={{0,32},{1,33},{2,34},{3,35},{4,36},{5,37},{6,38},{7,39},{8,40},{9,... | collective-permute-start | bytes 80 | tf_op jit(solution)/shard_map/ppermute | solution.py:76
  342.3 53.5 %collective-permute-start.52 = (f32[64,64]{1,0:T(8,128)S(1)}, f32[64,64]{1,0:T(8,128)S(1)}, u32[]{:S(2)}, u32[]{:S(2)}) collective-permute-start(f32[64,64]{1,0:T(8,128)S(1)} %get-tuple-element.71), channel_id=1, source_target_pairs={{1,0},{2,1},{3,2},{4,3},{5,4},{6,5},{7,6},{8,7},{9,8},{10,9},{11,1... | collective-permute-start | bytes 49160 | tf_op jit(solution)/shard_map/ppermute | solution.py:18
  348.9 46.9 %collective-permute-start.51 = (f32[64,64]{1,0:T(8,128)S(1)}, f32[64,64]{1,0:T(8,128)S(1)}, u32[]{:S(2)}, u32[]{:S(2)}) collective-permute-start(f32[64,64]{1,0:T(8,128)S(1)} %get-tuple-element.70), channel_id=1, source_target_pairs={{0,1},{1,2},{2,3},{3,4},{4,5},{5,6},{6,7},{7,8},{8,9},{9,10},{10,1... | collective-permute-start | bytes 49160 | tf_op jit(solution)/shard_map/ppermute | solution.py:17
  357.0 5.5 collective-permute-start.46
  362.5 7.0 %collective-permute-start.47 = (f32[7]{0:T(128)S(1)}, f32[7]{0:T(128)S(1)}, u32[]{:S(2)}, u32[]{:S(2)}) collective-permute-start(f32[7]{0:T(128)S(1)} %add.607), channel_id=1, source_target_pairs={{0,4},{1,5},{2,6},{3,7},{4,0},{5,1},{6,2},{7,3},{8,12},{9,13},{10,... | collective-permute-start | bytes 92 | tf_op jit(solution)/shard_map/ppermute | solution.py:76
  369.4 5.5 collective-permute-start.48
  374.9 6.3 %collective-permute-start.49 = (f32[7]{0:T(128)S(1)}, f32[7]{0:T(128)S(1)}, u32[]{:S(2)}, u32[]{:S(2)}) collective-permute-start(f32[7]{0:T(128)S(1)} %add.609), channel_id=1, source_target_pairs={{0,16},{1,17},{2,18},{3,19},{4,20},{5,21},{6,22},{7,23},{8,24},{9,... | collective-permute-start | bytes 92 | tf_op jit(solution)/shard_map/ppermute | solution.py:76
  381.2 9.4 %collective-permute-start.50 = (f32[7]{0:T(128)S(1)}, f32[7]{0:T(128)S(1)}, u32[]{:S(2)}, u32[]{:S(2)}) collective-permute-start(f32[7]{0:T(128)S(1)} %add.610), channel_id=1, source_target_pairs={{0,32},{1,33},{2,34},{3,35},{4,36},{5,37},{6,38},{7,39},{8,40},{9,... | collective-permute-start | bytes 92 | tf_op jit(solution)/shard_map/ppermute | solution.py:76
  406.4 16.4 %collective-permute-start.53 = (f32[8]{0:T(128)S(1)}, f32[8]{0:T(128)S(1)}, u32[]{:S(2)}, u32[]{:S(2)}) collective-permute-start(f32[8]{0:T(128)S(1)} %pad_maximum_fusion.8), channel_id=1, source_target_pairs={{0,1},{1,0},{2,3},{3,2},{4,5},{5,4},{6,7},{7,6},{8,9},{9,8},{10,11... | collective-permute-start | bytes 104 | tf_op jit(solution)/shard_map/ppermute | solution.py:76
  408.4 56.1 %collective-permute-start.60 = (f32[64,64]{1,0:T(8,128)S(1)}, f32[64,64]{1,0:T(8,128)S(1)}, u32[]{:S(2)}, u32[]{:S(2)}) collective-permute-start(f32[64,64]{1,0:T(8,128)S(1)} %get-tuple-element.69), channel_id=1, source_target_pairs={{1,0},{2,1},{3,2},{4,3},{5,4},{6,5},{7,6},{8,7},{9,8},{10,9},{11,1... | collective-permute-start | bytes 49160 | tf_op jit(solution)/shard_map/ppermute | solution.py:18
  420.9 43.6 %collective-permute-start.59 = (f32[64,64]{1,0:T(8,128)S(1)}, f32[64,64]{1,0:T(8,128)S(1)}, u32[]{:S(2)}, u32[]{:S(2)}) collective-permute-start(f32[64,64]{1,0:T(8,128)S(1)} %get-tuple-element.68), channel_id=1, source_target_pairs={{0,1},{1,2},{2,3},{3,4},{4,5},{5,6},{6,7},{7,8},{8,9},{9,10},{10,1... | collective-permute-start | bytes 49160 | tf_op jit(solution)/shard_map/ppermute | solution.py:17
  423.5 5.5 collective-permute-start.54
  429.0 7.0 %collective-permute-start.55 = (f32[8]{0:T(128)S(1)}, f32[8]{0:T(128)S(1)}, u32[]{:S(2)}, u32[]{:S(2)}) collective-permute-start(f32[8]{0:T(128)S(1)} %add.618), channel_id=1, source_target_pairs={{0,4},{1,5},{2,6},{3,7},{4,0},{5,1},{6,2},{7,3},{8,12},{9,13},{10,... | collective-permute-start | bytes 104 | tf_op jit(solution)/shard_map/ppermute | solution.py:76
  441.4 6.3 %collective-permute-start.57 = (f32[8]{0:T(128)S(1)}, f32[8]{0:T(128)S(1)}, u32[]{:S(2)}, u32[]{:S(2)}) collective-permute-start(f32[8]{0:T(128)S(1)} %add.620), channel_id=1, source_target_pairs={{0,16},{1,17},{2,18},{3,19},{4,20},{5,21},{6,22},{7,23},{8,24},{9,... | collective-permute-start | bytes 104 | tf_op jit(solution)/shard_map/ppermute | solution.py:76
  447.8 9.4 %collective-permute-start.58 = (f32[8]{0:T(128)S(1)}, f32[8]{0:T(128)S(1)}, u32[]{:S(2)}, u32[]{:S(2)}) collective-permute-start(f32[8]{0:T(128)S(1)} %add.621), channel_id=1, source_target_pairs={{0,32},{1,33},{2,34},{3,35},{4,36},{5,37},{6,38},{7,39},{8,40},{9,... | collective-permute-start | bytes 104 | tf_op jit(solution)/shard_map/ppermute | solution.py:76
  476.9 5.5 collective-permute-start.62
  482.3 7.0 %collective-permute-start.63 = (f32[9]{0:T(128)S(1)}, f32[9]{0:T(128)S(1)}, u32[]{:S(2)}, u32[]{:S(2)}) collective-permute-start(f32[9]{0:T(128)S(1)} %add.629), channel_id=1, source_target_pairs={{0,4},{1,5},{2,6},{3,7},{4,0},{5,1},{6,2},{7,3},{8,12},{9,13},{10,... | collective-permute-start | bytes 116 | tf_op jit(solution)/shard_map/ppermute | solution.py:76
  489.3 5.5 collective-permute-start.64
  494.8 6.3 %collective-permute-start.65 = (f32[9]{0:T(128)S(1)}, f32[9]{0:T(128)S(1)}, u32[]{:S(2)}, u32[]{:S(2)}) collective-permute-start(f32[9]{0:T(128)S(1)} %add.631), channel_id=1, source_target_pairs={{0,16},{1,17},{2,18},{3,19},{4,20},{5,21},{6,22},{7,23},{8,24},{9,... | collective-permute-start | bytes 116 | tf_op jit(solution)/shard_map/ppermute | solution.py:76
  501.1 9.4 %collective-permute-start.66 = (f32[9]{0:T(128)S(1)}, f32[9]{0:T(128)S(1)}, u32[]{:S(2)}, u32[]{:S(2)}) collective-permute-start(f32[9]{0:T(128)S(1)} %add.632), channel_id=1, source_target_pairs={{0,32},{1,33},{2,34},{3,35},{4,36},{5,37},{6,38},{7,39},{8,40},{9,... | collective-permute-start | bytes 116 | tf_op jit(solution)/shard_map/ppermute | solution.py:76
  522.3 5.6 collective-permute-start.68
  528.4 7.1 %collective-permute-start.69 = (f32[1]{0:T(128)}, f32[1]{0:T(128)}, u32[]{:S(2)}, u32[]{:S(2)}) collective-permute-start(f32[1]{0:T(128)} %add.637), channel_id=1, source_target_pairs={{0,4},{1,5},{2,6},{3,7},{4,0},{5,1},{6,2},{7,3},{8,12},{9,13},{10,... | collective-permute-start | bytes 20 | tf_op jit(solution)/shard_map/ppermute | solution.py:76
  536.0 5.6 collective-permute-start.70
  542.1 6.5 %collective-permute-start.71 = (f32[1]{0:T(128)}, f32[1]{0:T(128)}, u32[]{:S(2)}, u32[]{:S(2)}) collective-permute-start(f32[1]{0:T(128)} %add.639), channel_id=1, source_target_pairs={{0,16},{1,17},{2,18},{3,19},{4,20},{5,21},{6,22},{7,23},{8,24},{9,... | collective-permute-start | bytes 20 | tf_op jit(solution)/shard_map/ppermute | solution.py:76
  549.1 9.5 %collective-permute-start.72 = (f32[1]{0:T(128)}, f32[1]{0:T(128)}, u32[]{:S(2)}, u32[]{:S(2)}) collective-permute-start(f32[1]{0:T(128)} %add.640), channel_id=1, source_target_pairs={{0,32},{1,33},{2,34},{3,35},{4,36},{5,37},{6,38},{7,39},{8,40},{9,... | collective-permute-start | bytes 20 | tf_op jit(solution)/shard_map/ppermute | solution.py:76
  (21 other events, 440.7 us)

commit v7 on v6

--- a/solution.py
+++ b/solution.py
@@ -71,10 +71,10 @@
         if count & (count - 1):
             values = lax.psum(values, axis)
             continue
-        stride = 1
-        while stride < count:
+        stride = count // 2
+        while stride >= 1:
             values = values + lax.ppermute(values, axis, [(i, i ^ stride) for i in range(count)])
-            stride *= 2
+            stride //= 2
     return values
 
 
@@ -145,29 +145,29 @@
     columns = [[sums[1] / beta_norm / beta_norm]]
     ortho_ext = image_ext / beta_norm - columns[0][0] * krylov_ext[0]
     for j in range(1, ITERS):
-        ortho = inner(ortho_ext)
-        image = operate(ortho_ext)
-        last = j + 1 == ITERS
-        if not last:
-            image_ext = extend(image)
-        sums = all_sum(
-            jnp.concatenate([local_rows([ortho], ortho), local_rows(krylov + [ortho], image)])
-        )
-        length = jnp.sqrt(sums[0])
-        columns[j - 1].append(length)
-        krylov_ext.append(ortho_ext / length)
-        krylov.append(inner(krylov_ext[j]))
-        images.append(image / length)
-        projected = [sums[1 + i] / length for i in range(j)] + [sums[1 + j] / length / length]
-        columns.append(projected)
-        if last:
-            ortho = images[j]
-            for i in range(j + 1):
-                ortho = ortho - projected[i] * krylov[i]
-        else:
-            ortho_ext = image_ext / length
-            for i in range(j + 1):
-                ortho_ext = ortho_ext - projected[i] * krylov_ext[i]
+      ortho = inner(ortho_ext)
+      image = operate(ortho_ext)
+      last = j + 1 == ITERS
+      if not last:
+          image_ext = extend(image)
+      sums = all_sum(
+          jnp.concatenate([local_rows([ortho], ortho), local_rows(krylov + [ortho], image)])
+      )
+      length = jnp.sqrt(sums[0])
+      columns[j - 1].append(length)
+      krylov_ext.append(ortho_ext / length)
+      krylov.append(inner(krylov_ext[j]))
+      images.append(image / length)
+      projected = [sums[1 + i] / length for i in range(j)] + [sums[1 + j] / length / length]
+      columns.append(projected)
+      if last:
+          ortho = images[j]
+          for i in range(j + 1):
+              ortho = ortho - projected[i] * krylov[i]
+      else:
+          ortho_ext = image_ext / length
+          for i in range(j + 1):
+              ortho_ext = ortho_ext - projected[i] * krylov_ext[i]
     columns[ITERS - 1].append(jnp.sqrt(all_sum(jnp.sum(ortho * ortho)[None])[0]))
     coeffs = least_squares(columns, beta_norm)
     correction = coeffs[0] * krylov[0]

time: 571 us -> 560 us (0.981)
  starting transfers between devices: 223 us -> 204 us
  waiting for transfers between devices: 215 us -> 222 us
    ppermute x54, starting transfers between devices: 129 us -> 116 us  [all_sum(): lax.ppermute(values, axis, [(i, i ^ stride) for i in range(count)])]
    ppermute x54, waiting for transfers between devices: 198 us -> 205 us  [all_sum(): lax.ppermute(values, axis, [(i, i ^ stride) for i in range(count)])]
    ppermute x8, starting transfers between devices: 55.3 us -> 49.4 us  [with_halo(): after = lax.ppermute(leading, axis, down)]
where the time goes in v7:
time: 560 us; the launch traced here: 551 us
  waiting for transfers between devices  222 us (40%)
  starting transfers between devices  204 us (36%)
  between operations  37.2 us (7%)
  matrix products  35 us (6%)
  other arithmetic  29.9 us (5%)
  local copies, waits for them, and re-layouts  23 us (4%)
    ppermute x54, waiting for transfers between devices, all_sum(): lax.ppermute(values, axis, [(i, i ^ stride) for i in range(count)])  205 us
    ppermute x54, starting transfers between devices, all_sum(): lax.ppermute(values, axis, [(i, i ^ stride) for i in range(count)])  116 us
    ppermute x8, starting transfers between devices, with_halo(): after = lax.ppermute(leading, axis, down)  49.4 us
    dot_general x42, matrix products, matmul_high(): jnp.dot(left, right, precision=lax.Precision.HIGHEST, preferred_element_t...  35 us
    ppermute x3, starting transfers between devices, gather_harmonics(): lax.ppermute(values, 'harm', [(i, i ^ stride) for i in range(count)])  22.4 us
    ppermute x8, starting transfers between devices, with_halo(): before = lax.ppermute(last, axis, up)  15.9 us
  transfers between devices with their start and end apart: 73, of which 56 were waited for; matrix products, arithmetic and copies ran while one was open for 5% of the time, Pallas kernels for 0%

profile of v7, /device:TPU:6, one launch (start us, length us, event | category | flops | bytes accessed | tf_op | source)
XLA Modules:
  0.0 550.6 jit_solution(4585042057354794335)
XLA Ops:
  1.3 15.7 %collective-permute-start = (f32[8,256]{1,0:T(8,128)S(1)}, f32[8,256]{1,0:T(8,128)S(1)}, u32[]{:S(2)}, u32[]{:S(2)}) collective-permute-start(f32[8,256]{1,0:T(8,128)S(1)} %copy-done.11), channel_id=1, source_target_pairs={{0,64},{64,0},{128,192},{192,128},{256,320},{320,256},{384,448},{4... | collective-permute-start | bytes 24584 | tf_op jit(solution)/shard_map/ppermute | solution.py:85
  18.8 2.7 collective-permute-start.1
  21.6 2.8 collective-permute-done.1
  24.4 4.0 collective-permute-start.2
  28.4 3.2 collective-permute-done.2
  31.8 8.4 %collective-permute-start.4 = (f32[64,64]{1,0:T(8,128)S(1)}, f32[64,64]{1,0:T(8,128)S(1)}, u32[]{:S(2)}, u32[]{:S(2)}) collective-permute-start(f32[64,64]{1,0:T(8,128)S(1)} %get-tuple-element.83), channel_id=1, source_target_pairs={{1,0},{2,1},{3,2},{4,3},{5,4},{6,5},{7,6},{8,7},{9,8},{10,9},{11,1... | collective-permute-start | bytes 49160 | tf_op jit(solution)/shard_map/ppermute | solution.py:18
  43.3 10.8 %collective-permute-done.3 = f32[64,64]{1,0:T(8,128)S(1)} collective-permute-done((f32[64,64]{1,0:T(8,128)S(1)}, f32[64,64]{1,0:T(8,128)S(1)}, u32[]{:S(2)}, u32[]{:S(2)}) %collective-permute-start.3) | collective-permute-done | bytes 16416 | tf_op jit(solution)/shard_map/ppermute | solution.py:17
  61.4 2.4 collective-permute-start.11
  67.8 7.4 %collective-permute-done.5 = f32[2]{0:T(128)S(1)} collective-permute-done((f32[2]{0:T(128)S(1)}, f32[2]{0:T(128)S(1)}, u32[]{:S(2)}, u32[]{:S(2)}) %collective-permute-start.5) | collective-permute-done | bytes 40 | tf_op jit(solution)/shard_map/ppermute | solution.py:76
  78.5 4.4 collective-permute-done.6
  86.2 3.5 collective-permute-done.7
  91.7 5.0 collective-permute-done.8
  98.7 3.5 collective-permute-done.9
  114.2 6.1 %collective-permute-start.20 = (f32[64,64]{1,0:T(8,128)S(1)}, f32[64,64]{1,0:T(8,128)S(1)}, u32[]{:S(2)}, u32[]{:S(2)}) collective-permute-start(f32[64,64]{1,0:T(8,128)S(1)} %get-tuple-element.79), channel_id=1, source_target_pairs={{1,0},{2,1},{3,2},{4,3},{5,4},{6,5},{7,6},{8,7},{9,8},{10,9},{11,1... | collective-permute-start | bytes 49160 | tf_op jit(solution)/shard_map/ppermute | solution.py:18
  125.0 7.4 %collective-permute-done.13 = f32[3]{0:T(128)S(1)} collective-permute-done((f32[3]{0:T(128)S(1)}, f32[3]{0:T(128)S(1)}, u32[]{:S(2)}, u32[]{:S(2)}) %collective-permute-start.13) | collective-permute-done | bytes 44 | tf_op jit(solution)/shard_map/ppermute | solution.py:76
  135.0 4.4 collective-permute-done.14
  141.4 3.5 collective-permute-done.15
  146.8 5.0 collective-permute-done.16
  153.8 3.5 collective-permute-done.17
  169.9 6.6 %collective-permute-start.28 = (f32[64,64]{1,0:T(8,128)S(1)}, f32[64,64]{1,0:T(8,128)S(1)}, u32[]{:S(2)}, u32[]{:S(2)}) collective-permute-start(f32[64,64]{1,0:T(8,128)S(1)} %get-tuple-element.77), channel_id=1, source_target_pairs={{1,0},{2,1},{3,2},{4,3},{5,4},{6,5},{7,6},{8,7},{9,8},{10,9},{11,1... | collective-permute-start | bytes 49160 | tf_op jit(solution)/shard_map/ppermute | solution.py:18
  182.1 6.6 %collective-permute-done.21 = f32[4]{0:T(128)S(1)} collective-permute-done((f32[4]{0:T(128)S(1)}, f32[4]{0:T(128)S(1)}, u32[]{:S(2)}, u32[]{:S(2)}) %collective-permute-start.21) | collective-permute-done | bytes 48 | tf_op jit(solution)/shard_map/ppermute | solution.py:76
  191.4 4.4 collective-permute-done.22
  197.7 3.5 collective-permute-done.23
  203.2 5.0 collective-permute-done.24
  210.1 3.5 collective-permute-done.25
  226.2 6.6 %collective-permute-start.36 = (f32[64,64]{1,0:T(8,128)S(1)}, f32[64,64]{1,0:T(8,128)S(1)}, u32[]{:S(2)}, u32[]{:S(2)}) collective-permute-start(f32[64,64]{1,0:T(8,128)S(1)} %get-tuple-element.75), channel_id=1, source_target_pairs={{1,0},{2,1},{3,2},{4,3},{5,4},{6,5},{7,6},{8,7},{9,8},{10,9},{11,1... | collective-permute-start | bytes 49160 | tf_op jit(solution)/shard_map/ppermute | solution.py:18
  238.3 6.6 %collective-permute-done.29 = f32[5]{0:T(128)S(1)} collective-permute-done((f32[5]{0:T(128)S(1)}, f32[5]{0:T(128)S(1)}, u32[]{:S(2)}, u32[]{:S(2)}) %collective-permute-start.29) | collective-permute-done | bytes 52 | tf_op jit(solution)/shard_map/ppermute | solution.py:76
  247.6 4.4 collective-permute-done.30
  254.0 3.5 collective-permute-done.31
  259.4 5.0 collective-permute-done.32
  266.4 3.5 collective-permute-done.33
  283.1 6.6 %collective-permute-start.44 = (f32[64,64]{1,0:T(8,128)S(1)}, f32[64,64]{1,0:T(8,128)S(1)}, u32[]{:S(2)}, u32[]{:S(2)}) collective-permute-start(f32[64,64]{1,0:T(8,128)S(1)} %get-tuple-element.73), channel_id=1, source_target_pairs={{1,0},{2,1},{3,2},{4,3},{5,4},{6,5},{7,6},{8,7},{9,8},{10,9},{11,1... | collective-permute-start | bytes 49160 | tf_op jit(solution)/shard_map/ppermute | solution.py:18
  295.3 7.4 %collective-permute-done.37 = f32[6]{0:T(128)S(1)} collective-permute-done((f32[6]{0:T(128)S(1)}, f32[6]{0:T(128)S(1)}, u32[]{:S(2)}, u32[]{:S(2)}) %collective-permute-start.37) | collective-permute-done | bytes 56 | tf_op jit(solution)/shard_map/ppermute | solution.py:76
  305.4 4.4 collective-permute-done.38
  311.7 3.5 collective-permute-done.39
  317.2 5.0 collective-permute-done.40
  324.1 3.5 collective-permute-done.41
  342.3 6.6 %collective-permute-start.52 = (f32[64,64]{1,0:T(8,128)S(1)}, f32[64,64]{1,0:T(8,128)S(1)}, u32[]{:S(2)}, u32[]{:S(2)}) collective-permute-start(f32[64,64]{1,0:T(8,128)S(1)} %get-tuple-element.71), channel_id=1, source_target_pairs={{1,0},{2,1},{3,2},{4,3},{5,4},{6,5},{7,6},{8,7},{9,8},{10,9},{11,1... | collective-permute-start | bytes 49160 | tf_op jit(solution)/shard_map/ppermute | solution.py:18
  355.2 7.4 %collective-permute-done.45 = f32[7]{0:T(128)S(1)} collective-permute-done((f32[7]{0:T(128)S(1)}, f32[7]{0:T(128)S(1)}, u32[]{:S(2)}, u32[]{:S(2)}) %collective-permute-start.45) | collective-permute-done | bytes 60 | tf_op jit(solution)/shard_map/ppermute | solution.py:76
  365.2 4.4 collective-permute-done.46
  371.6 3.5 collective-permute-done.47
  377.1 5.0 collective-permute-done.48
  384.0 3.5 collective-permute-done.49
  408.4 6.6 %collective-permute-start.60 = (f32[64,64]{1,0:T(8,128)S(1)}, f32[64,64]{1,0:T(8,128)S(1)}, u32[]{:S(2)}, u32[]{:S(2)}) collective-permute-start(f32[64,64]{1,0:T(8,128)S(1)} %get-tuple-element.69), channel_id=1, source_target_pairs={{1,0},{2,1},{3,2},{4,3},{5,4},{6,5},{7,6},{8,7},{9,8},{10,9},{11,1... | collective-permute-start | bytes 49160 | tf_op jit(solution)/shard_map/ppermute | solution.py:18
  419.6 4.4 collective-permute-done.54
  425.9 3.5 collective-permute-done.55
  431.4 5.0 collective-permute-done.56
  438.3 3.5 collective-permute-done.57
  460.9 4.9 collective-permute-start.61
  465.7 4.5 collective-permute-done.61
  472.9 4.4 collective-permute-done.62
  479.2 3.5 collective-permute-done.63
  484.7 5.0 collective-permute-done.64
  491.7 3.5 collective-permute-done.65
  505.5 4.9 collective-permute-start.67
  510.4 4.7 collective-permute-done.67
  516.3 3.2 collective-permute-start.68
  519.5 3.2 collective-permute-done.68
  523.3 3.2 collective-permute-start.69
  526.5 2.4 collective-permute-done.69
  529.4 3.2 collective-permute-start.70
  532.7 3.9 collective-permute-done.70
  537.1 3.2 collective-permute-start.71
  543.2 2.9 collective-permute-start.72
  (342 shorter events, 204.8 us)
Async XLA Ops:
  1.3 17.4 %collective-permute-start = (f32[8,256]{1,0:T(8,128)S(1)}, f32[8,256]{1,0:T(8,128)S(1)}, u32[]{:S(2)}, u32[]{:S(2)}) collective-permute-start(f32[8,256]{1,0:T(8,128)S(1)} %copy-done.11), channel_id=1, source_target_pairs={{0,64},{64,0},{128,192},{192,128},{256,320},{320,256},{384,448},{4... | collective-permute-start | bytes 24584 | tf_op jit(solution)/shard_map/ppermute | solution.py:85
  18.8 5.6 %collective-permute-start.1 = (f32[16,256]{1,0:T(8,128)S(1)}, f32[16,256]{1,0:T(8,128)S(1)}, u32[]{:S(2)}, u32[]{:S(2)}) collective-permute-start(f32[16,256]{1,0:T(8,128)S(1)} %maximum_select_fusion.3), channel_id=1, source_target_pairs={{0,128},{64,192},{128,0},{192,64},{256,384},{320,448},{384,256},{4... | collective-permute-start | bytes 49160 | tf_op jit(solution)/shard_map/ppermute | solution.py:85
  24.4 7.3 %collective-permute-start.2 = (f32[32,256]{1,0:T(8,128)S(1)}, f32[32,256]{1,0:T(8,128)S(1)}, u32[]{:S(2)}, u32[]{:S(2)}) collective-permute-start(f32[32,256]{1,0:T(8,128)S(1)} %maximum_select_fusion.2), channel_id=1, source_target_pairs={{0,256},{64,320},{128,384},{192,448},{256,0},{320,64},{384,128},{4... | collective-permute-start | bytes 98312 | tf_op jit(solution)/shard_map/ppermute | solution.py:85
  31.8 11.6 %collective-permute-start.4 = (f32[64,64]{1,0:T(8,128)S(1)}, f32[64,64]{1,0:T(8,128)S(1)}, u32[]{:S(2)}, u32[]{:S(2)}) collective-permute-start(f32[64,64]{1,0:T(8,128)S(1)} %get-tuple-element.83), channel_id=1, source_target_pairs={{1,0},{2,1},{3,2},{4,3},{5,4},{6,5},{7,6},{8,7},{9,8},{10,9},{11,1... | collective-permute-start | bytes 49160 | tf_op jit(solution)/shard_map/ppermute | solution.py:18
  40.2 13.9 %collective-permute-start.3 = (f32[64,64]{1,0:T(8,128)S(1)}, f32[64,64]{1,0:T(8,128)S(1)}, u32[]{:S(2)}, u32[]{:S(2)}) collective-permute-start(f32[64,64]{1,0:T(8,128)S(1)} %get-tuple-element.82), channel_id=1, source_target_pairs={{0,1},{1,2},{2,3},{3,4},{4,5},{5,6},{6,7},{7,8},{8,9},{9,10},{10,1... | collective-permute-start | bytes 49160 | tf_op jit(solution)/shard_map/ppermute | solution.py:17
  59.4 47.7 %collective-permute-start.12 = (f32[64,64]{1,0:T(8,128)S(1)}, f32[64,64]{1,0:T(8,128)S(1)}, u32[]{:S(2)}, u32[]{:S(2)}) collective-permute-start(f32[64,64]{1,0:T(8,128)S(1)} %get-tuple-element.81), channel_id=1, source_target_pairs={{1,0},{2,1},{3,2},{4,3},{5,4},{6,5},{7,6},{8,7},{9,8},{10,9},{11,1... | collective-permute-start | bytes 49160 | tf_op jit(solution)/shard_map/ppermute | solution.py:18
  61.4 45.8 %collective-permute-start.11 = (f32[64,64]{1,0:T(8,128)S(1)}, f32[64,64]{1,0:T(8,128)S(1)}, u32[]{:S(2)}, u32[]{:S(2)}) collective-permute-start(f32[64,64]{1,0:T(8,128)S(1)} %get-tuple-element.80), channel_id=1, source_target_pairs={{0,1},{1,2},{2,3},{3,4},{4,5},{5,6},{6,7},{7,8},{8,9},{9,10},{10,1... | collective-permute-start | bytes 49160 | tf_op jit(solution)/shard_map/ppermute | solution.py:17
  65.9 9.4 %collective-permute-start.5 = (f32[2]{0:T(128)S(1)}, f32[2]{0:T(128)S(1)}, u32[]{:S(2)}, u32[]{:S(2)}) collective-permute-start(f32[2]{0:T(128)S(1)} %pad_maximum_fusion.2), channel_id=1, source_target_pairs={{0,32},{1,33},{2,34},{3,35},{4,36},{5,37},{6,38},{7,39},{8,40},{9,... | collective-permute-start | bytes 32 | tf_op jit(solution)/shard_map/ppermute | solution.py:76
  76.6 6.3 %collective-permute-start.6 = (f32[2]{0:T(128)S(1)}, f32[2]{0:T(128)S(1)}, u32[]{:S(2)}, u32[]{:S(2)}) collective-permute-start(f32[2]{0:T(128)S(1)} %fusion.421), channel_id=1, source_target_pairs={{0,16},{1,17},{2,18},{3,19},{4,20},{5,21},{6,22},{7,23},{8,24},{9,... | collective-permute-start | bytes 32 | tf_op jit(solution)/shard_map/ppermute | solution.py:76
  84.3 5.5 collective-permute-start.7
  89.8 7.0 %collective-permute-start.8 = (f32[2]{0:T(128)S(1)}, f32[2]{0:T(128)S(1)}, u32[]{:S(2)}, u32[]{:S(2)}) collective-permute-start(f32[2]{0:T(128)S(1)} %add.551), channel_id=1, source_target_pairs={{0,4},{1,5},{2,6},{3,7},{4,0},{5,1},{6,2},{7,3},{8,12},{9,13},{10,... | collective-permute-start | bytes 32 | tf_op jit(solution)/shard_map/ppermute | solution.py:76
  96.7 5.5 collective-permute-start.9
  114.2 49.6 %collective-permute-start.20 = (f32[64,64]{1,0:T(8,128)S(1)}, f32[64,64]{1,0:T(8,128)S(1)}, u32[]{:S(2)}, u32[]{:S(2)}) collective-permute-start(f32[64,64]{1,0:T(8,128)S(1)} %get-tuple-element.79), channel_id=1, source_target_pairs={{1,0},{2,1},{3,2},{4,3},{5,4},{6,5},{7,6},{8,7},{9,8},{10,9},{11,1... | collective-permute-start | bytes 49160 | tf_op jit(solution)/shard_map/ppermute | solution.py:18
  120.3 43.5 %collective-permute-start.19 = (f32[64,64]{1,0:T(8,128)S(1)}, f32[64,64]{1,0:T(8,128)S(1)}, u32[]{:S(2)}, u32[]{:S(2)}) collective-permute-start(f32[64,64]{1,0:T(8,128)S(1)} %get-tuple-element.78), channel_id=1, source_target_pairs={{0,1},{1,2},{2,3},{3,4},{4,5},{5,6},{6,7},{7,8},{8,9},{9,10},{10,1... | collective-permute-start | bytes 49160 | tf_op jit(solution)/shard_map/ppermute | solution.py:17
  123.1 9.4 %collective-permute-start.13 = (f32[3]{0:T(128)S(1)}, f32[3]{0:T(128)S(1)}, u32[]{:S(2)}, u32[]{:S(2)}) collective-permute-start(f32[3]{0:T(128)S(1)} %pad_maximum_fusion.3), channel_id=1, source_target_pairs={{0,32},{1,33},{2,34},{3,35},{4,36},{5,37},{6,38},{7,39},{8,40},{9,... | collective-permute-start | bytes 44 | tf_op jit(solution)/shard_map/ppermute | solution.py:76
  133.1 6.3 %collective-permute-start.14 = (f32[3]{0:T(128)S(1)}, f32[3]{0:T(128)S(1)}, u32[]{:S(2)}, u32[]{:S(2)}) collective-permute-start(f32[3]{0:T(128)S(1)} %fusion.420), channel_id=1, source_target_pairs={{0,16},{1,17},{2,18},{3,19},{4,20},{5,21},{6,22},{7,23},{8,24},{9,... | collective-permute-start | bytes 44 | tf_op jit(solution)/shard_map/ppermute | solution.py:76
  139.5 5.5 collective-permute-start.15
  144.9 7.0 %collective-permute-start.16 = (f32[3]{0:T(128)S(1)}, f32[3]{0:T(128)S(1)}, u32[]{:S(2)}, u32[]{:S(2)}) collective-permute-start(f32[3]{0:T(128)S(1)} %add.564), channel_id=1, source_target_pairs={{0,4},{1,5},{2,6},{3,7},{4,0},{5,1},{6,2},{7,3},{8,12},{9,13},{10,... | collective-permute-start | bytes 44 | tf_op jit(solution)/shard_map/ppermute | solution.py:76
  151.9 5.5 collective-permute-start.17
  169.9 50.2 %collective-permute-start.28 = (f32[64,64]{1,0:T(8,128)S(1)}, f32[64,64]{1,0:T(8,128)S(1)}, u32[]{:S(2)}, u32[]{:S(2)}) collective-permute-start(f32[64,64]{1,0:T(8,128)S(1)} %get-tuple-element.77), channel_id=1, source_target_pairs={{1,0},{2,1},{3,2},{4,3},{5,4},{6,5},{7,6},{8,7},{9,8},{10,9},{11,1... | collective-permute-start | bytes 49160 | tf_op jit(solution)/shard_map/ppermute | solution.py:18
  176.5 43.6 %collective-permute-start.27 = (f32[64,64]{1,0:T(8,128)S(1)}, f32[64,64]{1,0:T(8,128)S(1)}, u32[]{:S(2)}, u32[]{:S(2)}) collective-permute-start(f32[64,64]{1,0:T(8,128)S(1)} %get-tuple-element.76), channel_id=1, source_target_pairs={{0,1},{1,2},{2,3},{3,4},{4,5},{5,6},{6,7},{7,8},{8,9},{9,10},{10,1... | collective-permute-start | bytes 49160 | tf_op jit(solution)/shard_map/ppermute | solution.py:17
  179.4 9.4 %collective-permute-start.21 = (f32[4]{0:T(128)S(1)}, f32[4]{0:T(128)S(1)}, u32[]{:S(2)}, u32[]{:S(2)}) collective-permute-start(f32[4]{0:T(128)S(1)} %pad_maximum_fusion.4), channel_id=1, source_target_pairs={{0,32},{1,33},{2,34},{3,35},{4,36},{5,37},{6,38},{7,39},{8,40},{9,... | collective-permute-start | bytes 56 | tf_op jit(solution)/shard_map/ppermute | solution.py:76
  189.4 6.3 %collective-permute-start.22 = (f32[4]{0:T(128)S(1)}, f32[4]{0:T(128)S(1)}, u32[]{:S(2)}, u32[]{:S(2)}) collective-permute-start(f32[4]{0:T(128)S(1)} %fusion.419), channel_id=1, source_target_pairs={{0,16},{1,17},{2,18},{3,19},{4,20},{5,21},{6,22},{7,23},{8,24},{9,... | collective-permute-start | bytes 56 | tf_op jit(solution)/shard_map/ppermute | solution.py:76
  195.8 5.5 collective-permute-start.23
  201.3 7.0 %collective-permute-start.24 = (f32[4]{0:T(128)S(1)}, f32[4]{0:T(128)S(1)}, u32[]{:S(2)}, u32[]{:S(2)}) collective-permute-start(f32[4]{0:T(128)S(1)} %add.575), channel_id=1, source_target_pairs={{0,4},{1,5},{2,6},{3,7},{4,0},{5,1},{6,2},{7,3},{8,12},{9,13},{10,... | collective-permute-start | bytes 56 | tf_op jit(solution)/shard_map/ppermute | solution.py:76
  208.2 5.5 collective-permute-start.25
  226.2 50.9 %collective-permute-start.36 = (f32[64,64]{1,0:T(8,128)S(1)}, f32[64,64]{1,0:T(8,128)S(1)}, u32[]{:S(2)}, u32[]{:S(2)}) collective-permute-start(f32[64,64]{1,0:T(8,128)S(1)} %get-tuple-element.75), channel_id=1, source_target_pairs={{1,0},{2,1},{3,2},{4,3},{5,4},{6,5},{7,6},{8,7},{9,8},{10,9},{11,1... | collective-permute-start | bytes 49160 | tf_op jit(solution)/shard_map/ppermute | solution.py:18
  232.7 44.3 %collective-permute-start.35 = (f32[64,64]{1,0:T(8,128)S(1)}, f32[64,64]{1,0:T(8,128)S(1)}, u32[]{:S(2)}, u32[]{:S(2)}) collective-permute-start(f32[64,64]{1,0:T(8,128)S(1)} %get-tuple-element.74), channel_id=1, source_target_pairs={{0,1},{1,2},{2,3},{3,4},{4,5},{5,6},{6,7},{7,8},{8,9},{9,10},{10,1... | collective-permute-start | bytes 49160 | tf_op jit(solution)/shard_map/ppermute | solution.py:17
  235.6 9.4 %collective-permute-start.29 = (f32[5]{0:T(128)S(1)}, f32[5]{0:T(128)S(1)}, u32[]{:S(2)}, u32[]{:S(2)}) collective-permute-start(f32[5]{0:T(128)S(1)} %pad_maximum_fusion.5), channel_id=1, source_target_pairs={{0,32},{1,33},{2,34},{3,35},{4,36},{5,37},{6,38},{7,39},{8,40},{9,... | collective-permute-start | bytes 68 | tf_op jit(solution)/shard_map/ppermute | solution.py:76
  245.7 6.3 %collective-permute-start.30 = (f32[5]{0:T(128)S(1)}, f32[5]{0:T(128)S(1)}, u32[]{:S(2)}, u32[]{:S(2)}) collective-permute-start(f32[5]{0:T(128)S(1)} %fusion.418), channel_id=1, source_target_pairs={{0,16},{1,17},{2,18},{3,19},{4,20},{5,21},{6,22},{7,23},{8,24},{9,... | collective-permute-start | bytes 68 | tf_op jit(solution)/shard_map/ppermute | solution.py:76
  252.0 5.5 collective-permute-start.31
  257.5 7.0 %collective-permute-start.32 = (f32[5]{0:T(128)S(1)}, f32[5]{0:T(128)S(1)}, u32[]{:S(2)}, u32[]{:S(2)}) collective-permute-start(f32[5]{0:T(128)S(1)} %add.586), channel_id=1, source_target_pairs={{0,4},{1,5},{2,6},{3,7},{4,0},{5,1},{6,2},{7,3},{8,12},{9,13},{10,... | collective-permute-start | bytes 68 | tf_op jit(solution)/shard_map/ppermute | solution.py:76
  264.5 5.5 collective-permute-start.33
  283.1 53.1 %collective-permute-start.44 = (f32[64,64]{1,0:T(8,128)S(1)}, f32[64,64]{1,0:T(8,128)S(1)}, u32[]{:S(2)}, u32[]{:S(2)}) collective-permute-start(f32[64,64]{1,0:T(8,128)S(1)} %get-tuple-element.73), channel_id=1, source_target_pairs={{1,0},{2,1},{3,2},{4,3},{5,4},{6,5},{7,6},{8,7},{9,8},{10,9},{11,1... | collective-permute-start | bytes 49160 | tf_op jit(solution)/shard_map/ppermute | solution.py:18
  289.7 46.5 %collective-permute-start.43 = (f32[64,64]{1,0:T(8,128)S(1)}, f32[64,64]{1,0:T(8,128)S(1)}, u32[]{:S(2)}, u32[]{:S(2)}) collective-permute-start(f32[64,64]{1,0:T(8,128)S(1)} %get-tuple-element.72), channel_id=1, source_target_pairs={{0,1},{1,2},{2,3},{3,4},{4,5},{5,6},{6,7},{7,8},{8,9},{9,10},{10,1... | collective-permute-start | bytes 49160 | tf_op jit(solution)/shard_map/ppermute | solution.py:17
  293.4 9.4 %collective-permute-start.37 = (f32[6]{0:T(128)S(1)}, f32[6]{0:T(128)S(1)}, u32[]{:S(2)}, u32[]{:S(2)}) collective-permute-start(f32[6]{0:T(128)S(1)} %pad_maximum_fusion.6), channel_id=1, source_target_pairs={{0,32},{1,33},{2,34},{3,35},{4,36},{5,37},{6,38},{7,39},{8,40},{9,... | collective-permute-start | bytes 80 | tf_op jit(solution)/shard_map/ppermute | solution.py:76
  303.5 6.3 %collective-permute-start.38 = (f32[6]{0:T(128)S(1)}, f32[6]{0:T(128)S(1)}, u32[]{:S(2)}, u32[]{:S(2)}) collective-permute-start(f32[6]{0:T(128)S(1)} %fusion.417), channel_id=1, source_target_pairs={{0,16},{1,17},{2,18},{3,19},{4,20},{5,21},{6,22},{7,23},{8,24},{9,... | collective-permute-start | bytes 80 | tf_op jit(solution)/shard_map/ppermute | solution.py:76
  309.8 5.5 collective-permute-start.39
  315.3 7.0 %collective-permute-start.40 = (f32[6]{0:T(128)S(1)}, f32[6]{0:T(128)S(1)}, u32[]{:S(2)}, u32[]{:S(2)}) collective-permute-start(f32[6]{0:T(128)S(1)} %add.597), channel_id=1, source_target_pairs={{0,4},{1,5},{2,6},{3,7},{4,0},{5,1},{6,2},{7,3},{8,12},{9,13},{10,... | collective-permute-start | bytes 80 | tf_op jit(solution)/shard_map/ppermute | solution.py:76
  322.2 5.5 collective-permute-start.41
  342.3 53.5 %collective-permute-start.52 = (f32[64,64]{1,0:T(8,128)S(1)}, f32[64,64]{1,0:T(8,128)S(1)}, u32[]{:S(2)}, u32[]{:S(2)}) collective-permute-start(f32[64,64]{1,0:T(8,128)S(1)} %get-tuple-element.71), channel_id=1, source_target_pairs={{1,0},{2,1},{3,2},{4,3},{5,4},{6,5},{7,6},{8,7},{9,8},{10,9},{11,1... | collective-permute-start | bytes 49160 | tf_op jit(solution)/shard_map/ppermute | solution.py:18
  348.9 46.9 %collective-permute-start.51 = (f32[64,64]{1,0:T(8,128)S(1)}, f32[64,64]{1,0:T(8,128)S(1)}, u32[]{:S(2)}, u32[]{:S(2)}) collective-permute-start(f32[64,64]{1,0:T(8,128)S(1)} %get-tuple-element.70), channel_id=1, source_target_pairs={{0,1},{1,2},{2,3},{3,4},{4,5},{5,6},{6,7},{7,8},{8,9},{9,10},{10,1... | collective-permute-start | bytes 49160 | tf_op jit(solution)/shard_map/ppermute | solution.py:17
  353.2 9.4 %collective-permute-start.45 = (f32[7]{0:T(128)S(1)}, f32[7]{0:T(128)S(1)}, u32[]{:S(2)}, u32[]{:S(2)}) collective-permute-start(f32[7]{0:T(128)S(1)} %pad_maximum_fusion.7), channel_id=1, source_target_pairs={{0,32},{1,33},{2,34},{3,35},{4,36},{5,37},{6,38},{7,39},{8,40},{9,... | collective-permute-start | bytes 92 | tf_op jit(solution)/shard_map/ppermute | solution.py:76
  363.3 6.3 %collective-permute-start.46 = (f32[7]{0:T(128)S(1)}, f32[7]{0:T(128)S(1)}, u32[]{:S(2)}, u32[]{:S(2)}) collective-permute-start(f32[7]{0:T(128)S(1)} %fusion.416), channel_id=1, source_target_pairs={{0,16},{1,17},{2,18},{3,19},{4,20},{5,21},{6,22},{7,23},{8,24},{9,... | collective-permute-start | bytes 92 | tf_op jit(solution)/shard_map/ppermute | solution.py:76
  369.7 5.5 collective-permute-start.47
  375.1 7.0 %collective-permute-start.48 = (f32[7]{0:T(128)S(1)}, f32[7]{0:T(128)S(1)}, u32[]{:S(2)}, u32[]{:S(2)}) collective-permute-start(f32[7]{0:T(128)S(1)} %add.608), channel_id=1, source_target_pairs={{0,4},{1,5},{2,6},{3,7},{4,0},{5,1},{6,2},{7,3},{8,12},{9,13},{10,... | collective-permute-start | bytes 92 | tf_op jit(solution)/shard_map/ppermute | solution.py:76
  382.1 5.5 collective-permute-start.49
  406.4 10.5 %collective-permute-start.53 = (f32[8]{0:T(128)S(1)}, f32[8]{0:T(128)S(1)}, u32[]{:S(2)}, u32[]{:S(2)}) collective-permute-start(f32[8]{0:T(128)S(1)} %pad_maximum_fusion.8), channel_id=1, source_target_pairs={{0,32},{1,33},{2,34},{3,35},{4,36},{5,37},{6,38},{7,39},{8,40},{9,... | collective-permute-start | bytes 104 | tf_op jit(solution)/shard_map/ppermute | solution.py:76
  408.4 43.9 %collective-permute-start.60 = (f32[64,64]{1,0:T(8,128)S(1)}, f32[64,64]{1,0:T(8,128)S(1)}, u32[]{:S(2)}, u32[]{:S(2)}) collective-permute-start(f32[64,64]{1,0:T(8,128)S(1)} %get-tuple-element.69), channel_id=1, source_target_pairs={{1,0},{2,1},{3,2},{4,3},{5,4},{6,5},{7,6},{8,7},{9,8},{10,9},{11,1... | collective-permute-start | bytes 49160 | tf_op jit(solution)/shard_map/ppermute | solution.py:18
  415.0 37.3 %collective-permute-start.59 = (f32[64,64]{1,0:T(8,128)S(1)}, f32[64,64]{1,0:T(8,128)S(1)}, u32[]{:S(2)}, u32[]{:S(2)}) collective-permute-start(f32[64,64]{1,0:T(8,128)S(1)} %get-tuple-element.68), channel_id=1, source_target_pairs={{0,1},{1,2},{2,3},{3,4},{4,5},{5,6},{6,7},{7,8},{8,9},{9,10},{10,1... | collective-permute-start | bytes 49160 | tf_op jit(solution)/shard_map/ppermute | solution.py:17
  417.6 6.3 %collective-permute-start.54 = (f32[8]{0:T(128)S(1)}, f32[8]{0:T(128)S(1)}, u32[]{:S(2)}, u32[]{:S(2)}) collective-permute-start(f32[8]{0:T(128)S(1)} %fusion.415), channel_id=1, source_target_pairs={{0,16},{1,17},{2,18},{3,19},{4,20},{5,21},{6,22},{7,23},{8,24},{9,... | collective-permute-start | bytes 104 | tf_op jit(solution)/shard_map/ppermute | solution.py:76
  424.0 5.5 collective-permute-start.55
  429.4 7.0 %collective-permute-start.56 = (f32[8]{0:T(128)S(1)}, f32[8]{0:T(128)S(1)}, u32[]{:S(2)}, u32[]{:S(2)}) collective-permute-start(f32[8]{0:T(128)S(1)} %add.619), channel_id=1, source_target_pairs={{0,4},{1,5},{2,6},{3,7},{4,0},{5,1},{6,2},{7,3},{8,12},{9,13},{10,... | collective-permute-start | bytes 104 | tf_op jit(solution)/shard_map/ppermute | solution.py:76
  436.4 5.5 collective-permute-start.57
  460.9 9.4 %collective-permute-start.61 = (f32[9]{0:T(128)S(1)}, f32[9]{0:T(128)S(1)}, u32[]{:S(2)}, u32[]{:S(2)}) collective-permute-start(f32[9]{0:T(128)S(1)} %pad_maximum_fusion.9), channel_id=1, source_target_pairs={{0,32},{1,33},{2,34},{3,35},{4,36},{5,37},{6,38},{7,39},{8,40},{9,... | collective-permute-start | bytes 116 | tf_op jit(solution)/shard_map/ppermute | solution.py:76
  471.0 6.3 %collective-permute-start.62 = (f32[9]{0:T(128)S(1)}, f32[9]{0:T(128)S(1)}, u32[]{:S(2)}, u32[]{:S(2)}) collective-permute-start(f32[9]{0:T(128)S(1)} %fusion.414), channel_id=1, source_target_pairs={{0,16},{1,17},{2,18},{3,19},{4,20},{5,21},{6,22},{7,23},{8,24},{9,... | collective-permute-start | bytes 116 | tf_op jit(solution)/shard_map/ppermute | solution.py:76
  477.3 5.5 collective-permute-start.63
  482.8 7.0 %collective-permute-start.64 = (f32[9]{0:T(128)S(1)}, f32[9]{0:T(128)S(1)}, u32[]{:S(2)}, u32[]{:S(2)}) collective-permute-start(f32[9]{0:T(128)S(1)} %add.630), channel_id=1, source_target_pairs={{0,4},{1,5},{2,6},{3,7},{4,0},{5,1},{6,2},{7,3},{8,12},{9,13},{10,... | collective-permute-start | bytes 116 | tf_op jit(solution)/shard_map/ppermute | solution.py:76
  489.7 5.5 collective-permute-start.65
  505.5 9.6 %collective-permute-start.67 = (f32[1]{0:T(128)}, f32[1]{0:T(128)}, u32[]{:S(2)}, u32[]{:S(2)}) collective-permute-start(f32[1]{0:T(128)} %bitcast.70), channel_id=1, source_target_pairs={{0,32},{1,33},{2,34},{3,35},{4,36},{5,37},{6,38},{7,39},{8,40},{9,... | collective-permute-start | bytes 20 | tf_op jit(solution)/shard_map/ppermute | solution.py:76
  516.3 6.5 %collective-permute-start.68 = (f32[1]{0:T(128)}, f32[1]{0:T(128)}, u32[]{:S(2)}, u32[]{:S(2)}) collective-permute-start(f32[1]{0:T(128)} %add.636), channel_id=1, source_target_pairs={{0,16},{1,17},{2,18},{3,19},{4,20},{5,21},{6,22},{7,23},{8,24},{9,... | collective-permute-start | bytes 20 | tf_op jit(solution)/shard_map/ppermute | solution.py:76
  523.3 5.6 %collective-permute-start.69 = (f32[1]{0:T(128)}, f32[1]{0:T(128)}, u32[]{:S(2)}, u32[]{:S(2)}) collective-permute-start(f32[1]{0:T(128)} %add.637), channel_id=1, source_target_pairs={{0,8},{1,9},{2,10},{3,11},{4,12},{5,13},{6,14},{7,15},{8,0},{9,1},... | collective-permute-start | bytes 20 | tf_op jit(solution)/shard_map/ppermute | solution.py:76
  529.4 7.1 %collective-permute-start.70 = (f32[1]{0:T(128)}, f32[1]{0:T(128)}, u32[]{:S(2)}, u32[]{:S(2)}) collective-permute-start(f32[1]{0:T(128)} %add.638), channel_id=1, source_target_pairs={{0,4},{1,5},{2,6},{3,7},{4,0},{5,1},{6,2},{7,3},{8,12},{9,13},{10,... | collective-permute-start | bytes 20 | tf_op jit(solution)/shard_map/ppermute | solution.py:76
  537.1 5.6 %collective-permute-start.71 = (f32[1]{0:T(128)}, f32[1]{0:T(128)}, u32[]{:S(2)}, u32[]{:S(2)}) collective-permute-start(f32[1]{0:T(128)} %add.639), channel_id=1, source_target_pairs={{0,2},{1,3},{2,0},{3,1},{4,6},{5,7},{6,4},{7,5},{8,10},{9,11},{10,... | collective-permute-start | bytes 20 | tf_op jit(solution)/shard_map/ppermute | solution.py:76
  (21 other events, 438.2 us)
